TPU v7x, 32 devices: a whole 2x2x4 slice. The times are simulated.
32 devices in a mesh: groups: 2 (over y), ctx: 8 (over z, x), head: 2 (over core).
Axes of the slice: x: 2, y: 2, z: 4, core: 2. Of those that a mesh axis runs over, the one named last changes fastest.
Arguments:
- byte_states: float32 [4096, 1024], P(('groups', 'ctx'), 'head'), parts along dimension 0, may hold values from -8 to 8
- doc_length: int32 [2], P('groups'), parts along dimension 0, may hold values from 1920 to 2048
- block_ids: int32 [1024], P('groups'), parts along dimension 0, may hold values from 0 to 31, never falling along the last dimension, each value on 1 to 64 neighbouring positions
- qk_kernel: float32 [8, 4, 1024], P(None, None, 'head'), may hold values from -2 to 2
- value_kernel: float32 [8, 4, 1024], P(None, None, 'head'), may hold values from -2 to 2
- up_kernel: float32 [8, 4, 1024], P(None, None, 'head'), may hold values from -2 to 2
Outputs:
- mixed: float32 [4096, 1024], P(('groups', 'ctx'), 'head'), parts along dimension 0
There are 2 independent parts, one for each index of `groups`. A program takes and returns all parts, laid end to end along the dimension named above; an argument that names none is the same for every part. Nothing has to cross between parts.
Inputs may be any that keep to these rules, and one draw needn't show every extreme that they name: block_ids never falls along the positions.
All inputs are finite; a program needn't handle non-finite values.
Results may differ from a plain program's by a relative error of at most 0.012.
Values may be sent and summed in bfloat16 or wider, within the bound.
No kernel may reach another device: no remote copies, remote signals or barrier semaphores. Data moves between devices by JAX's collectives and lax.ppermute only.
A program may use at most 64 MiB of HBM per device.

v0:
```python
import math

import jax
import jax.numpy as jnp
from jax import lax
from jax.sharding import PartitionSpec as P

CHANNEL_WIDTH = 128
STRIDE = 4
KERNEL = 8


def shifted(x, axis, by):
    devices = lax.axis_size(axis)
    pairs = [(i, i + by) for i in range(devices) if 0 <= i + by < devices]
    return lax.ppermute(x, axis, pairs)


def shorten(earlier, current, kernel):
    totals = jnp.zeros(current.shape, jnp.float32)
    for offset in range(STRIDE):
        totals = totals + earlier[:, offset, None, :] * kernel[offset][None]
        totals = totals + current[:, offset, None, :] * kernel[offset + STRIDE][None]
    return totals.astype(jnp.bfloat16)


def body(byte_states, doc_length, block_ids, qk_kernel, value_kernel, up_kernel):
    rows_here, channels = byte_states.shape
    lat_dev = rows_here // STRIDE
    n_ctx = lax.axis_size("ctx")
    device = lax.axis_index("ctx")
    lat_total = lat_dev * n_ctx
    rim_rows = shifted(byte_states[rows_here - (KERNEL - STRIDE) :], "ctx", 1)
    earlier = jnp.concatenate([rim_rows, byte_states[: rows_here - STRIDE]], 0).reshape(
        lat_dev, STRIDE, channels
    )
    current = byte_states.reshape(lat_dev, STRIDE, channels)
    key_local = shorten(earlier, current, qk_kernel).reshape(lat_dev, STRIDE * channels)
    value_local = shorten(earlier, current, value_kernel).reshape(lat_dev, STRIDE * channels)
    local_heads = STRIDE * channels // CHANNEL_WIDTH
    copies_n = max(1, n_ctx // local_heads)
    groups_n = n_ctx // copies_n
    head_width = STRIDE * channels // groups_n
    head_here = head_width // CHANNEL_WIDTH
    query_rows = lat_dev // copies_n
    stripe = device % copies_n

    def to_copies(local_rows):
        grouped = local_rows.reshape(lat_dev, groups_n, head_width).transpose(1, 0, 2)
        spread = jnp.broadcast_to(grouped[:, None], (groups_n, copies_n, lat_dev, head_width))
        return spread.reshape(n_ctx, lat_dev, head_width)

    key_all, value_all = (
        lax.all_to_all(to_copies(key_local), "ctx", split_axis=0, concat_axis=0, tiled=True),
        lax.all_to_all(to_copies(value_local), "ctx", split_axis=0, concat_axis=0, tiled=True),
    )
    queries = lax.dynamic_index_in_dim(
        key_all.reshape(n_ctx, copies_n, query_rows, head_width), stripe, 1, keepdims=False
    )
    key_all = key_all.reshape(lat_total, head_here, CHANNEL_WIDTH)
    value_all = value_all.reshape(lat_total, head_here, CHANNEL_WIDTH)
    query_count = n_ctx * query_rows
    query_heads = queries.reshape(query_count, head_here, CHANNEL_WIDTH).transpose(1, 0, 2)
    key_heads = key_all.transpose(1, 0, 2)
    value_heads = value_all.transpose(1, 0, 2)
    asking_index = (
        jnp.arange(n_ctx, dtype=jnp.int32)[:, None] * lat_dev
        + stripe * query_rows
        + jnp.arange(query_rows, dtype=jnp.int32)[None, :]
    ).reshape(query_count)
    query_seg = lax.dynamic_index_in_dim(
        block_ids.reshape(n_ctx, copies_n, query_rows), stripe, 1, keepdims=False
    ).reshape(query_count)
    lat_len = doc_length[0] // STRIDE
    sharpness_divisor = jnp.log(asking_index.astype(jnp.float32) + 2.0) / (
        math.sqrt(float(CHANNEL_WIDTH)) * math.sqrt(math.log(float(lat_total)))
    )
    block_len = min(lat_total, max(512, lat_total // 16))
    block_count = lat_total // block_len

    def attend(running, key_start):
        key_block = lax.dynamic_slice_in_dim(key_heads, key_start, block_len, 1)
        value_block = lax.dynamic_slice_in_dim(value_heads, key_start, block_len, 1)
        seg_block = lax.dynamic_slice_in_dim(block_ids, key_start, block_len, 0)
        key_pos = key_start + jnp.arange(block_len, dtype=jnp.int32)
        run_max, run_sum, run_acc = running
        raw_affinity = (
            jnp.einsum("hqd,hkd->hqk", query_heads, key_block, preferred_element_type=jnp.float32)
            * sharpness_divisor[None, :, None]
        )
        visible = (
            (seg_block[None, :] <= query_seg[:, None])
            & (key_pos[None, :] < lat_len)
            & ((key_pos[None, :] != asking_index[:, None]) | (asking_index[:, None] == 0))
        )
        new_max = jnp.maximum(
            run_max, jnp.max(jnp.where(visible[None], raw_affinity, -1e30), axis=2)
        )
        weights = jnp.where(visible[None], jnp.exp(raw_affinity - new_max[:, :, None]), 0.0)
        factor = jnp.exp(run_max - new_max)
        new_sum = run_sum * factor + jnp.sum(weights, axis=2)
        new_acc = run_acc * factor[:, :, None] + jnp.einsum(
            "hqk,hkd->hqd",
            weights.astype(jnp.bfloat16),
            value_block,
            preferred_element_type=jnp.float32,
        )
        updated = (new_max, new_sum, new_acc)
        return (updated, None)

    initial = (
        jnp.full((head_here, query_count), -1e30, jnp.float32),
        jnp.zeros((head_here, query_count), jnp.float32),
        jnp.zeros((head_here, query_count, CHANNEL_WIDTH), jnp.float32),
    )
    finals, unused = lax.scan(attend, initial, jnp.arange(block_count, dtype=jnp.int32) * block_len)
    attended = (finals[2] / finals[1][:, :, None]).astype(jnp.bfloat16)
    attended = attended.transpose(1, 0, 2).reshape(n_ctx, query_rows, head_width)
    returned = lax.all_to_all(attended, "ctx", split_axis=0, concat_axis=0, tiled=True)
    attended_local = returned.reshape(groups_n, copies_n, query_rows, head_width).transpose(
        1, 2, 0, 3
    )
    attended_local = attended_local.reshape(lat_dev, STRIDE, channels)
    rim_latent = shifted(attended_local[lat_dev - 2 :], "ctx", 1)
    extended = jnp.concatenate([rim_latent, attended_local], 0).astype(jnp.float32)
    prior_one = extended[1:-1]
    prior_two = extended[:-2]
    branch = jnp.zeros((lat_dev, STRIDE, channels), jnp.float32)
    for offset in range(STRIDE):
        branch = branch + prior_one[:, offset, None, :] * up_kernel[:STRIDE, offset][None]
        branch = branch + prior_two[:, offset, None, :] * up_kernel[STRIDE:, offset][None]
    branch = branch.reshape(rows_here, channels)
    byte_pos = device * rows_here + jnp.arange(rows_here, dtype=jnp.int32)
    return byte_states + jnp.where(byte_pos[:, None] < doc_length[0], branch, 0.0)


def solution(mesh):
    return jax.shard_map(
        body,
        mesh=mesh,
        in_specs=(
            P(("groups", "ctx"), "head"),
            P("groups"),
            P("groups"),
            P(None, None, "head"),
            P(None, None, "head"),
            P(None, None, "head"),
        ),
        out_specs=P(("groups", "ctx"), "head"),
        check_vma=False,
    )
```

profile of v0, /device:TPU:0, one launch (start us, length us, event | category | flops | bytes accessed | tf_op | source)
XLA Modules:
  0.0 87.8 jit_solution(5428284050091208952)
XLA Ops:
  0.0 0.7 slice.150
  0.7 4.8 %collective-permute-start = (f32[4,512]{1,0:T(4,128)S(1)}, f32[4,512]{1,0:T(4,128)S(1)}, u32[]{:S(2)}, u32[]{:S(2)}) collective-permute-start(f32[4,512]{1,0:T(4,128)S(1)} %slice.150), channel_id=1, source_target_pairs={{0,2},{2,4},{4,6},{6,8},{8,10},{10,12},{12,14},{1,3},{3,5},{5,7},{... | collective-permute-start | bytes 24584 | tf_op jit(solution)/shard_map/ppermute | solution.py:16
  5.6 1.2 %reshape.264 = f32[64,4,512]{2,1,0:T(4,128)S(1)} reshape(f32[256,512]{1,0:T(8,128)} %param.6) | data formatting | bytes 1048576 | tf_op jit(solution)/shard_map/reshape | solution.py:37
  7.6 0.8 fusion.25
  8.4 0.8 fusion.24
  9.2 1.6 %fusion.23 = (f32[4,1,512]{2,1,0:T(1,128)S(1)}, f32[4,1,512]{2,1,0:T(1,128)}, f32[4,1,512]{2,1,0:T(1,128)}, f32[4,1,512]{2,1,0:T(1,128)}, f32[4,1,512]{2,1,0:T(1...) fusion(f32[8,4,512]{2,1,0:T(4,128)} %param.11), kind=kLoop, calls=%fused_computation.65 | loop fusion | bytes 131072 | tf_op jit(solution)/shard_map/slice | solution.py:130
  11.3 1.1 %fusion.10 = pred[512,512]{0,1:T(8,128)(4,1)} fusion(s32[512]{0:T(512)S(1)} %add.191, s32[512]{0:T(512)S(1)} %copy-done.26, pred[512]{0:T(512)(128)(4,1)S(1)} %get-tuple-element.85, pred[512]{0:T(512)(128)(4,1)S(1)} %get-tuple-element.86), kind=kLoop, calls=%fused_computation.13 | loop fusion | flops 1310720 | bytes 267264 | tf_op jit(solution)/shard_map/while/body/eval_jaxpr/and | solution.py:92
  12.4 0.6 copy_bitcast_fusion.22
  13.0 0.6 mul.517
  14.2 0.6 mul.505
  14.8 0.6 mul.499
  15.4 0.6 mul.493
  16.0 0.6 mul.529
  16.6 0.6 mul.523
  17.3 0.6 mul.552
  17.9 0.6 mul.549
  19.1 0.6 mul.543
  20.3 0.6 mul.558
  20.9 0.6 mul.555
  22.9 0.9 pad_maximum_fusion
  23.8 1.2 %reshape.263 = f32[64,4,512]{2,1,0:T(4,128)S(1)} reshape(f32[256,512]{1,0:T(8,128)} %pad_maximum_fusion) | data formatting | bytes 1048576 | tf_op jit(solution)/shard_map/reshape | solution.py:34
  25.0 1.0 %fusion.21 = (f32[64,1,512]{2,1,0:T(1,128)S(1)}, f32[64,1,512]{2,1,0:T(1,128)S(1)}, f32[64,1,512]{2,1,0:T(1,128)S(1)}, f32[64,1,512]{2,1,0:T(1,128)}) fusion(f32[64,4,512]{2,1,0:T(4,128)S(1)} %reshape.263), kind=kLoop, calls=%fused_computation.63 | loop fusion | bytes 1048576 | tf_op jit(solution)/shard_map/slice | solution.py:22
  26.0 0.9 %mul.521 = f32[64,4,512]{2,1,0:T(4,128)} broadcast(f32[64,512]{1,0:T(8,128)S(1)} %get-tuple-element.91), dimensions={0,2} | broadcast | bytes 655360 | tf_op jit(solution)/shard_map/mul | solution.py:22
  26.9 1.3 %mul.522 = f32[64,8,256]{2,1,0:T(8,128)S(1)} reshape(f32[64,4,512]{2,1,0:T(4,128)} %mul.521) | data formatting | bytes 1048576 | tf_op jit(solution)/shard_map/mul | solution.py:22
  28.1 0.9 %copy_bitcast_fusion.13 = (f32[64,512]{1,0:T(8,128)S(1)}, f32[64,512]{1,0:T(8,128)S(1)}) fusion(f32[64,1,512]{2,1,0:T(1,128)} %get-tuple-element.52, f32[64,1,512]{2,1,0:T(1,128)S(1)} %get-tuple-element.35), kind=kLoop, calls=%fused_computation.41 | loop fusion | bytes 524288
  29.1 0.9 %mul.497 = f32[64,4,512]{2,1,0:T(4,128)} broadcast(f32[64,512]{1,0:T(8,128)S(1)} %get-tuple-element.93), dimensions={0,2} | broadcast | bytes 655360 | tf_op jit(solution)/shard_map/mul | solution.py:22
  30.0 2.2 %mul.498 = f32[64,8,256]{2,1,0:T(8,128)} reshape(f32[64,4,512]{2,1,0:T(4,128)} %mul.497) | data formatting | bytes 1048576 | tf_op jit(solution)/shard_map/mul | solution.py:22
  32.2 0.9 %mul.509 = f32[64,4,512]{2,1,0:T(4,128)} broadcast(f32[64,512]{1,0:T(8,128)S(1)} %get-tuple-element.92), dimensions={0,2} | broadcast | bytes 655360 | tf_op jit(solution)/shard_map/mul | solution.py:22
  33.0 2.1 %mul.510 = f32[64,8,256]{2,1,0:T(8,128)} reshape(f32[64,4,512]{2,1,0:T(4,128)} %mul.509) | data formatting | bytes 1048576 | tf_op jit(solution)/shard_map/mul | solution.py:22
  35.1 0.9 %mul.485 = f32[64,4,512]{2,1,0:T(4,128)} broadcast(f32[64,512]{1,0:T(8,128)S(1)} %get-tuple-element.94), dimensions={0,2} | broadcast | bytes 655360 | tf_op jit(solution)/shard_map/mul | solution.py:22
  36.0 2.0 %mul.486 = f32[64,8,256]{2,1,0:T(8,128)} reshape(f32[64,4,512]{2,1,0:T(4,128)} %mul.485) | data formatting | bytes 1048576 | tf_op jit(solution)/shard_map/mul | solution.py:22
  38.2 1.7 %fusion.17 = bf16[8,64,256]{2,0,1:T(8,128)(2,1)S(1)} fusion(f32[64,8,256]{2,1,0:T(8,128)S(1)} %mul.528, f32[8,256]{1,0:T(8,128)S(1)} %copy-done.13, f32[64,8,256]{2,1,0:T(8,128)S(1)} %mul.522, f32[8,256]{1,0:T(8,128)S(1)} %copy-done.15, f32[64,8,256]{2,1,0:T(8,128)S(1)} %mul.516, f32[8,256]{1,0:T(8,128)S(1)} %copy-done.3, f32[64,8,256]{2,1,0:T(8,128)} %mul.510, ...), kind=kLoop, calls=%fused_computation.26 | loop fusion | flops 2097152 | bytes 4521984 | tf_op jit(solution)/shard_map/transpose | solution.py:49
  39.9 0.8 copy.21
  40.6 4.9 %all-to-all-start = ((bf16[8,64,256]{2,1,0:T(8,128)(2,1)}), bf16[8,64,256]{2,1,0:T(8,128)(2,1)S(1)}, u32[]{:S(2)}, u32[]{:S(2)}) async-start(bf16[8,64,256]{2,1,0:T(8,128)(2,1)} %copy.21), calls=%async_computation | async-start | bytes 524288 | tf_op jit(solution)/shard_map/all_to_all | solution.py:54
  45.6 1.7 %fusion.18 = bf16[8,64,256]{2,0,1:T(8,128)(2,1)S(1)} fusion(f32[64,8,256]{2,1,0:T(8,128)S(1)} %mul.528, f32[8,256]{1,0:T(8,128)S(1)} %copy-done.12, f32[64,8,256]{2,1,0:T(8,128)S(1)} %mul.522, f32[8,256]{1,0:T(8,128)S(1)} %copy-done.14, f32[64,8,256]{2,1,0:T(8,128)S(1)} %mul.516, f32[8,256]{1,0:T(8,128)S(1)} %copy-done.2, f32[64,8,256]{2,1,0:T(8,128)} %mul.510, ...), kind=kLoop, calls=%fused_computation.27 | loop fusion | flops 2097152 | bytes 4521984 | tf_op jit(solution)/shard_map/transpose | solution.py:49
  47.3 0.8 copy.23
  48.0 6.1 %all-to-all-done = bf16[8,64,256]{2,1,0:T(8,128)(2,1)S(1)} async-done(((bf16[8,64,256]{2,1,0:T(8,128)(2,1)}), bf16[8,64,256]{2,1,0:T(8,128)(2,1)S(1)}, u32[]{:S(2)}, u32[]{:S(2)}) %all-to-all-start) | async-done | bytes 262176 | tf_op jit(solution)/shard_map/all_to_all | solution.py:54
  54.1 3.6 %all-to-all-start.1 = ((bf16[8,64,256]{2,1,0:T(8,128)(2,1)}), bf16[8,64,256]{2,1,0:T(8,128)(2,1)S(1)}, u32[]{:S(2)}, u32[]{:S(2)}) async-start(bf16[8,64,256]{2,1,0:T(8,128)(2,1)} %copy.23), calls=%async_computation.1 | async-start | bytes 524288 | tf_op jit(solution)/shard_map/all_to_all | solution.py:55
  57.7 0.8 reshape.265
  58.5 1.7 %select_reduce_fusion = (f32[2,512]{1,0:T(2,128)S(1)}, f32[2,512,512]{1,2,0:T(8,128)S(1)}) fusion(f32[512]{0:T(512)S(1)} %log_multiply_fusion, pred[512,512]{0,1:T(8,128)(4,1)} %fusion.10, bf16[512,2,128]{2,1,0:T(2,128)(2,1)} %reshape.265), kind=kOutput, calls=%fused_computation.1 | convolution fusion | flops 135789568 | bytes 2627584 | tf_op jit(solution)/shard_map/while/body/eval_jaxpr/hqd,hkd->hqk/dot_general | solution.py:88
  60.7 5.5 %all-to-all-done.1 = bf16[8,64,256]{2,1,0:T(8,128)(2,1)S(1)} async-done(((bf16[8,64,256]{2,1,0:T(8,128)(2,1)}), bf16[8,64,256]{2,1,0:T(8,128)(2,1)S(1)}, u32[]{:S(2)}, u32[]{:S(2)}) %all-to-all-start.1) | async-done | bytes 262176 | tf_op jit(solution)/shard_map/all_to_all | solution.py:55
  66.4 1.0 %fusion.4 = bf16[512,2,128]{2,0,1:T(8,128)(2,1)S(1)} fusion(f32[2,512,512]{1,2,0:T(8,128)S(1)} %get-tuple-element.84, f32[2,512]{1,0:T(2,128)S(1)} %get-tuple-element.82, f32[512]{0:T(512)S(1)} %log_multiply_fusion, pred[512,512]{0,1:T(8,128)(4,1)S(1)} %copy-done.1, bf16[512,2,128]{2,1,0:T(2,128)(2,1)S(1)} %reshape.266, f32[512,2]{0,1:T(2,128)S(1)} %bitcast_add_fusion, ...), kind=kOutput, calls=%fused_computation.7 | convolution fusion | flops 136708096 | bytes 2897920 | tf_op jit(solution)/shard_map/while/body/eval_jaxpr/hqk,hkd->hqd/dot_general | solution.py:102
  67.6 0.9 reshape.267
  68.5 3.5 %all-to-all-start.2 = ((bf16[8,64,256]{2,1,0:T(8,128)(2,1)}), bf16[8,64,256]{2,1,0:T(8,128)(2,1)S(1)}, u32[]{:S(2)}, u32[]{:S(2)}) async-start(bf16[8,64,256]{2,1,0:T(8,128)(2,1)} %reshape.267), calls=%async_computation.2 | async-start | bytes 524288 | tf_op jit(solution)/shard_map/all_to_all | solution.py:119
  72.2 8.4 %all-to-all-done.2 = bf16[8,64,256]{2,1,0:T(8,128)(2,1)S(1)} async-done(((bf16[8,64,256]{2,1,0:T(8,128)(2,1)}), bf16[8,64,256]{2,1,0:T(8,128)(2,1)S(1)}, u32[]{:S(2)}, u32[]{:S(2)}) %all-to-all-start.2) | async-done | bytes 262176 | tf_op jit(solution)/shard_map/all_to_all | solution.py:119
  80.6 3.3 %collective-permute-start.1 = (bf16[2,4,512]{2,1,0:T(4,128)(2,1)S(1)}, bf16[2,4,512]{2,1,0:T(4,128)(2,1)S(1)}, u32[]{:S(2)}, u32[]{:S(2)}) collective-permute-start(bf16[2,4,512]{2,1,0:T(4,128)(2,1)S(1)} %slice.177), channel_id=1, source_target_pairs={{0,2},{2,4},{4,6},{6,8},{8,10},{10,12},{12,14},{1,3},{3,5},{5,7},{... | collective-permute-start | bytes 24584 | tf_op jit(solution)/shard_map/ppermute | solution.py:16
  84.3 1.0 %collective-permute-done.1 = bf16[2,4,512]{2,1,0:T(4,128)(2,1)S(1)} collective-permute-done((bf16[2,4,512]{2,1,0:T(4,128)(2,1)S(1)}, bf16[2,4,512]{2,1,0:T(4,128)(2,1)S(1)}, u32[]{:S(2)}, u32[]{:S(2)}) %collective-permute-start.1) | collective-permute-done | bytes 8224 | tf_op jit(solution)/shard_map/ppermute | solution.py:16
  86.9 0.9 %select_add_fusion = f32[256,512]{1,0:T(8,128)} fusion(f32[256,512]{1,0:T(8,128)S(1)} %copy-done, f32[256,512]{1,0:T(8,128)S(1)} %reshape.273, pred[256]{0:T(512)(128)(4,1)S(1)} %add_compare_fusion), kind=kLoop, calls=%fused_computation.17 | loop fusion | flops 262144 | bytes 1573120 | tf_op jit(solution)/shard_map/add | solution.py:134
  (103 shorter events, 6.7 us)
Async XLA Ops:
  0.0 11.3 %copy-start.26 = (s32[512]{0:T(512)S(1)}, s32[512]{0:T(512)}, u32[]{:S(2)}) copy-start(s32[512]{0:T(512)} %param.8) | copy-start | bytes 6148
  0.7 22.0 %collective-permute-start = (f32[4,512]{1,0:T(4,128)S(1)}, f32[4,512]{1,0:T(4,128)S(1)}, u32[]{:S(2)}, u32[]{:S(2)}) collective-permute-start(f32[4,512]{1,0:T(4,128)S(1)} %slice.150), channel_id=1, source_target_pairs={{0,2},{2,4},{4,6},{6,8},{8,10},{10,12},{12,14},{1,3},{3,5},{5,7},{... | collective-permute-start | bytes 24584 | tf_op jit(solution)/shard_map/ppermute | solution.py:16
  7.6 13.9 %copy-start.18 = (s32[512]{0:T(512)}, s32[512]{0:T(512)S(1)}, u32[]{:S(2)}) copy-start(s32[512]{0:T(512)S(1)} %add.191) | copy-start | bytes 6148
  21.9 1.0 %copy-start = (f32[256,512]{1,0:T(8,128)S(1)}, f32[256,512]{1,0:T(8,128)}, u32[]{:S(2)}) copy-start(f32[256,512]{1,0:T(8,128)} %param.6) | copy-start | bytes 1572868
  30.0 8.1 %copy-start.3 = (f32[8,256]{1,0:T(8,128)S(1)}, f32[8,256]{1,0:T(8,128)}, u32[]{:S(2)}) copy-start(f32[8,256]{1,0:T(8,128)} %mul.517) | copy-start | bytes 24580
  30.0 8.1 %copy-start.5 = (f32[8,256]{1,0:T(8,128)S(1)}, f32[8,256]{1,0:T(8,128)}, u32[]{:S(2)}) copy-start(f32[8,256]{1,0:T(8,128)} %mul.511) | copy-start | bytes 24580
  30.0 8.1 %copy-start.7 = (f32[8,256]{1,0:T(8,128)S(1)}, f32[8,256]{1,0:T(8,128)}, u32[]{:S(2)}) copy-start(f32[8,256]{1,0:T(8,128)} %mul.505) | copy-start | bytes 24580
  30.0 8.1 %copy-start.9 = (f32[8,256]{1,0:T(8,128)S(1)}, f32[8,256]{1,0:T(8,128)}, u32[]{:S(2)}) copy-start(f32[8,256]{1,0:T(8,128)} %mul.499) | copy-start | bytes 24580
  30.0 8.1 %copy-start.11 = (f32[8,256]{1,0:T(8,128)S(1)}, f32[8,256]{1,0:T(8,128)}, u32[]{:S(2)}) copy-start(f32[8,256]{1,0:T(8,128)} %mul.493) | copy-start | bytes 24580
  30.0 8.1 %copy-start.13 = (f32[8,256]{1,0:T(8,128)S(1)}, f32[8,256]{1,0:T(8,128)}, u32[]{:S(2)}) copy-start(f32[8,256]{1,0:T(8,128)} %mul.529) | copy-start | bytes 24580
  30.0 8.1 %copy-start.15 = (f32[8,256]{1,0:T(8,128)S(1)}, f32[8,256]{1,0:T(8,128)}, u32[]{:S(2)}) copy-start(f32[8,256]{1,0:T(8,128)} %mul.523) | copy-start | bytes 24580
  38.1 7.4 %copy-start.19 = (s32[512]{0:T(512)S(1)}, s32[512]{0:T(512)}, u32[]{:S(2)}) copy-start(s32[512]{0:T(512)} %copy-done.18) | copy-start | bytes 6148
  38.1 7.4 %copy-start.2 = (f32[8,256]{1,0:T(8,128)S(1)}, f32[8,256]{1,0:T(8,128)}, u32[]{:S(2)}) copy-start(f32[8,256]{1,0:T(8,128)} %mul.552) | copy-start | bytes 24580
  38.1 7.4 %copy-start.4 = (f32[8,256]{1,0:T(8,128)S(1)}, f32[8,256]{1,0:T(8,128)}, u32[]{:S(2)}) copy-start(f32[8,256]{1,0:T(8,128)} %mul.549) | copy-start | bytes 24580
  38.1 7.4 %copy-start.6 = (f32[8,256]{1,0:T(8,128)S(1)}, f32[8,256]{1,0:T(8,128)}, u32[]{:S(2)}) copy-start(f32[8,256]{1,0:T(8,128)} %mul.546) | copy-start | bytes 24580
  38.1 7.4 %copy-start.8 = (f32[8,256]{1,0:T(8,128)S(1)}, f32[8,256]{1,0:T(8,128)}, u32[]{:S(2)}) copy-start(f32[8,256]{1,0:T(8,128)} %mul.543) | copy-start | bytes 24580
  38.1 7.4 %copy-start.10 = (f32[8,256]{1,0:T(8,128)S(1)}, f32[8,256]{1,0:T(8,128)}, u32[]{:S(2)}) copy-start(f32[8,256]{1,0:T(8,128)} %mul.540) | copy-start | bytes 24580
  38.1 7.4 %copy-start.12 = (f32[8,256]{1,0:T(8,128)S(1)}, f32[8,256]{1,0:T(8,128)}, u32[]{:S(2)}) copy-start(f32[8,256]{1,0:T(8,128)} %mul.558) | copy-start | bytes 24580
  38.1 7.4 %copy-start.14 = (f32[8,256]{1,0:T(8,128)S(1)}, f32[8,256]{1,0:T(8,128)}, u32[]{:S(2)}) copy-start(f32[8,256]{1,0:T(8,128)} %mul.555) | copy-start | bytes 24580
  40.6 13.5 %all-to-all-start = ((bf16[8,64,256]{2,1,0:T(8,128)(2,1)}), bf16[8,64,256]{2,1,0:T(8,128)(2,1)S(1)}, u32[]{:S(2)}, u32[]{:S(2)}) async-start(bf16[8,64,256]{2,1,0:T(8,128)(2,1)} %copy.21), calls=%async_computation | async-start | bytes 524288 | tf_op jit(solution)/shard_map/all_to_all | solution.py:54
  47.3 12.9 %copy-start.1 = (pred[512,512]{0,1:T(8,128)(4,1)S(1)}, pred[512,512]{0,1:T(8,128)(4,1)}, u32[]{:S(2)}) copy-start(pred[512,512]{0,1:T(8,128)(4,1)} %fusion.10) | copy-start | bytes 786436
  54.1 12.1 %all-to-all-start.1 = ((bf16[8,64,256]{2,1,0:T(8,128)(2,1)}), bf16[8,64,256]{2,1,0:T(8,128)(2,1)S(1)}, u32[]{:S(2)}, u32[]{:S(2)}) async-start(bf16[8,64,256]{2,1,0:T(8,128)(2,1)} %copy.23), calls=%async_computation.1 | async-start | bytes 524288 | tf_op jit(solution)/shard_map/all_to_all | solution.py:55
  66.3 5.7 %copy-start.24 = (f32[4,1,512]{2,1,0:T(1,128)S(1)}, f32[4,1,512]{2,1,0:T(1,128)}, u32[]{:S(2)}) copy-start(f32[4,1,512]{2,1,0:T(1,128)} %get-tuple-element.58) | copy-start | bytes 24580
  66.3 5.7 %copy-start.25 = (f32[4,1,512]{2,1,0:T(1,128)S(1)}, f32[4,1,512]{2,1,0:T(1,128)}, u32[]{:S(2)}) copy-start(f32[4,1,512]{2,1,0:T(1,128)} %get-tuple-element.59) | copy-start | bytes 24580
  66.4 5.7 %copy-start.22 = (f32[4,1,512]{2,1,0:T(1,128)S(1)}, f32[4,1,512]{2,1,0:T(1,128)}, u32[]{:S(2)}) copy-start(f32[4,1,512]{2,1,0:T(1,128)} %get-tuple-element.60) | copy-start | bytes 24580
  66.4 5.7 %copy-start.23 = (f32[4,1,512]{2,1,0:T(1,128)S(1)}, f32[4,1,512]{2,1,0:T(1,128)}, u32[]{:S(2)}) copy-start(f32[4,1,512]{2,1,0:T(1,128)} %get-tuple-element.61) | copy-start | bytes 24580
  66.4 5.8 %copy-start.20 = (f32[4,1,512]{2,1,0:T(1,128)S(1)}, f32[4,1,512]{2,1,0:T(1,128)}, u32[]{:S(2)}) copy-start(f32[4,1,512]{2,1,0:T(1,128)} %get-tuple-element.63) | copy-start | bytes 24580
  66.4 5.8 %copy-start.21 = (f32[4,1,512]{2,1,0:T(1,128)S(1)}, f32[4,1,512]{2,1,0:T(1,128)}, u32[]{:S(2)}) copy-start(f32[4,1,512]{2,1,0:T(1,128)} %get-tuple-element.64) | copy-start | bytes 24580
  68.5 12.1 %all-to-all-start.2 = ((bf16[8,64,256]{2,1,0:T(8,128)(2,1)}), bf16[8,64,256]{2,1,0:T(8,128)(2,1)S(1)}, u32[]{:S(2)}, u32[]{:S(2)}) async-start(bf16[8,64,256]{2,1,0:T(8,128)(2,1)} %reshape.267), calls=%async_computation.2 | async-start | bytes 524288 | tf_op jit(solution)/shard_map/all_to_all | solution.py:119
  80.6 4.6 %collective-permute-start.1 = (bf16[2,4,512]{2,1,0:T(4,128)(2,1)S(1)}, bf16[2,4,512]{2,1,0:T(4,128)(2,1)S(1)}, u32[]{:S(2)}, u32[]{:S(2)}) collective-permute-start(bf16[2,4,512]{2,1,0:T(4,128)(2,1)S(1)} %slice.177), channel_id=1, source_target_pairs={{0,2},{2,4},{4,6},{6,8},{8,10},{10,12},{12,14},{1,3},{3,5},{5,7},{... | collective-permute-start | bytes 24584 | tf_op jit(solution)/shard_map/ppermute | solution.py:16
  85.4 0.7 copy-start.16
  85.4 0.7 copy-start.17
where the time goes:
time: 88.9 us; the launch traced here: 87.8 us
  local copies, waits for them, and re-layouts  35.1 us (39%)
  waiting for transfers between devices  21.1 us (24%)
  starting transfers between devices  20.1 us (23%)
  other arithmetic  7.53 us (8%)
  matrix products  2.63 us (3%)
  between operations  1.37 us (2%)
    mul x16, local copies, waits for them, and re-layouts, shorten(): totals = totals + earlier[:, offset, None, :] * kernel[offset][None]  14.7 us
    all_to_all x1, waiting for transfers between devices, body(): lax.all_to_all(attended, 'ctx', split_axis=0, concat_axis=0, tiled=True)  8.43 us
    ppermute x2, starting transfers between devices, shifted(): return lax.ppermute(x, axis, pairs)  8.1 us
    all_to_all x1, waiting for transfers between devices, body(): lax.all_to_all(to_copies(key_local), 'ctx', split_axis=0, concat_axis=0,...  6.1 us
    mul x16, local copies, waits for them, and re-layouts, shorten(): current[:, offset, None, :] * kernel[offset + STRIDE][None]  6.02 us
    all_to_all x1, waiting for transfers between devices, body(): lax.all_to_all(to_copies(value_local), 'ctx', split_axis=0, concat_axis=0...  5.54 us
    all_to_all x1, starting transfers between devices, body(): lax.all_to_all(to_copies(key_local), 'ctx', split_axis=0, concat_axis=0,...  4.88 us
    all_to_all x1, starting transfers between devices, body(): lax.all_to_all(to_copies(value_local), 'ctx', split_axis=0, concat_axis=0...  3.59 us
  transfers between devices with their start and end apart: 5, of which 4 were waited for; matrix products, arithmetic and copies ran while one was open for 25% of the time, Pallas kernels for 0%

commit v1 on v0

--- a/solution.py
+++ b/solution.py
@@ -1,8 +1,11 @@
+import functools
 import math
 
 import jax
 import jax.numpy as jnp
 from jax import lax
+from jax.experimental import pallas as pl
+from jax.experimental.pallas import tpu as pltpu
 from jax.sharding import PartitionSpec as P
 
 CHANNEL_WIDTH = 128
@@ -16,12 +19,49 @@
     return lax.ppermute(x, axis, pairs)
 
 
-def shorten(earlier, current, kernel):
-    totals = jnp.zeros(current.shape, jnp.float32)
-    for offset in range(STRIDE):
-        totals = totals + earlier[:, offset, None, :] * kernel[offset][None]
-        totals = totals + current[:, offset, None, :] * kernel[offset + STRIDE][None]
-    return totals.astype(jnp.bfloat16)
+def shorten_kernel(x_ref, rim_ref, qk_ref, vk_ref, out_ref):
+    rows, lanes = x_ref.shape
+    lat = rows // STRIDE
+    first_row = lax.broadcasted_iota(jnp.int32, (lat, lanes), 0) == 0
+    taps = [None] * KERNEL
+    for k in range(STRIDE):
+        current = x_ref[pl.ds(k, lat, stride=STRIDE), :]
+        earlier = pltpu.roll(current, 1, 0)
+        earlier = jnp.where(first_row, rim_ref[pl.ds(k, 1), :], earlier)
+        taps[k] = earlier
+        taps[k + STRIDE] = current
+    for which, kern_ref in enumerate((qk_ref, vk_ref)):
+        for t in range(STRIDE):
+            total = taps[0] * kern_ref[0, pl.ds(t, 1), :]
+            for k in range(1, KERNEL):
+                total = total + taps[k] * kern_ref[k, pl.ds(t, 1), :]
+            out_ref[t, 0, which, 0] = total.astype(jnp.bfloat16)
+
+
+def shorten_both(byte_states, rim_rows, qk_kernel, value_kernel, per_t, nq):
+    rows, channels = byte_states.shape
+    lat = rows // STRIDE
+    lanes = CHANNEL_WIDTH
+    blocks = channels // lanes
+    return pl.pallas_call(
+        shorten_kernel,
+        grid=(blocks,),
+        out_shape=jax.ShapeDtypeStruct((STRIDE, per_t, 2, nq, lat, lanes), jnp.bfloat16),
+        in_specs=[
+            pl.BlockSpec((rows, lanes), lambda b: (0, b)),
+            pl.BlockSpec((KERNEL - STRIDE, lanes), lambda b: (0, b)),
+            pl.BlockSpec((KERNEL, STRIDE, lanes), lambda b: (0, 0, b)),
+            pl.BlockSpec((KERNEL, STRIDE, lanes), lambda b: (0, 0, b)),
+        ],
+        out_specs=pl.BlockSpec(
+            (STRIDE, 1, 2, 1, lat, lanes), lambda b: (0, b // nq, 0, b % nq, 0, 0)
+        ),
+        cost_estimate=pl.CostEstimate(
+            flops=4 * KERNEL * rows * channels,
+            bytes_accessed=4 * rows * channels + 2 * KERNEL * STRIDE * channels * 4 + 2 * rows * channels * 2,
+            transcendentals=0,
+        ),
+    )(byte_states, rim_rows, qk_kernel, value_kernel)
 
 
 def body(byte_states, doc_length, block_ids, qk_kernel, value_kernel, up_kernel):
@@ -31,12 +71,6 @@
     device = lax.axis_index("ctx")
     lat_total = lat_dev * n_ctx
     rim_rows = shifted(byte_states[rows_here - (KERNEL - STRIDE) :], "ctx", 1)
-    earlier = jnp.concatenate([rim_rows, byte_states[: rows_here - STRIDE]], 0).reshape(
-        lat_dev, STRIDE, channels
-    )
-    current = byte_states.reshape(lat_dev, STRIDE, channels)
-    key_local = shorten(earlier, current, qk_kernel).reshape(lat_dev, STRIDE * channels)
-    value_local = shorten(earlier, current, value_kernel).reshape(lat_dev, STRIDE * channels)
     local_heads = STRIDE * channels // CHANNEL_WIDTH
     copies_n = max(1, n_ctx // local_heads)
     groups_n = n_ctx // copies_n
@@ -45,24 +79,26 @@
     query_rows = lat_dev // copies_n
     stripe = device % copies_n
 
-    def to_copies(local_rows):
-        grouped = local_rows.reshape(lat_dev, groups_n, head_width).transpose(1, 0, 2)
-        spread = jnp.broadcast_to(grouped[:, None], (groups_n, copies_n, lat_dev, head_width))
-        return spread.reshape(n_ctx, lat_dev, head_width)
-
-    key_all, value_all = (
-        lax.all_to_all(to_copies(key_local), "ctx", split_axis=0, concat_axis=0, tiled=True),
-        lax.all_to_all(to_copies(value_local), "ctx", split_axis=0, concat_axis=0, tiled=True),
-    )
-    queries = lax.dynamic_index_in_dim(
-        key_all.reshape(n_ctx, copies_n, query_rows, head_width), stripe, 1, keepdims=False
-    )
-    key_all = key_all.reshape(lat_total, head_here, CHANNEL_WIDTH)
-    value_all = value_all.reshape(lat_total, head_here, CHANNEL_WIDTH)
+    nq = head_here
+    per_t = channels // head_width
+    both_local = shorten_both(byte_states, rim_rows, qk_kernel, value_kernel, per_t, nq)
+    both_local = both_local.reshape(groups_n, 2 * nq, lat_dev, CHANNEL_WIDTH)
+    if copies_n > 1:
+        both_local = jnp.broadcast_to(
+            both_local[:, None], (groups_n, copies_n, 2 * nq, lat_dev, CHANNEL_WIDTH)
+        ).reshape(n_ctx, 2 * nq, lat_dev, CHANNEL_WIDTH)
+    both_all = lax.all_to_all(both_local, "ctx", split_axis=0, concat_axis=0, tiled=True)
+    key_all = both_all[:, :nq]
+    value_all = both_all[:, nq:]
+    queries = key_all.reshape(n_ctx, nq, copies_n, query_rows, CHANNEL_WIDTH)[:, :, 0]
+    if copies_n > 1:
+        queries = lax.dynamic_index_in_dim(
+            key_all.reshape(n_ctx, nq, copies_n, query_rows, CHANNEL_WIDTH), stripe, 2, keepdims=False
+        )
     query_count = n_ctx * query_rows
-    query_heads = queries.reshape(query_count, head_here, CHANNEL_WIDTH).transpose(1, 0, 2)
-    key_heads = key_all.transpose(1, 0, 2)
-    value_heads = value_all.transpose(1, 0, 2)
+    query_heads = queries.transpose(1, 0, 2, 3).reshape(nq, query_count, CHANNEL_WIDTH)
+    key_heads = key_all.transpose(1, 0, 2, 3).reshape(nq, lat_total, CHANNEL_WIDTH)
+    value_heads = value_all.transpose(1, 0, 2, 3).reshape(nq, lat_total, CHANNEL_WIDTH)
     asking_index = (
         jnp.arange(n_ctx, dtype=jnp.int32)[:, None] * lat_dev
         + stripe * query_rows
@@ -115,13 +151,17 @@
     )
     finals, unused = lax.scan(attend, initial, jnp.arange(block_count, dtype=jnp.int32) * block_len)
     attended = (finals[2] / finals[1][:, :, None]).astype(jnp.bfloat16)
-    attended = attended.transpose(1, 0, 2).reshape(n_ctx, query_rows, head_width)
-    returned = lax.all_to_all(attended, "ctx", split_axis=0, concat_axis=0, tiled=True)
-    attended_local = returned.reshape(groups_n, copies_n, query_rows, head_width).transpose(
-        1, 2, 0, 3
+    attended = attended.reshape(nq, n_ctx, query_rows, CHANNEL_WIDTH).transpose(1, 0, 2, 3)
+    rim_out = jnp.concatenate(
+        [jnp.zeros((1, nq, 2, CHANNEL_WIDTH), jnp.bfloat16), attended[:-1, :, query_rows - 2 :]], 0
     )
+    outgoing = jnp.concatenate([attended, rim_out], 2)
+    returned = lax.all_to_all(outgoing, "ctx", split_axis=0, concat_axis=0, tiled=True)
+    returned = returned.reshape(groups_n, copies_n, nq, query_rows + 2, CHANNEL_WIDTH)
+    attended_local = returned[:, :, :, :query_rows].transpose(1, 3, 0, 2, 4)
     attended_local = attended_local.reshape(lat_dev, STRIDE, channels)
-    rim_latent = shifted(attended_local[lat_dev - 2 :], "ctx", 1)
+    rim_latent = returned[:, copies_n - 1, :, query_rows:].transpose(2, 0, 1, 3)
+    rim_latent = rim_latent.reshape(2, STRIDE, channels)
     extended = jnp.concatenate([rim_latent, attended_local], 0).astype(jnp.float32)
     prior_one = extended[1:-1]
     prior_two = extended[:-2]

time: 88.9 us -> 50.3 us (0.57)
  local copies, waits for them, and re-layouts: 35.1 us -> 3.4 us
  starting transfers between devices: 20.1 us -> 15.1 us
  other arithmetic: 7.53 us -> 3.52 us
  Pallas kernels: 0 us -> 3.46 us
  matrix products: 2.63 us -> 1.52 us
    mul x32 -> x0, local copies, waits for them, and re-layouts: 20.7 us -> none  [the longest x16 14.7 us: shorten(): totals = totals + earlier[:, offset, None, :] * kernel[offset][None]]
    reshape x5 -> x2, local copies, waits for them, and re-layouts: 4.08 us -> 0.28 us  [the longest x1 0.27 us: body(): attended.reshape(nq, n_ctx, query_rows, CHANNEL_WIDTH).transpose(1, 0, 2, 3)]
    pallas_call x0 -> x1, Pallas kernels: none -> 3.46 us  [shorten_both(): pl.pallas_call(shorten_kernel, grid=(blocks,), out_shape=jax.ShapeDtypeSt...]
    transpose x2 -> x0, other arithmetic: 3.39 us -> none  [to_copies(): local_rows.reshape(lat_dev, groups_n, head_width).transpose(1, 0, 2)]
    ppermute x2 -> x1, starting transfers between devices: 8.1 us -> 4.83 us  [shifted(): return lax.ppermute(x, axis, pairs)]
    slice x7 -> x1, local copies, waits for them, and re-layouts: 3.07 us -> 0.01 us  [body(): attended[:-1, :, query_rows - 2:]]
    all_to_all x3 -> x2, starting transfers between devices: 12 us -> 10.3 us  [the longest x1 6.6 us: body(): lax.all_to_all(both_local, 'ctx', split_axis=0, concat_axis=0, tiled=True)]
    slice x1, local copies, waits for them, and re-layouts: 1.63 us -> 0.05 us  [body(): up_kernel[:STRIDE, offset][None]]
  transfers between devices with their start and end apart: 5 -> 3, of which waited for: 4 -> 3; matrix products, arithmetic and copies ran while one was open for 25% -> 1% of each run, Pallas kernels for 0% -> 0%
where the time goes in v1:
time: 50.3 us; the launch traced here: 49.8 us
  waiting for transfers between devices  21.8 us (43%)
  starting transfers between devices  15.1 us (30%)
  other arithmetic  3.52 us (7%)
  Pallas kernels  3.46 us (7%)
  local copies, waits for them, and re-layouts  3.4 us (7%)
  matrix products  1.52 us (3%)
  between operations  0.97 us (2%)
    all_to_all x1, waiting for transfers between devices, body(): lax.all_to_all(both_local, 'ctx', split_axis=0, concat_axis=0, tiled=True)  12.9 us
    all_to_all x1, waiting for transfers between devices, body(): lax.all_to_all(outgoing, 'ctx', split_axis=0, concat_axis=0, tiled=True)  8.44 us
    all_to_all x1, starting transfers between devices, body(): lax.all_to_all(both_local, 'ctx', split_axis=0, concat_axis=0, tiled=True)  6.6 us
    ppermute x1, starting transfers between devices, shifted(): return lax.ppermute(x, axis, pairs)  4.83 us
    all_to_all x1, starting transfers between devices, body(): lax.all_to_all(outgoing, 'ctx', split_axis=0, concat_axis=0, tiled=True)  3.68 us
    pallas_call x1, Pallas kernels, shorten_both(): pl.pallas_call(shorten_kernel, grid=(blocks,), out_shape=jax.ShapeDtypeSt...  3.46 us
  transfers between devices with their start and end apart: 3, of which 3 were waited for; matrix products, arithmetic and copies ran while one was open for 1% of the time, Pallas kernels for 0%

profile of v1, /device:TPU:0, one launch (start us, length us, event | category | flops | bytes accessed | tf_op | source)
XLA Modules:
  0.0 49.8 jit_solution(17948232035095915172)
XLA Ops:
  0.0 0.0 copy-start.1
  0.0 0.0 copy-start.3
  0.0 0.8 %slice.76 = f32[4,512]{1,0:T(4,128)S(1)} slice(f32[256,512]{1,0:T(8,128)} %x_ref.1), slice={[252:256], [0:512]} | slice | bytes 16384 | tf_op jit(solution)/shard_map/slice | solution.py:73
  0.8 4.8 %collective-permute-start = (f32[4,512]{1,0:T(4,128)S(1)}, f32[4,512]{1,0:T(4,128)S(1)}, u32[]{:S(2)}, u32[]{:S(2)}) collective-permute-start(f32[4,512]{1,0:T(4,128)S(1)} %slice.76), channel_id=1, source_target_pairs={{0,2},{2,4},{4,6},{6,8},{8,10},{10,12},{12,14},{1,3},{3,5},{5,7},{... | collective-permute-start | bytes 24584 | tf_op jit(solution)/shard_map/ppermute | solution.py:19
  5.6 0.1 iota_add_fusion
  5.7 0.1 add.122
  6.4 0.5 %collective-permute-done.rim_ref = f32[4,512]{1,0:T(4,128)S(1)} collective-permute-done((f32[4,512]{1,0:T(4,128)S(1)}, f32[4,512]{1,0:T(4,128)S(1)}, u32[]{:S(2)}, u32[]{:S(2)}) %collective-permute-start) | collective-permute-done | bytes 8224 | tf_op jit(solution)/shard_map/ppermute | solution.py:19
  6.9 0.0 copy-start.2
  6.9 0.6 %copy-done.2 = f32[4,512]{1,0:T(4,128)} copy-done((f32[4,512]{1,0:T(4,128)}, f32[4,512]{1,0:T(4,128)S(1)}, u32[]{:S(2)}) %copy-start.2) | copy-done | bytes 8216
  7.5 3.5 %shard_map.64 = bf16[4,2,2,2,64,128]{5,4,3,2,1,0:T(8,128)(2,1)} custom-call(f32[256,512]{1,0:T(8,128)} %x_ref.1, f32[4,512]{1,0:T(4,128)} %copy-done.2, f32[8,4,512]{2,1,0:T(4,128)} %qk_ref.1, f32[8,4,512]{2,1,0:T(4,128)} %vk_ref.1), custom_call_target="tpu_custom_call" | custom-call | flops 4194304 | bytes 1179648 | tf_op jit(solution)/shard_map/pallas_call | solution.py:46
  11.0 6.6 %all-to-all-start = ((bf16[8,4,64,128]{3,2,1,0:T(8,128)(2,1)}), bf16[8,4,64,128]{3,2,1,0:T(8,128)(2,1)S(1)}, u32[]{:S(2)}, u32[]{:S(2)}) async-start(bf16[8,4,64,128]{3,2,1,0:T(8,128)(2,1)} %bitcast.68), calls=%async_computation | async-start | bytes 1048576 | tf_op jit(solution)/shard_map/all_to_all | solution.py:90
  17.6 0.0 copy-done.1
  17.7 0.0 copy-done.3
  17.7 0.4 fusion.9
  18.1 12.9 %all-to-all-done = bf16[8,4,64,128]{3,2,1,0:T(8,128)(2,1)S(1)} async-done(((bf16[8,4,64,128]{3,2,1,0:T(8,128)(2,1)}), bf16[8,4,64,128]{3,2,1,0:T(8,128)(2,1)S(1)}, u32[]{:S(2)}, u32[]{:S(2)}) %all-to-all-start) | async-done | bytes 524320 | tf_op jit(solution)/shard_map/all_to_all | solution.py:90
  31.0 0.5 %select_reduce_fusion = (f32[2,512]{1,0:T(2,128)S(1)}, f32[2,512,512]{1,2,0:T(8,128)S(1)}) fusion(f32[512]{0:T(512)S(1)} %log_multiply_fusion, pred[512,512]{0,1:T(8,128)(4,1)S(1)} %fusion.9, bf16[2,512,128]{2,1,0:T(8,128)(2,1)S(1)} %bitcast.67), kind=kOutput, calls=%fused_computation.1 | convolution fusion | flops 135789568 | bytes 2627584 | tf_op jit(solution)/shard_map/while/body/eval_jaxpr/hqd,hkd->hqk/dot_general | solution.py:124
  31.6 0.5 %fusion = f32[2,512]{1,0:T(2,128)S(1)} fusion(f32[2,512,512]{1,2,0:T(8,128)S(1)} %get-tuple-element.87, f32[2,512]{1,0:T(2,128)S(1)} %broadcast_maximum_fusion, f32[512]{0:T(512)S(1)} %log_multiply_fusion, pred[512,512]{0,1:T(8,128)(4,1)S(1)} %fusion.9), kind=kLoop, calls=%fused_computation.2 | loop fusion | flops 2096128 | bytes 2369536 | tf_op jit(solution)/shard_map/while/body/eval_jaxpr/reduce_sum | solution.py:137
  32.1 1.0 %fusion.3 = bf16[2,512,128]{2,1,0:T(8,128)(2,1)S(1)} fusion(bf16[2,512,128]{2,1,0:T(8,128)(2,1)S(1)} %bitcast.81, f32[2,512,512]{1,2,0:T(8,128)S(1)} %get-tuple-element.87, f32[2,512]{1,0:T(2,128)S(1)} %broadcast_maximum_fusion, f32[512]{0:T(512)S(1)} %log_multiply_fusion, pred[512,512]{0,1:T(8,128)(4,1)S(1)} %fusion.9, f32[2,512]{1,0:T(2,128)S(1)} %get-tuple-element.85, ...), kind=kOutput, calls=%fused_computation.6 | convolution fusion | flops 136708096 | bytes 2897920 | tf_op jit(solution)/shard_map/while/body/eval_jaxpr/hqk,hkd->hqd/dot_general | solution.py:138
  33.1 0.3 copy.54
  33.4 0.9 %fusion.11 = bf16[8,2,66,128]{3,1,2,0:T(2,128)(2,1)} fusion(bf16[7,2,2,128]{3,1,2,0:T(2,128)(2,1)S(1)} %slice.100, bf16[8,2,64,128]{3,1,2,0:T(2,128)(2,1)S(1)} %bitcast.72), kind=kLoop, calls=%fused_computation.17 | loop fusion | flops 811008 | bytes 539648 | tf_op jit(solution)/shard_map/concatenate | solution.py:158
  34.4 3.7 %all-to-all-start.1 = ((bf16[8,2,66,128]{3,1,2,0:T(2,128)(2,1)}), bf16[8,2,66,128]{3,1,2,0:T(2,128)(2,1)S(1)}, u32[]{:S(2)}, u32[]{:S(2)}) async-start(bf16[8,2,66,128]{3,1,2,0:T(2,128)(2,1)} %fusion.11), calls=%async_computation.1 | async-start | bytes 540672 | tf_op jit(solution)/shard_map/all_to_all | solution.py:159
  38.1 8.4 %all-to-all-done.1 = bf16[8,2,66,128]{3,1,2,0:T(2,128)(2,1)S(1)} async-done(((bf16[8,2,66,128]{3,1,2,0:T(2,128)(2,1)}), bf16[8,2,66,128]{3,1,2,0:T(2,128)(2,1)S(1)}, u32[]{:S(2)}, u32[]{:S(2)}) %all-to-all-start.1) | async-done | bytes 270368 | tf_op jit(solution)/shard_map/all_to_all | solution.py:159
  46.5 0.2 slice_bitcast_fusion
  46.7 0.2 copy.19
  46.9 0.1 reshape.192
  47.0 0.2 maximum_convert_fusion
  47.2 0.6 %fusion.14 = (f32[64,1,512]{2,1,0:T(1,128)S(1)}, f32[64,1,512]{2,1,0:T(1,128)S(1)}, f32[64,1,512]{2,1,0:T(1,128)S(1)}, f32[64,1,512]{2,1,0:T(1,128)S(1)}, f32[64...) fusion(f32[66,4,512]{2,1,0:T(4,128)S(1)} %maximum_convert_fusion), kind=kLoop, calls=%fused_computation.50 | loop fusion | bytes 2097152 | tf_op jit(solution)/shard_map/slice | solution.py:170
  47.8 0.0 copy-start
  48.0 0.5 %add_add_fusion = f32[64,4,512]{2,1,0:T(4,128)S(1)} fusion(f32[4,512]{1,0:T(4,128)S(1)} %get-tuple-element.90, f32[64,512]{1,0:T(8,128)S(1)} %bitcast.73, f32[4,512]{1,0:T(4,128)S(1)} %get-tuple-element.91, f32[64,512]{1,0:T(8,128)S(1)} %bitcast.74, f32[4,512]{1,0:T(4,128)S(1)} %get-tuple-element.92, f32[64,512]{1,0:T(8,128)S(1)} %bitcast.75, ...), kind=kLoop, calls=%fused_computation.15 | loop fusion | flops 1966080 | bytes 1638400 | tf_op jit(solution)/shard_map/add | solution.py:171
  48.5 0.2 reshape.196
  48.7 0.2 copy-done
  48.9 0.9 %select_add_fusion = f32[256,512]{1,0:T(8,128)} fusion(f32[256,512]{1,0:T(8,128)S(1)} %copy-done, f32[256,512]{1,0:T(8,128)S(1)} %reshape.196, pred[256]{0:T(512)(128)(4,1)S(1)} %add_compare_fusion), kind=kLoop, calls=%fused_computation.16 | loop fusion | flops 262144 | bytes 1573120 | tf_op jit(solution)/shard_map/add | solution.py:174
  (26 shorter events, 0.3 us)
Async XLA Ops:
  0.0 17.6 %copy-start.1 = (f32[8,4,512]{2,1,0:T(4,128)S(1)}, f32[8,4,512]{2,1,0:T(4,128)}, u32[]{:S(2)}) copy-start(f32[8,4,512]{2,1,0:T(4,128)} %param.11) | copy-start | bytes 196612
  0.0 17.7 %copy-start.3 = (s32[512]{0:T(512)S(1)}, s32[512]{0:T(512)}, u32[]{:S(2)}) copy-start(s32[512]{0:T(512)} %param.8) | copy-start | bytes 6148
  0.8 6.2 %collective-permute-start = (f32[4,512]{1,0:T(4,128)S(1)}, f32[4,512]{1,0:T(4,128)S(1)}, u32[]{:S(2)}, u32[]{:S(2)}) collective-permute-start(f32[4,512]{1,0:T(4,128)S(1)} %slice.76), channel_id=1, source_target_pairs={{0,2},{2,4},{4,6},{6,8},{8,10},{10,12},{12,14},{1,3},{3,5},{5,7},{... | collective-permute-start | bytes 24584 | tf_op jit(solution)/shard_map/ppermute | solution.py:19
  6.9 0.6 %copy-start.2 = (f32[4,512]{1,0:T(4,128)}, f32[4,512]{1,0:T(4,128)S(1)}, u32[]{:S(2)}) copy-start(f32[4,512]{1,0:T(4,128)S(1)} %collective-permute-done.rim_ref) | copy-start | bytes 24580
  11.0 19.9 %all-to-all-start = ((bf16[8,4,64,128]{3,2,1,0:T(8,128)(2,1)}), bf16[8,4,64,128]{3,2,1,0:T(8,128)(2,1)S(1)}, u32[]{:S(2)}, u32[]{:S(2)}) async-start(bf16[8,4,64,128]{3,2,1,0:T(8,128)(2,1)} %bitcast.68), calls=%async_computation | async-start | bytes 1048576 | tf_op jit(solution)/shard_map/all_to_all | solution.py:90
  34.4 12.2 %all-to-all-start.1 = ((bf16[8,2,66,128]{3,1,2,0:T(2,128)(2,1)}), bf16[8,2,66,128]{3,1,2,0:T(2,128)(2,1)S(1)}, u32[]{:S(2)}, u32[]{:S(2)}) async-start(bf16[8,2,66,128]{3,1,2,0:T(2,128)(2,1)} %fusion.11), calls=%async_computation.1 | async-start | bytes 540672 | tf_op jit(solution)/shard_map/all_to_all | solution.py:159
  47.8 1.0 %copy-start = (f32[256,512]{1,0:T(8,128)S(1)}, f32[256,512]{1,0:T(8,128)}, u32[]{:S(2)}) copy-start(f32[256,512]{1,0:T(8,128)} %x_ref.1) | copy-start | bytes 1572868

commit v2 on v1

--- a/solution.py
+++ b/solution.py
@@ -64,6 +64,64 @@
     )(byte_states, rim_rows, qk_kernel, value_kernel)
 
 
+def up_kernel_fn(copies_n, per_t, nq, qr, lim_ref, ret_ref, x_ref, up_ref, out_ref):
+    rows, lanes = x_ref.shape
+    lat = rows // STRIDE
+    block = pl.program_id(0)
+    sub = block // nq
+    q = block % nq
+    row = lax.broadcasted_iota(jnp.int32, (lat, lanes), 0)
+    prior_one = []
+    prior_two = []
+    for t in range(STRIDE):
+        g = t * per_t + sub
+        parts = [
+            ret_ref[g * copies_n + s, pl.ds(pl.multiple_of(q * qr, qr), qr), :] for s in range(copies_n)
+        ]
+        att = (parts[0] if copies_n == 1 else jnp.concatenate(parts, 0)).astype(jnp.float32)
+        rims = ret_ref[g * copies_n + copies_n - 1, pl.ds(nq * qr, 2 * nq), :].astype(jnp.float32)
+        rim = rims[0:2]
+        for other in range(1, nq):
+            rim = jnp.where(q == other, rims[2 * other : 2 * other + 2], rim)
+        one = pltpu.roll(att, 1, 0)
+        one = jnp.where(row == 0, rim[1:2], one)
+        two = pltpu.roll(att, 2, 0)
+        two = jnp.where(row == 0, rim[0:1], jnp.where(row == 1, rim[1:2], two))
+        prior_one.append(one)
+        prior_two.append(two)
+    limit = lim_ref[0]
+    for s in range(STRIDE):
+        total = prior_one[0] * up_ref[s, pl.ds(0, 1), :] + prior_two[0] * up_ref[s + STRIDE, pl.ds(0, 1), :]
+        for t in range(1, STRIDE):
+            total = total + prior_one[t] * up_ref[s, pl.ds(t, 1), :]
+            total = total + prior_two[t] * up_ref[s + STRIDE, pl.ds(t, 1), :]
+        here = x_ref[pl.ds(s, lat, stride=STRIDE), :]
+        inside = row * STRIDE + s < limit
+        out_ref[pl.ds(s, lat, stride=STRIDE), :] = here + jnp.where(inside, total, 0.0)
+
+
+def up_and_mix(limit, returned, byte_states, up_kernel, copies_n, per_t, nq, qr):
+    rows, channels = byte_states.shape
+    lanes = CHANNEL_WIDTH
+    return pl.pallas_call(
+        functools.partial(up_kernel_fn, copies_n, per_t, nq, qr),
+        grid=(channels // lanes,),
+        out_shape=jax.ShapeDtypeStruct((rows, channels), jnp.float32),
+        in_specs=[
+            pl.BlockSpec(memory_space=pltpu.SMEM),
+            pl.BlockSpec(returned.shape, lambda b: (0, 0, 0)),
+            pl.BlockSpec((rows, lanes), lambda b: (0, b)),
+            pl.BlockSpec((KERNEL, STRIDE, lanes), lambda b: (0, 0, b)),
+        ],
+        out_specs=pl.BlockSpec((rows, lanes), lambda b: (0, b)),
+        cost_estimate=pl.CostEstimate(
+            flops=4 * KERNEL * rows * channels,
+            bytes_accessed=8 * rows * channels + returned.size * 2,
+            transcendentals=0,
+        ),
+    )(limit, returned, byte_states, up_kernel)
+
+
 def body(byte_states, doc_length, block_ids, qk_kernel, value_kernel, up_kernel):
     rows_here, channels = byte_states.shape
     lat_dev = rows_here // STRIDE
@@ -155,24 +213,20 @@
     rim_out = jnp.concatenate(
         [jnp.zeros((1, nq, 2, CHANNEL_WIDTH), jnp.bfloat16), attended[:-1, :, query_rows - 2 :]], 0
     )
-    outgoing = jnp.concatenate([attended, rim_out], 2)
+    main_rows = nq * query_rows
+    used_rows = main_rows + 2 * nq
+    ret_rows = -(-used_rows // 16) * 16
+    outgoing = jnp.concatenate(
+        [
+            attended.reshape(n_ctx, main_rows, CHANNEL_WIDTH),
+            rim_out.reshape(n_ctx, 2 * nq, CHANNEL_WIDTH),
+            jnp.zeros((n_ctx, ret_rows - used_rows, CHANNEL_WIDTH), jnp.bfloat16),
+        ],
+        1,
+    )
     returned = lax.all_to_all(outgoing, "ctx", split_axis=0, concat_axis=0, tiled=True)
-    returned = returned.reshape(groups_n, copies_n, nq, query_rows + 2, CHANNEL_WIDTH)
-    attended_local = returned[:, :, :, :query_rows].transpose(1, 3, 0, 2, 4)
-    attended_local = attended_local.reshape(lat_dev, STRIDE, channels)
-    rim_latent = returned[:, copies_n - 1, :, query_rows:].transpose(2, 0, 1, 3)
-    rim_latent = rim_latent.reshape(2, STRIDE, channels)
-    extended = jnp.concatenate([rim_latent, attended_local], 0).astype(jnp.float32)
-    prior_one = extended[1:-1]
-    prior_two = extended[:-2]
-    branch = jnp.zeros((lat_dev, STRIDE, channels), jnp.float32)
-    for offset in range(STRIDE):
-        branch = branch + prior_one[:, offset, None, :] * up_kernel[:STRIDE, offset][None]
-        branch = branch + prior_two[:, offset, None, :] * up_kernel[STRIDE:, offset][None]
-    branch = branch.reshape(rows_here, channels)
-    byte_pos = device * rows_here + jnp.arange(rows_here, dtype=jnp.int32)
-    return byte_states + jnp.where(byte_pos[:, None] < doc_length[0], branch, 0.0)
-
+    limit = (doc_length[0] - device * rows_here).reshape(1).astype(jnp.int32)
+    return up_and_mix(limit, returned, byte_states, up_kernel, copies_n, per_t, nq, query_rows)
 
 def solution(mesh):
     return jax.shard_map(

time: 50.3 us -> 51.4 us (1.022)
  Pallas kernels: 3.46 us -> 6.99 us
  other arithmetic: 3.52 us -> 1.82 us
  local copies, waits for them, and re-layouts: 3.4 us -> 2.32 us
    pallas_call x0 -> x1, Pallas kernels: none -> 3.52 us  [up_and_mix(): pl.pallas_call(functools.partial(up_kernel_fn, copies_n, per_t, nq, qr),...]
    add x2 -> x0, other arithmetic: 1.44 us -> none  [the longest x1 0.91 us: body(): byte_states + jnp.where(byte_pos[:, None] < doc_length[0], branch, 0.0)]
    ppermute x1, waiting for transfers between devices: 0.5 us -> 1.35 us  [shifted(): return lax.ppermute(x, axis, pairs)]
    all_to_all x1, waiting for transfers between devices: 12.9 us -> 12 us  [body(): lax.all_to_all(both_local, 'ctx', split_axis=0, concat_axis=0, tiled=True)]
    slice x2 -> x0, local copies, waits for them, and re-layouts: 0.61 us -> none  [the longest x1 0.57 us: body(): prior_one[:, offset, None, :] * up_kernel[:STRIDE, offset][None]]
    unnamed x20 -> x6, local copies, waits for them, and re-layouts: 0.92 us -> 1.31 us
where the time goes in v2:
time: 51.4 us; the launch traced here: 50.9 us
  waiting for transfers between devices  22.3 us (43%)
  starting transfers between devices  15.1 us (29%)
  Pallas kernels  6.99 us (14%)
  local copies, waits for them, and re-layouts  2.32 us (5%)
  other arithmetic  1.82 us (4%)
  matrix products  1.53 us (3%)
  between operations  0.78 us (2%)
    all_to_all x1, waiting for transfers between devices, body(): lax.all_to_all(both_local, 'ctx', split_axis=0, concat_axis=0, tiled=True)  12 us
    all_to_all x1, waiting for transfers between devices, body(): lax.all_to_all(outgoing, 'ctx', split_axis=0, concat_axis=0, tiled=True)  8.93 us
    all_to_all x1, starting transfers between devices, body(): lax.all_to_all(both_local, 'ctx', split_axis=0, concat_axis=0, tiled=True)  6.6 us
    ppermute x1, starting transfers between devices, shifted(): return lax.ppermute(x, axis, pairs)  4.83 us
    all_to_all x1, starting transfers between devices, body(): lax.all_to_all(outgoing, 'ctx', split_axis=0, concat_axis=0, tiled=True)  3.68 us
    pallas_call x1, Pallas kernels, up_and_mix(): pl.pallas_call(functools.partial(up_kernel_fn, copies_n, per_t, nq, qr),...  3.52 us
    pallas_call x1, Pallas kernels, shorten_both(): pl.pallas_call(shorten_kernel, grid=(blocks,), out_shape=jax.ShapeDtypeSt...  3.46 us
    ppermute x1, waiting for transfers between devices, shifted(): return lax.ppermute(x, axis, pairs)  1.35 us
  transfers between devices with their start and end apart: 3, of which 3 were waited for; matrix products, arithmetic and copies ran while one was open for 1% of the time, Pallas kernels for 0%

profile of v2, /device:TPU:0, one launch (start us, length us, event | category | flops | bytes accessed | tf_op | source)
XLA Modules:
  0.0 50.9 jit_solution(6084540571238447707)
XLA Ops:
  0.0 0.0 copy-start.2
  0.0 0.7 %slice.12 = f32[4,512]{1,0:T(4,128)S(1)} slice(f32[256,512]{1,0:T(8,128)} %x_ref.3), slice={[252:256], [0:512]} | slice | bytes 16384 | tf_op jit(solution)/shard_map/slice | solution.py:131
  0.7 4.8 %collective-permute-start = (f32[4,512]{1,0:T(4,128)S(1)}, f32[4,512]{1,0:T(4,128)S(1)}, u32[]{:S(2)}, u32[]{:S(2)}) collective-permute-start(f32[4,512]{1,0:T(4,128)S(1)} %slice.12), channel_id=1, source_target_pairs={{0,2},{2,4},{4,6},{6,8},{8,10},{10,12},{12,14},{1,3},{3,5},{5,7},{... | collective-permute-start | bytes 24584 | tf_op jit(solution)/shard_map/ppermute | solution.py:19
  5.6 1.3 %collective-permute-done.rim_ref = f32[4,512]{1,0:T(4,128)S(1)} collective-permute-done((f32[4,512]{1,0:T(4,128)S(1)}, f32[4,512]{1,0:T(4,128)S(1)}, u32[]{:S(2)}, u32[]{:S(2)}) %collective-permute-start) | collective-permute-done | bytes 8224 | tf_op jit(solution)/shard_map/ppermute | solution.py:19
  6.9 0.0 copy-start.1
  6.9 0.6 %copy-done.1 = f32[4,512]{1,0:T(4,128)} copy-done((f32[4,512]{1,0:T(4,128)}, f32[4,512]{1,0:T(4,128)S(1)}, u32[]{:S(2)}) %copy-start.1) | copy-done | bytes 8216
  7.5 3.5 %shard_map.64 = bf16[4,2,2,2,64,128]{5,4,3,2,1,0:T(8,128)(2,1)} custom-call(f32[256,512]{1,0:T(8,128)} %x_ref.3, f32[4,512]{1,0:T(4,128)} %copy-done.1, f32[8,4,512]{2,1,0:T(4,128)} %qk_ref.1, f32[8,4,512]{2,1,0:T(4,128)} %vk_ref.1), custom_call_target="tpu_custom_call" | custom-call | flops 4194304 | bytes 1179648 | tf_op jit(solution)/shard_map/pallas_call | solution.py:46
  11.0 6.6 %all-to-all-start = ((bf16[8,4,64,128]{3,2,1,0:T(8,128)(2,1)}), bf16[8,4,64,128]{3,2,1,0:T(8,128)(2,1)S(1)}, u32[]{:S(2)}, u32[]{:S(2)}) async-start(bf16[8,4,64,128]{3,2,1,0:T(8,128)(2,1)} %bitcast.24), calls=%async_computation | async-start | bytes 1048576 | tf_op jit(solution)/shard_map/all_to_all | solution.py:148
  18.3 0.1 iota_add_fusion
  18.3 0.1 add.74
  18.4 0.1 pad.3.clone
  18.5 0.0 copy-done.2
  18.5 0.4 fusion.9
  18.9 12.0 %all-to-all-done = bf16[8,4,64,128]{3,2,1,0:T(8,128)(2,1)S(1)} async-done(((bf16[8,4,64,128]{3,2,1,0:T(8,128)(2,1)}), bf16[8,4,64,128]{3,2,1,0:T(8,128)(2,1)S(1)}, u32[]{:S(2)}, u32[]{:S(2)}) %all-to-all-start) | async-done | bytes 524320 | tf_op jit(solution)/shard_map/all_to_all | solution.py:148
  31.0 0.5 %select_reduce_fusion = (f32[2,512]{1,0:T(2,128)S(1)}, f32[2,512,512]{1,2,0:T(8,128)S(1)}) fusion(f32[512]{0:T(512)S(1)} %log_multiply_fusion, pred[512,512]{0,1:T(8,128)(4,1)S(1)} %fusion.9, bf16[2,512,128]{2,1,0:T(8,128)(2,1)S(1)} %bitcast.23), kind=kOutput, calls=%fused_computation.1 | convolution fusion | flops 135789568 | bytes 2627584 | tf_op jit(solution)/shard_map/while/body/eval_jaxpr/hqd,hkd->hqk/dot_general | solution.py:182
  31.6 0.5 %fusion = f32[2,512]{1,0:T(2,128)S(1)} fusion(f32[2,512,512]{1,2,0:T(8,128)S(1)} %get-tuple-element.73, f32[2,512]{1,0:T(2,128)S(1)} %broadcast_maximum_fusion, f32[512]{0:T(512)S(1)} %log_multiply_fusion, pred[512,512]{0,1:T(8,128)(4,1)S(1)} %fusion.9), kind=kLoop, calls=%fused_computation.2 | loop fusion | flops 2096128 | bytes 2369536 | tf_op jit(solution)/shard_map/while/body/eval_jaxpr/reduce_sum | solution.py:195
  32.1 1.0 %fusion.3 = bf16[2,512,128]{2,1,0:T(8,128)(2,1)S(1)} fusion(bf16[2,512,128]{2,1,0:T(8,128)(2,1)S(1)} %bitcast.27, f32[2,512,512]{1,2,0:T(8,128)S(1)} %get-tuple-element.73, f32[2,512]{1,0:T(2,128)S(1)} %broadcast_maximum_fusion, f32[512]{0:T(512)S(1)} %log_multiply_fusion, pred[512,512]{0,1:T(8,128)(4,1)S(1)} %fusion.9, f32[2,512]{1,0:T(2,128)S(1)} %get-tuple-element.71, ...), kind=kOutput, calls=%fused_computation.6 | convolution fusion | flops 136708096 | bytes 2897920 | tf_op jit(solution)/shard_map/while/body/eval_jaxpr/hqk,hkd->hqd/dot_general | solution.py:196
  33.2 0.8 %maximum_maximum_fusion = bf16[8,144,128]{2,1,0:T(8,128)(2,1)} fusion(bf16[8,4,128]{2,1,0:T(4,128)(2,1)S(1)} %bitcast.29, bf16[8,128,128]{2,1,0:T(8,128)(2,1)S(1)} %bitcast.26, bf16[144]{0:T(256)(128)(2,1)S(1)} %pad.3.clone), kind=kLoop, calls=%fused_computation.14 | loop fusion | flops 884736 | bytes 565536 | tf_op jit(solution)/shard_map/concatenate | solution.py:219
  34.0 3.7 %all-to-all-start.1 = ((bf16[8,144,128]{2,1,0:T(8,128)(2,1)}), bf16[8,144,128]{2,1,0:T(8,128)(2,1)S(1)}, u32[]{:S(2)}, u32[]{:S(2)}) async-start(bf16[8,144,128]{2,1,0:T(8,128)(2,1)} %maximum_maximum_fusion), calls=%async_computation.1 | async-start | bytes 589824 | tf_op jit(solution)/shard_map/all_to_all | solution.py:227
  37.7 8.9 %all-to-all-done.1.ret_ref = bf16[8,144,128]{2,1,0:T(8,128)(2,1)S(1)} async-done(((bf16[8,144,128]{2,1,0:T(8,128)(2,1)}), bf16[8,144,128]{2,1,0:T(8,128)(2,1)S(1)}, u32[]{:S(2)}, u32[]{:S(2)}) %all-to-all-start.1) | async-done | bytes 294944 | tf_op jit(solution)/shard_map/all_to_all | solution.py:227
  46.6 0.0 copy-start
  46.6 0.7 %copy-done = bf16[8,144,128]{2,1,0:T(8,128)(2,1)} copy-done((bf16[8,144,128]{2,1,0:T(8,128)(2,1)}, bf16[8,144,128]{2,1,0:T(8,128)(2,1)S(1)}, u32[]{:S(2)}) %copy-start) | copy-done | bytes 294936
  47.3 3.5 %shard_map.65 = f32[256,512]{1,0:T(8,128)} custom-call(s32[1]{0:T(128)} %bitcast.1.lim_ref, bf16[8,144,128]{2,1,0:T(8,128)(2,1)} %copy-done, f32[256,512]{1,0:T(8,128)} %x_ref.3, f32[8,4,512]{2,1,0:T(4,128)} %up_ref.1), custom_call_target="tpu_custom_call" | custom-call | flops 4194304 | bytes 1343488 | tf_op jit(solution)/shard_map/pallas_call | solution.py:106
  (12 shorter events, 0.2 us)
Async XLA Ops:
  0.0 18.5 %copy-start.2 = (s32[512]{0:T(512)S(1)}, s32[512]{0:T(512)}, u32[]{:S(2)}) copy-start(s32[512]{0:T(512)} %param.8) | copy-start | bytes 6148
  0.7 6.2 %collective-permute-start = (f32[4,512]{1,0:T(4,128)S(1)}, f32[4,512]{1,0:T(4,128)S(1)}, u32[]{:S(2)}, u32[]{:S(2)}) collective-permute-start(f32[4,512]{1,0:T(4,128)S(1)} %slice.12), channel_id=1, source_target_pairs={{0,2},{2,4},{4,6},{6,8},{8,10},{10,12},{12,14},{1,3},{3,5},{5,7},{... | collective-permute-start | bytes 24584 | tf_op jit(solution)/shard_map/ppermute | solution.py:19
  6.9 0.6 %copy-start.1 = (f32[4,512]{1,0:T(4,128)}, f32[4,512]{1,0:T(4,128)S(1)}, u32[]{:S(2)}) copy-start(f32[4,512]{1,0:T(4,128)S(1)} %collective-permute-done.rim_ref) | copy-start | bytes 24580
  11.0 19.9 %all-to-all-start = ((bf16[8,4,64,128]{3,2,1,0:T(8,128)(2,1)}), bf16[8,4,64,128]{3,2,1,0:T(8,128)(2,1)S(1)}, u32[]{:S(2)}, u32[]{:S(2)}) async-start(bf16[8,4,64,128]{3,2,1,0:T(8,128)(2,1)} %bitcast.24), calls=%async_computation | async-start | bytes 1048576 | tf_op jit(solution)/shard_map/all_to_all | solution.py:148
  34.0 12.6 %all-to-all-start.1 = ((bf16[8,144,128]{2,1,0:T(8,128)(2,1)}), bf16[8,144,128]{2,1,0:T(8,128)(2,1)S(1)}, u32[]{:S(2)}, u32[]{:S(2)}) async-start(bf16[8,144,128]{2,1,0:T(8,128)(2,1)} %maximum_maximum_fusion), calls=%async_computation.1 | async-start | bytes 589824 | tf_op jit(solution)/shard_map/all_to_all | solution.py:227
  46.6 0.7 %copy-start = (bf16[8,144,128]{2,1,0:T(8,128)(2,1)}, bf16[8,144,128]{2,1,0:T(8,128)(2,1)S(1)}, u32[]{:S(2)}) copy-start(bf16[8,144,128]{2,1,0:T(8,128)(2,1)S(1)} %all-to-all-done.1.ret_ref) | copy-start | bytes 884740

commit v3 on v2

--- a/solution.py
+++ b/solution.py
@@ -19,49 +19,77 @@
     return lax.ppermute(x, axis, pairs)
 
 
-def shorten_kernel(x_ref, rim_ref, qk_ref, vk_ref, out_ref):
+def shorten_kernel(nq, x_ref, extra_ref, qk_ref, vk_ref, out_ref):
     rows, lanes = x_ref.shape
     lat = rows // STRIDE
+    block = pl.program_id(0)
+    sub = block // nq
+    q = block % nq
+    per_t = out_ref.shape[0] // STRIDE
     first_row = lax.broadcasted_iota(jnp.int32, (lat, lanes), 0) == 0
     taps = [None] * KERNEL
     for k in range(STRIDE):
         current = x_ref[pl.ds(k, lat, stride=STRIDE), :]
-        earlier = pltpu.roll(current, 1, 0)
-        earlier = jnp.where(first_row, rim_ref[pl.ds(k, 1), :], earlier)
-        taps[k] = earlier
+        taps[k] = jnp.where(first_row, 0.0, pltpu.roll(current, 1, 0))
         taps[k + STRIDE] = current
     for which, kern_ref in enumerate((qk_ref, vk_ref)):
+        slot = which * nq + q
         for t in range(STRIDE):
             total = taps[0] * kern_ref[0, pl.ds(t, 1), :]
             for k in range(1, KERNEL):
                 total = total + taps[k] * kern_ref[k, pl.ds(t, 1), :]
-            out_ref[t, 0, which, 0] = total.astype(jnp.bfloat16)
-
-
-def shorten_both(byte_states, rim_rows, qk_kernel, value_kernel, per_t, nq):
+            out_ref[t * per_t + sub, pl.ds(pl.multiple_of(slot * lat, lat), lat), :] = total.astype(
+                jnp.bfloat16
+            )
+
+    @pl.when(block == 0)
+    def _():
+        out_ref[:, pl.ds(2 * nq * lat, extra_ref.shape[1]), :] = extra_ref[...]
+
+
+def shorten_both(byte_states, extras, qk_kernel, value_kernel, groups_n, nq):
     rows, channels = byte_states.shape
     lat = rows // STRIDE
     lanes = CHANNEL_WIDTH
     blocks = channels // lanes
+    kv_rows = 2 * nq * lat + extras.shape[1]
     return pl.pallas_call(
-        shorten_kernel,
+        functools.partial(shorten_kernel, nq),
         grid=(blocks,),
-        out_shape=jax.ShapeDtypeStruct((STRIDE, per_t, 2, nq, lat, lanes), jnp.bfloat16),
+        out_shape=jax.ShapeDtypeStruct((groups_n, kv_rows, lanes), jnp.bfloat16),
         in_specs=[
             pl.BlockSpec((rows, lanes), lambda b: (0, b)),
-            pl.BlockSpec((KERNEL - STRIDE, lanes), lambda b: (0, b)),
+            pl.BlockSpec(extras.shape, lambda b: (0, 0, 0)),
             pl.BlockSpec((KERNEL, STRIDE, lanes), lambda b: (0, 0, b)),
             pl.BlockSpec((KERNEL, STRIDE, lanes), lambda b: (0, 0, b)),
         ],
-        out_specs=pl.BlockSpec(
-            (STRIDE, 1, 2, 1, lat, lanes), lambda b: (0, b // nq, 0, b % nq, 0, 0)
-        ),
+        out_specs=pl.BlockSpec((groups_n, kv_rows, lanes), lambda b: (0, 0, 0)),
         cost_estimate=pl.CostEstimate(
             flops=4 * KERNEL * rows * channels,
             bytes_accessed=4 * rows * channels + 2 * KERNEL * STRIDE * channels * 4 + 2 * rows * channels * 2,
             transcendentals=0,
         ),
-    )(byte_states, rim_rows, qk_kernel, value_kernel)
+    )(byte_states, extras, qk_kernel, value_kernel)
+
+
+def split_hi_lo(value):
+    hi = value.astype(jnp.bfloat16)
+    lo = (value - hi.astype(jnp.float32)).astype(jnp.bfloat16)
+    return hi, lo
+
+
+def edge_terms(byte_states, qk_kernel, value_kernel, per_t, nq):
+    rows, channels = byte_states.shape
+    kern = jnp.stack([qk_kernel, value_kernel], 0)
+    first = jnp.einsum("kc,wktc->wtc", byte_states[:STRIDE], kern[:, STRIDE:], precision=lax.Precision.HIGHEST)
+    last = jnp.einsum(
+        "kc,wktc->wtc", byte_states[rows - STRIDE :], kern[:, :STRIDE], precision=lax.Precision.HIGHEST
+    )
+    pieces = jnp.stack(split_hi_lo(first) + split_hi_lo(last), 0)
+    pieces = pieces.reshape(4, 2, STRIDE, per_t, nq, CHANNEL_WIDTH).transpose(2, 3, 0, 1, 4, 5)
+    pieces = pieces.reshape(STRIDE * per_t, 8 * nq, CHANNEL_WIDTH)
+    pad = -(-8 * nq // 16) * 16 - 8 * nq
+    return jnp.pad(pieces, ((0, 0), (0, pad), (0, 0)))
 
 
 def up_kernel_fn(copies_n, per_t, nq, qr, lim_ref, ret_ref, x_ref, up_ref, out_ref):
@@ -128,7 +156,6 @@
     n_ctx = lax.axis_size("ctx")
     device = lax.axis_index("ctx")
     lat_total = lat_dev * n_ctx
-    rim_rows = shifted(byte_states[rows_here - (KERNEL - STRIDE) :], "ctx", 1)
     local_heads = STRIDE * channels // CHANNEL_WIDTH
     copies_n = max(1, n_ctx // local_heads)
     groups_n = n_ctx // copies_n
@@ -139,15 +166,25 @@
 
     nq = head_here
     per_t = channels // head_width
-    both_local = shorten_both(byte_states, rim_rows, qk_kernel, value_kernel, per_t, nq)
-    both_local = both_local.reshape(groups_n, 2 * nq, lat_dev, CHANNEL_WIDTH)
+    extras = edge_terms(byte_states, qk_kernel, value_kernel, per_t, nq)
+    both_local = shorten_both(byte_states, extras, qk_kernel, value_kernel, groups_n, nq)
+    kv_rows = both_local.shape[1]
     if copies_n > 1:
         both_local = jnp.broadcast_to(
-            both_local[:, None], (groups_n, copies_n, 2 * nq, lat_dev, CHANNEL_WIDTH)
-        ).reshape(n_ctx, 2 * nq, lat_dev, CHANNEL_WIDTH)
+            both_local[:, None], (groups_n, copies_n, kv_rows, CHANNEL_WIDTH)
+        ).reshape(n_ctx, kv_rows, CHANNEL_WIDTH)
     both_all = lax.all_to_all(both_local, "ctx", split_axis=0, concat_axis=0, tiled=True)
-    key_all = both_all[:, :nq]
-    value_all = both_all[:, nq:]
+    main_kv = both_all[:, : 2 * nq * lat_dev].reshape(n_ctx, 2 * nq, lat_dev, CHANNEL_WIDTH)
+    edge = both_all[:, 2 * nq * lat_dev : 2 * nq * lat_dev + 8 * nq].astype(jnp.float32)
+    edge = edge.reshape(n_ctx, 4, 2 * nq, CHANNEL_WIDTH)
+    own_first = edge[:, 0] + edge[:, 1]
+    from_before = edge[:, 2] + edge[:, 3]
+    from_before = jnp.concatenate([jnp.zeros_like(from_before[:1]), from_before[:-1]], 0)
+    first_rows = (own_first + from_before).astype(jnp.bfloat16)
+    at_first = lax.broadcasted_iota(jnp.int32, main_kv.shape, 2) == 0
+    main_kv = jnp.where(at_first, first_rows[:, :, None, :], main_kv)
+    key_all = main_kv[:, :nq]
+    value_all = main_kv[:, nq:]
     queries = key_all.reshape(n_ctx, nq, copies_n, query_rows, CHANNEL_WIDTH)[:, :, 0]
     if copies_n > 1:
         queries = lax.dynamic_index_in_dim(

time: 51.4 us -> 49.4 us (0.961)
  starting transfers between devices: 15.1 us -> 10.9 us
  waiting for transfers between devices: 22.3 us -> 23.6 us
  other arithmetic: 1.82 us -> 2.86 us
    ppermute x1 -> x0, starting transfers between devices: 4.83 us -> none  [shifted(): return lax.ppermute(x, axis, pairs)]
    all_to_all x1, waiting for transfers between devices: 12 us -> 13.9 us  [body(): lax.all_to_all(both_local, 'ctx', split_axis=0, concat_axis=0, tiled=True)]
    ppermute x1 -> x0, waiting for transfers between devices: 1.35 us -> none  [shifted(): return lax.ppermute(x, axis, pairs)]
    dot_general x0 -> x1, other arithmetic: none -> 0.86 us  [edge_terms(): jnp.einsum('kc,wktc->wtc', byte_states[:STRIDE], kern[:, STRIDE:], precis...]
    all_to_all x1, waiting for transfers between devices: 8.93 us -> 9.75 us  [body(): lax.all_to_all(outgoing, 'ctx', split_axis=0, concat_axis=0, tiled=True)]
    slice x1 -> x3, local copies, waits for them, and re-layouts: 0.73 us -> 0.05 us  [the longest x1 0.04 us: body(): both_all[:, :2 * nq * lat_dev]]
    all_to_all x1, starting transfers between devices: 6.6 us -> 7.25 us  [body(): lax.all_to_all(both_local, 'ctx', split_axis=0, concat_axis=0, tiled=True)]
    transpose x0 -> x1, local copies, waits for them, and re-layouts: none -> 0.64 us  [edge_terms(): pieces.reshape(4, 2, STRIDE, per_t, nq, CHANNEL_WIDTH)]
  transfers between devices with their start and end apart: 3 -> 2, of which waited for: 3 -> 2; matrix products, arithmetic and copies ran while one was open for 1% -> 1% of each run, Pallas kernels for 0% -> 0%
where the time goes in v3:
time: 49.4 us; the launch traced here: 48.9 us
  waiting for transfers between devices  23.6 us (48%)
  starting transfers between devices  10.9 us (22%)
  Pallas kernels  6.7 us (14%)
  other arithmetic  2.86 us (6%)
  local copies, waits for them, and re-layouts  2.42 us (5%)
  matrix products  1.52 us (3%)
  between operations  0.83 us (2%)
    all_to_all x1, waiting for transfers between devices, body(): lax.all_to_all(both_local, 'ctx', split_axis=0, concat_axis=0, tiled=True)  13.9 us
    all_to_all x1, waiting for transfers between devices, body(): lax.all_to_all(outgoing, 'ctx', split_axis=0, concat_axis=0, tiled=True)  9.75 us
    all_to_all x1, starting transfers between devices, body(): lax.all_to_all(both_local, 'ctx', split_axis=0, concat_axis=0, tiled=True)  7.25 us
    all_to_all x1, starting transfers between devices, body(): lax.all_to_all(outgoing, 'ctx', split_axis=0, concat_axis=0, tiled=True)  3.64 us
    pallas_call x1, Pallas kernels, up_and_mix(): pl.pallas_call(functools.partial(up_kernel_fn, copies_n, per_t, nq, qr),...  3.52 us
    pallas_call x1, Pallas kernels, shorten_both(): pl.pallas_call(functools.partial(shorten_kernel, nq), grid=(blocks,), out...  3.18 us
    unnamed x5, local copies, waits for them, and re-layouts  1.46 us
  transfers between devices with their start and end apart: 2, of which 2 were waited for; matrix products, arithmetic and copies ran while one was open for 1% of the time, Pallas kernels for 0%

profile of v3, /device:TPU:0, one launch (start us, length us, event | category | flops | bytes accessed | tf_op | source)
XLA Modules:
  0.0 48.9 jit_solution(8703430456108184527)
XLA Ops:
  0.0 0.0 copy-start.1
  0.0 0.8 %slice_bitcast_fusion.4 = (f32[512,4]{0,1:T(4,128)S(1)}, f32[512,4]{0,1:T(4,128)S(1)}) fusion(f32[256,512]{1,0:T(8,128)} %x_ref.3), kind=kLoop, calls=%fused_computation.43 | loop fusion | bytes 32768
  0.8 0.9 %fusion.14 = (f32[512,2,4]{0,2,1:T(4,128)S(1)}, f32[512,2,4]{0,2,1:T(4,128)S(1)}) fusion(f32[1,8,4,512]{3,2,1,0:T(4,128)} %bitcast.92, f32[1,8,4,512]{3,2,1,0:T(4,128)} %bitcast.93, f32[512,4]{0,1:T(4,128)S(1)} %get-tuple-element.75, f32[512,4]{0,1:T(4,128)S(1)} %get-tuple-element.74), kind=kLoop, calls=%fused_computation.23 | loop fusion | flops 90112 | bytes 180224 | tf_op jit(solution)/shard_map/kc,wktc->wtc/dot_general | solution.py:84
  1.7 0.6 %copy.13 = bf16[4,2,4,2,2,128]{5,4,3,2,1,0:T(2,128)(2,1)} copy(bf16[4,2,4,2,2,128]{5,0,4,1,3,2:T(4,128)(2,1)S(1)} %maximum_bitcast_fusion) | data formatting | bytes 65536 | tf_op jit(solution)/shard_map/transpose | solution.py:89
  2.3 3.2 %shard_map.64 = bf16[8,272,128]{2,1,0:T(8,128)(2,1)} custom-call(f32[256,512]{1,0:T(8,128)} %x_ref.3, bf16[8,16,128]{2,1,0:T(8,128)(2,1)} %bitcast.94, f32[8,4,512]{2,1,0:T(4,128)} %qk_ref.1, f32[8,4,512]{2,1,0:T(4,128)} %vk_ref.1), custom_call_target="tpu_custom_call" | custom-call | flops 4194304 | bytes 1179648 | tf_op jit(solution)/shard_map/pallas_call | solution.py:56
  5.5 7.3 %all-to-all-start = ((bf16[8,272,128]{2,1,0:T(8,128)(2,1)}), bf16[8,272,128]{2,1,0:T(8,128)(2,1)S(1)}, u32[]{:S(2)}, u32[]{:S(2)}) async-start(bf16[8,272,128]{2,1,0:T(8,128)(2,1)} %shard_map.64), calls=%async_computation | async-start | bytes 1114112 | tf_op jit(solution)/shard_map/all_to_all | solution.py:176
  13.4 0.1 iota_add_fusion
  13.5 0.1 add.89
  13.6 0.1 pad.4.clone
  13.7 0.0 copy-done.1
  13.7 0.4 fusion.9
  14.0 13.9 %all-to-all-done = bf16[8,272,128]{2,1,0:T(8,128)(2,1)S(1)} async-done(((bf16[8,272,128]{2,1,0:T(8,128)(2,1)}), bf16[8,272,128]{2,1,0:T(8,128)(2,1)S(1)}, u32[]{:S(2)}, u32[]{:S(2)}) %all-to-all-start) | async-done | bytes 557088 | tf_op jit(solution)/shard_map/all_to_all | solution.py:176
  28.0 0.1 broadcast_select_fusion
  28.2 0.5 %select_reduce_fusion = (f32[2,512]{1,0:T(2,128)S(1)}, f32[2,512,512]{1,2,0:T(8,128)S(1)}) fusion(f32[512]{0:T(512)S(1)} %log_multiply_fusion, pred[512,512]{0,1:T(8,128)(4,1)S(1)} %fusion.9, bf16[2,512,128]{2,1,0:T(8,128)(2,1)S(1)} %bitcast.84), kind=kOutput, calls=%fused_computation.1 | convolution fusion | flops 135789568 | bytes 2627584 | tf_op jit(solution)/shard_map/while/body/eval_jaxpr/hqd,hkd->hqk/dot_general | solution.py:219
  28.8 0.5 %fusion = f32[2,512]{1,0:T(2,128)S(1)} fusion(f32[2,512,512]{1,2,0:T(8,128)S(1)} %get-tuple-element.83, f32[2,512]{1,0:T(2,128)S(1)} %broadcast_maximum_fusion, f32[512]{0:T(512)S(1)} %log_multiply_fusion, pred[512,512]{0,1:T(8,128)(4,1)S(1)} %fusion.9), kind=kLoop, calls=%fused_computation.2 | loop fusion | flops 2096128 | bytes 2369536 | tf_op jit(solution)/shard_map/while/body/eval_jaxpr/reduce_sum | solution.py:232
  29.3 1.0 %fusion.3 = bf16[2,512,128]{2,1,0:T(8,128)(2,1)S(1)} fusion(bf16[2,512,128]{2,1,0:T(8,128)(2,1)S(1)} %bitcast.90, f32[2,512,512]{1,2,0:T(8,128)S(1)} %get-tuple-element.83, f32[2,512]{1,0:T(2,128)S(1)} %broadcast_maximum_fusion, f32[512]{0:T(512)S(1)} %log_multiply_fusion, pred[512,512]{0,1:T(8,128)(4,1)S(1)} %fusion.9, f32[2,512]{1,0:T(2,128)S(1)} %get-tuple-element.81, ...), kind=kOutput, calls=%fused_computation.6 | convolution fusion | flops 136708096 | bytes 2897920 | tf_op jit(solution)/shard_map/while/body/eval_jaxpr/hqk,hkd->hqd/dot_general | solution.py:233
  30.4 0.8 %maximum_maximum_fusion = bf16[8,144,128]{2,1,0:T(8,128)(2,1)} fusion(bf16[8,4,128]{2,1,0:T(4,128)(2,1)S(1)} %bitcast.95, bf16[8,128,128]{2,1,0:T(8,128)(2,1)S(1)} %bitcast.87, bf16[144]{0:T(256)(128)(2,1)S(1)} %pad.4.clone), kind=kLoop, calls=%fused_computation.15 | loop fusion | flops 884736 | bytes 565536 | tf_op jit(solution)/shard_map/concatenate | solution.py:256
  31.2 3.6 %all-to-all-start.1 = ((bf16[8,144,128]{2,1,0:T(8,128)(2,1)}), bf16[8,144,128]{2,1,0:T(8,128)(2,1)S(1)}, u32[]{:S(2)}, u32[]{:S(2)}) async-start(bf16[8,144,128]{2,1,0:T(8,128)(2,1)} %maximum_maximum_fusion), calls=%async_computation.1 | async-start | bytes 589824 | tf_op jit(solution)/shard_map/all_to_all | solution.py:264
  34.9 9.7 %all-to-all-done.1.ret_ref = bf16[8,144,128]{2,1,0:T(8,128)(2,1)S(1)} async-done(((bf16[8,144,128]{2,1,0:T(8,128)(2,1)}), bf16[8,144,128]{2,1,0:T(8,128)(2,1)S(1)}, u32[]{:S(2)}, u32[]{:S(2)}) %all-to-all-start.1) | async-done | bytes 294944 | tf_op jit(solution)/shard_map/all_to_all | solution.py:264
  44.6 0.0 copy-start
  44.6 0.7 %copy-done = bf16[8,144,128]{2,1,0:T(8,128)(2,1)} copy-done((bf16[8,144,128]{2,1,0:T(8,128)(2,1)}, bf16[8,144,128]{2,1,0:T(8,128)(2,1)S(1)}, u32[]{:S(2)}) %copy-start) | copy-done | bytes 294936
  45.3 3.5 %shard_map.65 = f32[256,512]{1,0:T(8,128)} custom-call(s32[1]{0:T(128)} %bitcast.5.lim_ref, bf16[8,144,128]{2,1,0:T(8,128)(2,1)} %copy-done, f32[256,512]{1,0:T(8,128)} %x_ref.3, f32[8,4,512]{2,1,0:T(4,128)} %up_ref.1), custom_call_target="tpu_custom_call" | custom-call | flops 4194304 | bytes 1343488 | tf_op jit(solution)/shard_map/pallas_call | solution.py:134
  (21 shorter events, 0.3 us)
Async XLA Ops:
  0.0 13.7 %copy-start.1 = (s32[512]{0:T(512)S(1)}, s32[512]{0:T(512)}, u32[]{:S(2)}) copy-start(s32[512]{0:T(512)} %param.8) | copy-start | bytes 6148
  5.5 22.4 %all-to-all-start = ((bf16[8,272,128]{2,1,0:T(8,128)(2,1)}), bf16[8,272,128]{2,1,0:T(8,128)(2,1)S(1)}, u32[]{:S(2)}, u32[]{:S(2)}) async-start(bf16[8,272,128]{2,1,0:T(8,128)(2,1)} %shard_map.64), calls=%async_computation | async-start | bytes 1114112 | tf_op jit(solution)/shard_map/all_to_all | solution.py:176
  31.2 13.4 %all-to-all-start.1 = ((bf16[8,144,128]{2,1,0:T(8,128)(2,1)}), bf16[8,144,128]{2,1,0:T(8,128)(2,1)S(1)}, u32[]{:S(2)}, u32[]{:S(2)}) async-start(bf16[8,144,128]{2,1,0:T(8,128)(2,1)} %maximum_maximum_fusion), calls=%async_computation.1 | async-start | bytes 589824 | tf_op jit(solution)/shard_map/all_to_all | solution.py:264
  44.6 0.7 %copy-start = (bf16[8,144,128]{2,1,0:T(8,128)(2,1)}, bf16[8,144,128]{2,1,0:T(8,128)(2,1)S(1)}, u32[]{:S(2)}) copy-start(bf16[8,144,128]{2,1,0:T(8,128)(2,1)S(1)} %all-to-all-done.1.ret_ref) | copy-start | bytes 884740

commit v4 on v2

--- a/solution.py
+++ b/solution.py
@@ -19,103 +19,130 @@
     return lax.ppermute(x, axis, pairs)
 
 
-def shorten_kernel(x_ref, rim_ref, qk_ref, vk_ref, out_ref):
-    rows, lanes = x_ref.shape
-    lat = rows // STRIDE
-    first_row = lax.broadcasted_iota(jnp.int32, (lat, lanes), 0) == 0
-    taps = [None] * KERNEL
-    for k in range(STRIDE):
-        current = x_ref[pl.ds(k, lat, stride=STRIDE), :]
-        earlier = pltpu.roll(current, 1, 0)
-        earlier = jnp.where(first_row, rim_ref[pl.ds(k, 1), :], earlier)
-        taps[k] = earlier
-        taps[k + STRIDE] = current
-    for which, kern_ref in enumerate((qk_ref, vk_ref)):
-        for t in range(STRIDE):
-            total = taps[0] * kern_ref[0, pl.ds(t, 1), :]
-            for k in range(1, KERNEL):
-                total = total + taps[k] * kern_ref[k, pl.ds(t, 1), :]
-            out_ref[t, 0, which, 0] = total.astype(jnp.bfloat16)
-
-
-def shorten_both(byte_states, rim_rows, qk_kernel, value_kernel, per_t, nq):
-    rows, channels = byte_states.shape
+def three_bf16(value):
+    hi = value.astype(jnp.bfloat16)
+    rest = value - hi.astype(jnp.float32)
+    mid = rest.astype(jnp.bfloat16)
+    lo = (rest - mid.astype(jnp.float32)).astype(jnp.bfloat16)
+    return hi, mid, lo
+
+
+def exact_rows(select, value):
+    total = None
+    for piece in three_bf16(value):
+        part = jnp.dot(select, piece, preferred_element_type=jnp.float32)
+        total = part if total is None else total + part
+    return total
+
+
+def split_pair(value):
+    hi = value.astype(jnp.bfloat16)
+    lo = (value - hi.astype(jnp.float32)).astype(jnp.bfloat16)
+    return hi, lo
+
+
+def shorten_kernel(per_t, nq, x_ref, qk_ref, vk_ref, out_ref):
+    rows, channels = x_ref.shape
     lat = rows // STRIDE
     lanes = CHANNEL_WIDTH
     blocks = channels // lanes
+    pick_row = lax.broadcasted_iota(jnp.int32, (rows, rows), 0)
+    pick_col = lax.broadcasted_iota(jnp.int32, (rows, rows), 1)
+    pick = (pick_col == (pick_row % lat) * STRIDE + pick_row // lat).astype(jnp.bfloat16)
+    by_phase = exact_rows(pick, x_ref[...])
+    phase = [by_phase[s * lat : (s + 1) * lat] for s in range(STRIDE)]
+    first_row = lax.broadcasted_iota(jnp.int32, (lat, channels), 0) == 0
+    edge_row = lax.broadcasted_iota(jnp.int32, (16, lanes), 0)
+    edge = [jnp.zeros((16, lanes), jnp.float32) for _ in range(STRIDE * per_t)]
+    for which, kern_ref in enumerate((qk_ref, vk_ref)):
+        for t in range(STRIDE):
+            own = phase[0] * kern_ref[STRIDE, pl.ds(t, 1), :]
+            before = phase[0] * kern_ref[0, pl.ds(t, 1), :]
+            for s in range(1, STRIDE):
+                own = own + phase[s] * kern_ref[STRIDE + s, pl.ds(t, 1), :]
+                before = before + phase[s] * kern_ref[s, pl.ds(t, 1), :]
+            total = own + jnp.where(first_row, 0.0, pltpu.roll(before, 1, 0))
+            total = total.astype(jnp.bfloat16)
+            own_hi, own_lo = split_pair(own[0:1])
+            next_hi, next_lo = split_pair(before[lat - 1 : lat])
+            for block in range(blocks):
+                lane = slice(block * lanes, (block + 1) * lanes)
+                g = t * per_t + block // nq
+                slot = which * nq + block % nq
+                out_ref[g, pl.ds(slot * lat, lat), :] = total[:, lane]
+                for e, piece in enumerate((own_hi, own_lo, next_hi, next_lo)):
+                    edge[g] = jnp.where(edge_row == e * 2 * nq + slot, piece[:, lane].astype(jnp.float32), edge[g])
+    for g in range(STRIDE * per_t):
+        out_ref[g, pl.ds(2 * nq * lat, 16), :] = edge[g].astype(jnp.bfloat16)
+
+
+def shorten_both(byte_states, qk_kernel, value_kernel, groups_n, per_t, nq):
+    rows, channels = byte_states.shape
+    lat = rows // STRIDE
+    kv_rows = 2 * nq * lat + 16
+    vmem = pl.BlockSpec(memory_space=pltpu.VMEM)
     return pl.pallas_call(
-        shorten_kernel,
-        grid=(blocks,),
-        out_shape=jax.ShapeDtypeStruct((STRIDE, per_t, 2, nq, lat, lanes), jnp.bfloat16),
-        in_specs=[
-            pl.BlockSpec((rows, lanes), lambda b: (0, b)),
-            pl.BlockSpec((KERNEL - STRIDE, lanes), lambda b: (0, b)),
-            pl.BlockSpec((KERNEL, STRIDE, lanes), lambda b: (0, 0, b)),
-            pl.BlockSpec((KERNEL, STRIDE, lanes), lambda b: (0, 0, b)),
-        ],
-        out_specs=pl.BlockSpec(
-            (STRIDE, 1, 2, 1, lat, lanes), lambda b: (0, b // nq, 0, b % nq, 0, 0)
-        ),
+        functools.partial(shorten_kernel, per_t, nq),
+        out_shape=jax.ShapeDtypeStruct((groups_n, kv_rows, CHANNEL_WIDTH), jnp.bfloat16),
+        in_specs=[vmem] * 3,
+        out_specs=vmem,
         cost_estimate=pl.CostEstimate(
-            flops=4 * KERNEL * rows * channels,
+            flops=4 * KERNEL * rows * channels + 6 * rows * rows * channels,
             bytes_accessed=4 * rows * channels + 2 * KERNEL * STRIDE * channels * 4 + 2 * rows * channels * 2,
             transcendentals=0,
         ),
-    )(byte_states, rim_rows, qk_kernel, value_kernel)
+    )(byte_states, qk_kernel, value_kernel)
 
 
 def up_kernel_fn(copies_n, per_t, nq, qr, lim_ref, ret_ref, x_ref, up_ref, out_ref):
-    rows, lanes = x_ref.shape
+    rows, channels = x_ref.shape
     lat = rows // STRIDE
-    block = pl.program_id(0)
-    sub = block // nq
-    q = block % nq
-    row = lax.broadcasted_iota(jnp.int32, (lat, lanes), 0)
+    lanes = CHANNEL_WIDTH
+    blocks = channels // lanes
+    row = lax.broadcasted_iota(jnp.int32, (lat, channels), 0)
     prior_one = []
     prior_two = []
     for t in range(STRIDE):
-        g = t * per_t + sub
-        parts = [
-            ret_ref[g * copies_n + s, pl.ds(pl.multiple_of(q * qr, qr), qr), :] for s in range(copies_n)
-        ]
-        att = (parts[0] if copies_n == 1 else jnp.concatenate(parts, 0)).astype(jnp.float32)
-        rims = ret_ref[g * copies_n + copies_n - 1, pl.ds(nq * qr, 2 * nq), :].astype(jnp.float32)
-        rim = rims[0:2]
-        for other in range(1, nq):
-            rim = jnp.where(q == other, rims[2 * other : 2 * other + 2], rim)
-        one = pltpu.roll(att, 1, 0)
-        one = jnp.where(row == 0, rim[1:2], one)
-        two = pltpu.roll(att, 2, 0)
-        two = jnp.where(row == 0, rim[0:1], jnp.where(row == 1, rim[1:2], two))
+        att_parts = []
+        rim_parts = []
+        for block in range(blocks):
+            g = t * per_t + block // nq
+            q = block % nq
+            pieces = [ret_ref[g * copies_n + s, pl.ds(q * qr, qr), :] for s in range(copies_n)]
+            att_parts.append(pieces[0] if copies_n == 1 else jnp.concatenate(pieces, 0))
+            rim_parts.append(ret_ref[g * copies_n + copies_n - 1, pl.ds(nq * qr + 2 * q, 2), :])
+        att = jnp.concatenate(att_parts, 1).astype(jnp.float32)
+        rim = jnp.concatenate(rim_parts, 1).astype(jnp.float32)
+        one = jnp.where(row == 0, rim[1:2], pltpu.roll(att, 1, 0))
+        two = jnp.where(row == 0, rim[0:1], jnp.where(row == 1, rim[1:2], pltpu.roll(att, 2, 0)))
         prior_one.append(one)
         prior_two.append(two)
-    limit = lim_ref[0]
+    by_phase = []
     for s in range(STRIDE):
         total = prior_one[0] * up_ref[s, pl.ds(0, 1), :] + prior_two[0] * up_ref[s + STRIDE, pl.ds(0, 1), :]
         for t in range(1, STRIDE):
             total = total + prior_one[t] * up_ref[s, pl.ds(t, 1), :]
             total = total + prior_two[t] * up_ref[s + STRIDE, pl.ds(t, 1), :]
-        here = x_ref[pl.ds(s, lat, stride=STRIDE), :]
-        inside = row * STRIDE + s < limit
-        out_ref[pl.ds(s, lat, stride=STRIDE), :] = here + jnp.where(inside, total, 0.0)
+        by_phase.append(total)
+    by_phase = jnp.concatenate(by_phase, 0)
+    put_row = lax.broadcasted_iota(jnp.int32, (rows, rows), 0)
+    put_col = lax.broadcasted_iota(jnp.int32, (rows, rows), 1)
+    put = (put_col == (put_row % STRIDE) * lat + put_row // STRIDE).astype(jnp.bfloat16)
+    branch = exact_rows(put, by_phase)
+    byte_row = lax.broadcasted_iota(jnp.int32, (rows, channels), 0)
+    out_ref[...] = x_ref[...] + jnp.where(byte_row < lim_ref[0], branch, 0.0)
 
 
 def up_and_mix(limit, returned, byte_states, up_kernel, copies_n, per_t, nq, qr):
     rows, channels = byte_states.shape
-    lanes = CHANNEL_WIDTH
+    vmem = pl.BlockSpec(memory_space=pltpu.VMEM)
     return pl.pallas_call(
         functools.partial(up_kernel_fn, copies_n, per_t, nq, qr),
-        grid=(channels // lanes,),
         out_shape=jax.ShapeDtypeStruct((rows, channels), jnp.float32),
-        in_specs=[
-            pl.BlockSpec(memory_space=pltpu.SMEM),
-            pl.BlockSpec(returned.shape, lambda b: (0, 0, 0)),
-            pl.BlockSpec((rows, lanes), lambda b: (0, b)),
-            pl.BlockSpec((KERNEL, STRIDE, lanes), lambda b: (0, 0, b)),
-        ],
-        out_specs=pl.BlockSpec((rows, lanes), lambda b: (0, b)),
+        in_specs=[pl.BlockSpec(memory_space=pltpu.SMEM), vmem, vmem, vmem],
+        out_specs=vmem,
         cost_estimate=pl.CostEstimate(
-            flops=4 * KERNEL * rows * channels,
+            flops=4 * KERNEL * rows * channels + 6 * rows * rows * channels,
             bytes_accessed=8 * rows * channels + returned.size * 2,
             transcendentals=0,
         ),
@@ -128,7 +155,6 @@
     n_ctx = lax.axis_size("ctx")
     device = lax.axis_index("ctx")
     lat_total = lat_dev * n_ctx
-    rim_rows = shifted(byte_states[rows_here - (KERNEL - STRIDE) :], "ctx", 1)
     local_heads = STRIDE * channels // CHANNEL_WIDTH
     copies_n = max(1, n_ctx // local_heads)
     groups_n = n_ctx // copies_n
@@ -139,15 +165,24 @@
 
     nq = head_here
     per_t = channels // head_width
-    both_local = shorten_both(byte_states, rim_rows, qk_kernel, value_kernel, per_t, nq)
-    both_local = both_local.reshape(groups_n, 2 * nq, lat_dev, CHANNEL_WIDTH)
+    both_local = shorten_both(byte_states, qk_kernel, value_kernel, groups_n, per_t, nq)
+    kv_rows = both_local.shape[1]
     if copies_n > 1:
         both_local = jnp.broadcast_to(
-            both_local[:, None], (groups_n, copies_n, 2 * nq, lat_dev, CHANNEL_WIDTH)
-        ).reshape(n_ctx, 2 * nq, lat_dev, CHANNEL_WIDTH)
+            both_local[:, None], (groups_n, copies_n, kv_rows, CHANNEL_WIDTH)
+        ).reshape(n_ctx, kv_rows, CHANNEL_WIDTH)
     both_all = lax.all_to_all(both_local, "ctx", split_axis=0, concat_axis=0, tiled=True)
-    key_all = both_all[:, :nq]
-    value_all = both_all[:, nq:]
+    main_kv = both_all[:, : 2 * nq * lat_dev].reshape(n_ctx, 2 * nq, lat_dev, CHANNEL_WIDTH)
+    edge = both_all[:, 2 * nq * lat_dev : 2 * nq * lat_dev + 8 * nq].astype(jnp.float32)
+    edge = edge.reshape(n_ctx, 4, 2 * nq, CHANNEL_WIDTH)
+    own_first = edge[:, 0] + edge[:, 1]
+    from_before = edge[:, 2] + edge[:, 3]
+    from_before = jnp.concatenate([jnp.zeros_like(from_before[:1]), from_before[:-1]], 0)
+    first_rows = (own_first + from_before).astype(jnp.bfloat16)
+    at_first = lax.broadcasted_iota(jnp.int32, main_kv.shape, 2) == 0
+    main_kv = jnp.where(at_first, first_rows[:, :, None, :], main_kv)
+    key_all = main_kv[:, :nq]
+    value_all = main_kv[:, nq:]
     queries = key_all.reshape(n_ctx, nq, copies_n, query_rows, CHANNEL_WIDTH)[:, :, 0]
     if copies_n > 1:
         queries = lax.dynamic_index_in_dim(

time: 51.4 us -> 46.1 us (0.90)
  starting transfers between devices: 15.1 us -> 10.9 us
  waiting for transfers between devices: 22.3 us -> 23.6 us
  local copies, waits for them, and re-layouts: 2.32 us -> 1.04 us
  Pallas kernels: 6.99 us -> 5.88 us
    ppermute x1 -> x0, starting transfers between devices: 4.83 us -> none  [shifted(): return lax.ppermute(x, axis, pairs)]
    all_to_all x1, waiting for transfers between devices: 12 us -> 13.9 us  [body(): lax.all_to_all(both_local, 'ctx', split_axis=0, concat_axis=0, tiled=True)]
    ppermute x1 -> x0, waiting for transfers between devices: 1.35 us -> none  [shifted(): return lax.ppermute(x, axis, pairs)]
    pallas_call x1, Pallas kernels: 3.52 us -> 2.7 us  [up_and_mix(): pl.pallas_call(functools.partial(up_kernel_fn, copies_n, per_t, nq, qr),...]
    all_to_all x1, waiting for transfers between devices: 8.93 us -> 9.75 us  [body(): lax.all_to_all(outgoing, 'ctx', split_axis=0, concat_axis=0, tiled=True)]
    slice x1 -> x3, local copies, waits for them, and re-layouts: 0.73 us -> 0.05 us  [the longest x1 0.04 us: body(): both_all[:, :2 * nq * lat_dev]]
    all_to_all x1, starting transfers between devices: 6.6 us -> 7.25 us  [body(): lax.all_to_all(both_local, 'ctx', split_axis=0, concat_axis=0, tiled=True)]
    unnamed x6 -> x4, local copies, waits for them, and re-layouts: 1.31 us -> 0.71 us
  transfers between devices with their start and end apart: 3 -> 2, of which waited for: 3 -> 2; matrix products, arithmetic and copies ran while one was open for 1% -> 1% of each run, Pallas kernels for 0% -> 0%
where the time goes in v4:
time: 46.1 us; the launch traced here: 45.7 us
  waiting for transfers between devices  23.6 us (51%)
  starting transfers between devices  10.9 us (24%)
  Pallas kernels  5.88 us (13%)
  other arithmetic  1.96 us (4%)
  matrix products  1.53 us (3%)
  local copies, waits for them, and re-layouts  1.04 us (2%)
  between operations  0.81 us (2%)
    all_to_all x1, waiting for transfers between devices, body(): lax.all_to_all(both_local, 'ctx', split_axis=0, concat_axis=0, tiled=True)  13.9 us
    all_to_all x1, waiting for transfers between devices, body(): lax.all_to_all(outgoing, 'ctx', split_axis=0, concat_axis=0, tiled=True)  9.75 us
    all_to_all x1, starting transfers between devices, body(): lax.all_to_all(both_local, 'ctx', split_axis=0, concat_axis=0, tiled=True)  7.25 us
    all_to_all x1, starting transfers between devices, body(): lax.all_to_all(outgoing, 'ctx', split_axis=0, concat_axis=0, tiled=True)  3.63 us
    pallas_call x1, Pallas kernels, shorten_both(): pl.pallas_call(functools.partial(shorten_kernel, per_t, nq), out_shape=ja...  3.18 us
    pallas_call x1, Pallas kernels, up_and_mix(): pl.pallas_call(functools.partial(up_kernel_fn, copies_n, per_t, nq, qr),...  2.7 us
    dot_general x1, matrix products, attend(): jnp.einsum('hqk,hkd->hqd', weights.astype(jnp.bfloat16), value_block, pre...  0.98 us
  transfers between devices with their start and end apart: 2, of which 2 were waited for; matrix products, arithmetic and copies ran while one was open for 1% of the time, Pallas kernels for 0%

profile of v4, /device:TPU:0, one launch (start us, length us, event | category | flops | bytes accessed | tf_op | source)
XLA Modules:
  0.0 45.7 jit_solution(13157073465204798923)
XLA Ops:
  0.0 0.0 copy-start.1
  0.0 3.2 %shard_map.64 = bf16[8,272,128]{2,1,0:T(8,128)(2,1)} custom-call(f32[256,512]{1,0:T(8,128)} %x_ref.3, f32[8,4,512]{2,1,0:T(4,128)} %qk_ref.1, f32[8,4,512]{2,1,0:T(4,128)} %vk_ref.1), custom_call_target="tpu_custom_call" | custom-call | flops 205520896 | bytes 1179648 | tf_op jit(solution)/shard_map/pallas_call | solution.py:84
  3.2 7.3 %all-to-all-start = ((bf16[8,272,128]{2,1,0:T(8,128)(2,1)}), bf16[8,272,128]{2,1,0:T(8,128)(2,1)S(1)}, u32[]{:S(2)}, u32[]{:S(2)}) async-start(bf16[8,272,128]{2,1,0:T(8,128)(2,1)} %shard_map.64), calls=%async_computation | async-start | bytes 1114112 | tf_op jit(solution)/shard_map/all_to_all | solution.py:174
  11.1 0.1 iota_add_fusion
  11.2 0.1 add.89
  11.3 0.1 pad.4.clone
  11.4 0.0 copy-done.1
  11.4 0.4 fusion.9
  11.7 13.9 %all-to-all-done = bf16[8,272,128]{2,1,0:T(8,128)(2,1)S(1)} async-done(((bf16[8,272,128]{2,1,0:T(8,128)(2,1)}), bf16[8,272,128]{2,1,0:T(8,128)(2,1)S(1)}, u32[]{:S(2)}, u32[]{:S(2)}) %all-to-all-start) | async-done | bytes 557088 | tf_op jit(solution)/shard_map/all_to_all | solution.py:174
  25.7 0.1 broadcast_select_fusion
  25.9 0.5 %select_reduce_fusion = (f32[2,512]{1,0:T(2,128)S(1)}, f32[2,512,512]{1,2,0:T(8,128)S(1)}) fusion(f32[512]{0:T(512)S(1)} %log_multiply_fusion, pred[512,512]{0,1:T(8,128)(4,1)S(1)} %fusion.9, bf16[2,512,128]{2,1,0:T(8,128)(2,1)S(1)} %bitcast.47), kind=kOutput, calls=%fused_computation.1 | convolution fusion | flops 135789568 | bytes 2627584 | tf_op jit(solution)/shard_map/while/body/eval_jaxpr/hqd,hkd->hqk/dot_general | solution.py:217
  26.5 0.5 %fusion = f32[2,512]{1,0:T(2,128)S(1)} fusion(f32[2,512,512]{1,2,0:T(8,128)S(1)} %get-tuple-element.75, f32[2,512]{1,0:T(2,128)S(1)} %broadcast_maximum_fusion, f32[512]{0:T(512)S(1)} %log_multiply_fusion, pred[512,512]{0,1:T(8,128)(4,1)S(1)} %fusion.9), kind=kLoop, calls=%fused_computation.2 | loop fusion | flops 2096128 | bytes 2369536 | tf_op jit(solution)/shard_map/while/body/eval_jaxpr/reduce_sum | solution.py:230
  27.0 1.0 %fusion.3 = bf16[2,512,128]{2,1,0:T(8,128)(2,1)S(1)} fusion(bf16[2,512,128]{2,1,0:T(8,128)(2,1)S(1)} %bitcast.53, f32[2,512,512]{1,2,0:T(8,128)S(1)} %get-tuple-element.75, f32[2,512]{1,0:T(2,128)S(1)} %broadcast_maximum_fusion, f32[512]{0:T(512)S(1)} %log_multiply_fusion, pred[512,512]{0,1:T(8,128)(4,1)S(1)} %fusion.9, f32[2,512]{1,0:T(2,128)S(1)} %get-tuple-element.73, ...), kind=kOutput, calls=%fused_computation.6 | convolution fusion | flops 136708096 | bytes 2897920 | tf_op jit(solution)/shard_map/while/body/eval_jaxpr/hqk,hkd->hqd/dot_general | solution.py:231
  28.1 0.8 %maximum_maximum_fusion = bf16[8,144,128]{2,1,0:T(8,128)(2,1)} fusion(bf16[8,4,128]{2,1,0:T(4,128)(2,1)S(1)} %bitcast.55, bf16[8,128,128]{2,1,0:T(8,128)(2,1)S(1)} %bitcast.50, bf16[144]{0:T(256)(128)(2,1)S(1)} %pad.4.clone), kind=kLoop, calls=%fused_computation.15 | loop fusion | flops 884736 | bytes 565536 | tf_op jit(solution)/shard_map/concatenate | solution.py:254
  28.9 3.6 %all-to-all-start.1 = ((bf16[8,144,128]{2,1,0:T(8,128)(2,1)}), bf16[8,144,128]{2,1,0:T(8,128)(2,1)S(1)}, u32[]{:S(2)}, u32[]{:S(2)}) async-start(bf16[8,144,128]{2,1,0:T(8,128)(2,1)} %maximum_maximum_fusion), calls=%async_computation.1 | async-start | bytes 589824 | tf_op jit(solution)/shard_map/all_to_all | solution.py:262
  32.6 9.8 %all-to-all-done.1.ret_ref = bf16[8,144,128]{2,1,0:T(8,128)(2,1)S(1)} async-done(((bf16[8,144,128]{2,1,0:T(8,128)(2,1)}), bf16[8,144,128]{2,1,0:T(8,128)(2,1)S(1)}, u32[]{:S(2)}, u32[]{:S(2)}) %all-to-all-start.1) | async-done | bytes 294944 | tf_op jit(solution)/shard_map/all_to_all | solution.py:262
  42.3 0.0 copy-start
  42.3 0.7 %copy-done = bf16[8,144,128]{2,1,0:T(8,128)(2,1)} copy-done((bf16[8,144,128]{2,1,0:T(8,128)(2,1)}, bf16[8,144,128]{2,1,0:T(8,128)(2,1)S(1)}, u32[]{:S(2)}) %copy-start) | copy-done | bytes 294936
  43.0 2.7 %shard_map.65 = f32[256,512]{1,0:T(8,128)} custom-call(s32[1]{0:T(128)} %bitcast.1.lim_ref, bf16[8,144,128]{2,1,0:T(8,128)(2,1)} %copy-done, f32[256,512]{1,0:T(8,128)} %x_ref.3, f32[8,4,512]{2,1,0:T(4,128)} %up_ref.1), custom_call_target="tpu_custom_call" | custom-call | flops 205520896 | bytes 1343488 | tf_op jit(solution)/shard_map/pallas_call | solution.py:139
  (19 shorter events, 0.2 us)
Async XLA Ops:
  0.0 11.4 %copy-start.1 = (s32[512]{0:T(512)S(1)}, s32[512]{0:T(512)}, u32[]{:S(2)}) copy-start(s32[512]{0:T(512)} %param.8) | copy-start | bytes 6148
  3.2 22.4 %all-to-all-start = ((bf16[8,272,128]{2,1,0:T(8,128)(2,1)}), bf16[8,272,128]{2,1,0:T(8,128)(2,1)S(1)}, u32[]{:S(2)}, u32[]{:S(2)}) async-start(bf16[8,272,128]{2,1,0:T(8,128)(2,1)} %shard_map.64), calls=%async_computation | async-start | bytes 1114112 | tf_op jit(solution)/shard_map/all_to_all | solution.py:174
  28.9 13.4 %all-to-all-start.1 = ((bf16[8,144,128]{2,1,0:T(8,128)(2,1)}), bf16[8,144,128]{2,1,0:T(8,128)(2,1)S(1)}, u32[]{:S(2)}, u32[]{:S(2)}) async-start(bf16[8,144,128]{2,1,0:T(8,128)(2,1)} %maximum_maximum_fusion), calls=%async_computation.1 | async-start | bytes 589824 | tf_op jit(solution)/shard_map/all_to_all | solution.py:262
  42.3 0.7 %copy-start = (bf16[8,144,128]{2,1,0:T(8,128)(2,1)}, bf16[8,144,128]{2,1,0:T(8,128)(2,1)S(1)}, u32[]{:S(2)}) copy-start(bf16[8,144,128]{2,1,0:T(8,128)(2,1)S(1)} %all-to-all-done.1.ret_ref) | copy-start | bytes 884740

commit v5 on v4

--- a/solution.py
+++ b/solution.py
@@ -149,6 +149,62 @@
     )(limit, returned, byte_states, up_kernel)
 
 
+def attend_kernel(lat, qr, nq, denom, lim_ref, kv_ref, segq_ref, segk_ref, out_ref):
+    n_ctx = kv_ref.shape[0]
+    total = n_ctx * lat
+    lanes = CHANNEL_WIDTH
+    lat_len = lim_ref[0]
+    qpos = lax.broadcasted_iota(jnp.int32, (total, total), 0)
+    kpos = lax.broadcasted_iota(jnp.int32, (total, total), 1)
+    visible = (
+        (segk_ref[...] <= segq_ref[...])
+        & (kpos < lat_len)
+        & ((kpos != qpos) | (qpos == 0))
+    )
+    sharp = jnp.log(lax.broadcasted_iota(jnp.int32, (total, 1), 0).astype(jnp.float32) + 2.0) / denom
+    tile_row = lax.broadcasted_iota(jnp.int32, (16, lanes), 0)
+    tiles = [jnp.zeros((16, lanes), jnp.float32) for _ in range(n_ctx)]
+    for q in range(nq):
+        keys = jnp.concatenate([kv_ref[i, q] for i in range(n_ctx)], 0)
+        values = jnp.concatenate([kv_ref[i, nq + q] for i in range(n_ctx)], 0)
+        scores = lax.dot_general(
+            keys, keys, (((1,), (1,)), ((), ())), preferred_element_type=jnp.float32
+        ) * sharp
+        scores = jnp.where(visible, scores, -1e30)
+        top = jnp.max(scores, axis=1, keepdims=True)
+        weights = jnp.where(visible, jnp.exp(scores - top), 0.0)
+        sums = jnp.sum(weights, axis=1, keepdims=True)
+        rows = jnp.dot(weights.astype(jnp.bfloat16), values, preferred_element_type=jnp.float32)
+        rows = (rows / sums).astype(jnp.bfloat16)
+        for d in range(n_ctx):
+            out_ref[d, pl.ds(q * qr, qr), :] = rows[d * lat : (d + 1) * lat]
+        wide = rows.astype(jnp.float32)
+        for d in range(1, n_ctx):
+            for e in range(2):
+                at = d * lat - 2 + e
+                tiles[d] = jnp.where(tile_row == 2 * q + e, wide[at : at + 1], tiles[d])
+    for d in range(n_ctx):
+        out_ref[d, pl.ds(nq * qr, 16), :] = tiles[d].astype(jnp.bfloat16)
+
+
+def attend_whole(lat_len, main_kv, block_ids, nq, denom):
+    n_ctx, _, lat, lanes = main_kv.shape
+    total = n_ctx * lat
+    vmem = pl.BlockSpec(memory_space=pltpu.VMEM)
+    ret_rows = nq * lat + 16
+    return pl.pallas_call(
+        functools.partial(attend_kernel, lat, lat, nq, denom),
+        out_shape=jax.ShapeDtypeStruct((n_ctx, ret_rows, lanes), jnp.bfloat16),
+        in_specs=[pl.BlockSpec(memory_space=pltpu.SMEM), vmem, vmem, vmem],
+        out_specs=vmem,
+        cost_estimate=pl.CostEstimate(
+            flops=4 * nq * total * total * lanes,
+            bytes_accessed=main_kv.size * 2 + n_ctx * ret_rows * lanes * 2,
+            transcendentals=nq * total * total,
+        ),
+    )(lat_len, main_kv, block_ids.reshape(total, 1), block_ids.reshape(1, total))
+
+
 def body(byte_states, doc_length, block_ids, qk_kernel, value_kernel, up_kernel):
     rows_here, channels = byte_states.shape
     lat_dev = rows_here // STRIDE
@@ -181,6 +237,20 @@
     first_rows = (own_first + from_before).astype(jnp.bfloat16)
     at_first = lax.broadcasted_iota(jnp.int32, main_kv.shape, 2) == 0
     main_kv = jnp.where(at_first, first_rows[:, :, None, :], main_kv)
+    lat_len = doc_length[0] // STRIDE
+    if copies_n == 1 and lat_total <= 1024 and nq <= 8 and query_rows % 16 == 0:
+        denom = math.sqrt(float(CHANNEL_WIDTH)) * math.sqrt(math.log(float(lat_total)))
+        outgoing = attend_whole(lat_len.reshape(1), main_kv, block_ids, nq, denom)
+    else:
+        outgoing = attend_scan(
+            main_kv, block_ids, lat_len, n_ctx, nq, copies_n, query_rows, lat_dev, lat_total, stripe
+        )
+    returned = lax.all_to_all(outgoing, "ctx", split_axis=0, concat_axis=0, tiled=True)
+    limit = (doc_length[0] - device * rows_here).reshape(1).astype(jnp.int32)
+    return up_and_mix(limit, returned, byte_states, up_kernel, copies_n, per_t, nq, query_rows)
+
+
+def attend_scan(main_kv, block_ids, lat_len, n_ctx, nq, copies_n, query_rows, lat_dev, lat_total, stripe):
     key_all = main_kv[:, :nq]
     value_all = main_kv[:, nq:]
     queries = key_all.reshape(n_ctx, nq, copies_n, query_rows, CHANNEL_WIDTH)[:, :, 0]
@@ -200,7 +270,6 @@
     query_seg = lax.dynamic_index_in_dim(
         block_ids.reshape(n_ctx, copies_n, query_rows), stripe, 1, keepdims=False
     ).reshape(query_count)
-    lat_len = doc_length[0] // STRIDE
     sharpness_divisor = jnp.log(asking_index.astype(jnp.float32) + 2.0) / (
         math.sqrt(float(CHANNEL_WIDTH)) * math.sqrt(math.log(float(lat_total)))
     )
@@ -238,9 +307,9 @@
         return (updated, None)
 
     initial = (
-        jnp.full((head_here, query_count), -1e30, jnp.float32),
-        jnp.zeros((head_here, query_count), jnp.float32),
-        jnp.zeros((head_here, query_count, CHANNEL_WIDTH), jnp.float32),
+        jnp.full((nq, query_count), -1e30, jnp.float32),
+        jnp.zeros((nq, query_count), jnp.float32),
+        jnp.zeros((nq, query_count, CHANNEL_WIDTH), jnp.float32),
     )
     finals, unused = lax.scan(attend, initial, jnp.arange(block_count, dtype=jnp.int32) * block_len)
     attended = (finals[2] / finals[1][:, :, None]).astype(jnp.bfloat16)
@@ -259,9 +328,8 @@
         ],
         1,
     )
-    returned = lax.all_to_all(outgoing, "ctx", split_axis=0, concat_axis=0, tiled=True)
-    limit = (doc_length[0] - device * rows_here).reshape(1).astype(jnp.int32)
-    return up_and_mix(limit, returned, byte_states, up_kernel, copies_n, per_t, nq, query_rows)
+    return outgoing
+
 
 def solution(mesh):
     return jax.shard_map(

time: 46.1 us -> 47.1 us (1.022)
  Pallas kernels: 5.88 us -> 9.2 us
  matrix products: 1.53 us -> 0 us
  local copies, waits for them, and re-layouts: 1.04 us -> 2.29 us
  other arithmetic: 1.96 us -> 0.93 us
  waiting for transfers between devices: 23.6 us -> 22.7 us
    pallas_call x0 -> x1, Pallas kernels: none -> 3.32 us  [attend_whole(): pl.pallas_call(functools.partial(attend_kernel, lat, lat, nq, denom), out...]
    dot_general x2 -> x0, matrix products: 1.53 us -> none  [the longest x1 0.98 us: attend(): jnp.einsum('hqk,hkd->hqd', weights.astype(jnp.bfloat16), value_block, pre...]
    all_to_all x1, waiting for transfers between devices: 13.9 us -> 13 us  [body(): lax.all_to_all(both_local, 'ctx', split_axis=0, concat_axis=0, tiled=True)]
    reshape x1, local copies, waits for them, and re-layouts: 0.02 us -> 0.86 us  [attend_whole(): block_ids.reshape(total, 1)]
    concatenate x1 -> x0, other arithmetic: 0.84 us -> none  [body(): jnp.concatenate([attended.reshape(n_ctx, main_rows, CHANNEL_WIDTH), rim_o...]
    select_n x1, other arithmetic: 0.11 us -> 0.9 us  [body(): main_kv = jnp.where(at_first, first_rows[:, :, None, :], main_kv)]
    unnamed x4 -> x5, local copies, waits for them, and re-layouts: 0.71 us -> 1.38 us
    reduce_sum x1 -> x0, other arithmetic: 0.52 us -> none  [attend(): new_sum = run_sum * factor + jnp.sum(weights, axis=2)]
  transfers between devices with their start and end apart: 2 -> 2, of which waited for: 2 -> 2; matrix products, arithmetic and copies ran while one was open for 1% -> 2% of each run, Pallas kernels for 0% -> 0%
where the time goes in v5:
time: 47.1 us; the launch traced here: 46.7 us
  waiting for transfers between devices  22.7 us (48%)
  starting transfers between devices  10.9 us (23%)
  Pallas kernels  9.2 us (20%)
  local copies, waits for them, and re-layouts  2.29 us (5%)
  other arithmetic  0.93 us (2%)
  between operations  0.72 us (2%)
    all_to_all x1, waiting for transfers between devices, body(): lax.all_to_all(both_local, 'ctx', split_axis=0, concat_axis=0, tiled=True)  13 us
    all_to_all x1, waiting for transfers between devices, body(): lax.all_to_all(outgoing, 'ctx', split_axis=0, concat_axis=0, tiled=True)  9.75 us
    all_to_all x1, starting transfers between devices, body(): lax.all_to_all(both_local, 'ctx', split_axis=0, concat_axis=0, tiled=True)  7.25 us
    all_to_all x1, starting transfers between devices, body(): lax.all_to_all(outgoing, 'ctx', split_axis=0, concat_axis=0, tiled=True)  3.64 us
    pallas_call x1, Pallas kernels, attend_whole(): pl.pallas_call(functools.partial(attend_kernel, lat, lat, nq, denom), out...  3.32 us
    pallas_call x1, Pallas kernels, shorten_both(): pl.pallas_call(functools.partial(shorten_kernel, per_t, nq), out_shape=ja...  3.18 us
    pallas_call x1, Pallas kernels, up_and_mix(): pl.pallas_call(functools.partial(up_kernel_fn, copies_n, per_t, nq, qr),...  2.7 us
    unnamed x5, local copies, waits for them, and re-layouts  1.38 us
  transfers between devices with their start and end apart: 2, of which 2 were waited for; matrix products, arithmetic and copies ran while one was open for 2% of the time, Pallas kernels for 0%

profile of v5, /device:TPU:0, one launch (start us, length us, event | category | flops | bytes accessed | tf_op | source)
XLA Modules:
  0.0 46.7 jit_solution(6484579089506362030)
XLA Ops:
  0.0 3.2 %shard_map.64 = bf16[8,272,128]{2,1,0:T(8,128)(2,1)} custom-call(f32[256,512]{1,0:T(8,128)} %x_ref.3, f32[8,4,512]{2,1,0:T(4,128)} %qk_ref.1, f32[8,4,512]{2,1,0:T(4,128)} %vk_ref.1), custom_call_target="tpu_custom_call" | custom-call | flops 205520896 | bytes 1179648 | tf_op jit(solution)/shard_map/pallas_call | solution.py:84
  3.2 7.3 %all-to-all-start = ((bf16[8,272,128]{2,1,0:T(8,128)(2,1)}), bf16[8,272,128]{2,1,0:T(8,128)(2,1)S(1)}, u32[]{:S(2)}, u32[]{:S(2)}) async-start(bf16[8,272,128]{2,1,0:T(8,128)(2,1)} %shard_map.64), calls=%async_computation | async-start | bytes 1114112 | tf_op jit(solution)/shard_map/all_to_all | solution.py:230
  11.1 0.0 copy-start.1
  11.1 0.7 %copy-done.1 = s32[512]{0:T(512)S(1)} copy-done((s32[512]{0:T(512)S(1)}, s32[512]{0:T(512)}, u32[]{:S(2)}) %copy-start.1) | copy-done | bytes 2072
  11.8 0.9 %copy.15.segq_ref = s32[512,1]{1,0:T(8,128)} copy(s32[512,1]{0,1:T(1,128)S(1)} %bitcast.42) | data formatting | bytes 4096 | tf_op jit(solution)/shard_map/reshape | solution.py:205
  12.7 13.0 %all-to-all-done = bf16[8,272,128]{2,1,0:T(8,128)(2,1)S(1)} async-done(((bf16[8,272,128]{2,1,0:T(8,128)(2,1)}), bf16[8,272,128]{2,1,0:T(8,128)(2,1)S(1)}, u32[]{:S(2)}, u32[]{:S(2)}) %all-to-all-start) | async-done | bytes 557088 | tf_op jit(solution)/shard_map/all_to_all | solution.py:230
  25.7 0.9 %broadcast_select_fusion.kv_ref = bf16[8,4,64,128]{3,2,1,0:T(8,128)(2,1)} fusion(bf16[8,4,64,128]{3,2,1,0:T(8,128)(2,1)S(1)} %bitcast.39, pred[64]{0:T(512)(128)(4,1)S(1)} %iota_compare_fusion, bf16[8,4,128]{2,1,0:T(4,128)(2,1)S(1)} %fusion.3), kind=kLoop, calls=%fused_computation | loop fusion | flops 262144 | bytes 1056832 | tf_op jit(solution)/shard_map/jit(_where)/select_n | solution.py:239
  26.6 3.3 %shard_map.65 = bf16[8,144,128]{2,1,0:T(8,128)(2,1)} custom-call(s32[1]{0:T(128)} %bitcast.2.lim_ref, bf16[8,4,64,128]{3,2,1,0:T(8,128)(2,1)} %broadcast_select_fusion.kv_ref, s32[512,1]{1,0:T(8,128)} %copy.15.segq_ref, s32[1,512]{1,0:T(1,128)} %bitcast.41), custom_call_target="tpu_custom_call" | custom-call | flops 268435456 | bytes 819200 | tf_op jit(solution)/shard_map/pallas_call | solution.py:195
  30.0 3.6 %all-to-all-start.1 = ((bf16[8,144,128]{2,1,0:T(8,128)(2,1)}), bf16[8,144,128]{2,1,0:T(8,128)(2,1)S(1)}, u32[]{:S(2)}, u32[]{:S(2)}) async-start(bf16[8,144,128]{2,1,0:T(8,128)(2,1)} %shard_map.65), calls=%async_computation.1 | async-start | bytes 589824 | tf_op jit(solution)/shard_map/all_to_all | solution.py:248
  33.6 9.8 %all-to-all-done.1.ret_ref = bf16[8,144,128]{2,1,0:T(8,128)(2,1)S(1)} async-done(((bf16[8,144,128]{2,1,0:T(8,128)(2,1)}), bf16[8,144,128]{2,1,0:T(8,128)(2,1)S(1)}, u32[]{:S(2)}, u32[]{:S(2)}) %all-to-all-start.1) | async-done | bytes 294944 | tf_op jit(solution)/shard_map/all_to_all | solution.py:248
  43.3 0.0 copy-start
  43.3 0.7 %copy-done = bf16[8,144,128]{2,1,0:T(8,128)(2,1)} copy-done((bf16[8,144,128]{2,1,0:T(8,128)(2,1)}, bf16[8,144,128]{2,1,0:T(8,128)(2,1)S(1)}, u32[]{:S(2)}) %copy-start) | copy-done | bytes 294936
  44.0 2.7 %shard_map.66 = f32[256,512]{1,0:T(8,128)} custom-call(s32[1]{0:T(128)} %bitcast.1.lim_ref, bf16[8,144,128]{2,1,0:T(8,128)(2,1)} %copy-done, f32[256,512]{1,0:T(8,128)} %x_ref.3, f32[8,4,512]{2,1,0:T(4,128)} %up_ref.1), custom_call_target="tpu_custom_call" | custom-call | flops 205520896 | bytes 1343488 | tf_op jit(solution)/shard_map/pallas_call | solution.py:139
  (7 shorter events, 0.1 us)
Async XLA Ops:
  3.2 22.4 %all-to-all-start = ((bf16[8,272,128]{2,1,0:T(8,128)(2,1)}), bf16[8,272,128]{2,1,0:T(8,128)(2,1)S(1)}, u32[]{:S(2)}, u32[]{:S(2)}) async-start(bf16[8,272,128]{2,1,0:T(8,128)(2,1)} %shard_map.64), calls=%async_computation | async-start | bytes 1114112 | tf_op jit(solution)/shard_map/all_to_all | solution.py:230
  11.1 0.7 %copy-start.1 = (s32[512]{0:T(512)S(1)}, s32[512]{0:T(512)}, u32[]{:S(2)}) copy-start(s32[512]{0:T(512)} %param.8) | copy-start | bytes 6148
  30.0 13.4 %all-to-all-start.1 = ((bf16[8,144,128]{2,1,0:T(8,128)(2,1)}), bf16[8,144,128]{2,1,0:T(8,128)(2,1)S(1)}, u32[]{:S(2)}, u32[]{:S(2)}) async-start(bf16[8,144,128]{2,1,0:T(8,128)(2,1)} %shard_map.65), calls=%async_computation.1 | async-start | bytes 589824 | tf_op jit(solution)/shard_map/all_to_all | solution.py:248
  43.3 0.7 %copy-start = (bf16[8,144,128]{2,1,0:T(8,128)(2,1)}, bf16[8,144,128]{2,1,0:T(8,128)(2,1)S(1)}, u32[]{:S(2)}) copy-start(bf16[8,144,128]{2,1,0:T(8,128)(2,1)S(1)} %all-to-all-done.1.ret_ref) | copy-start | bytes 884740

commit v6 on v4

--- a/solution.py
+++ b/solution.py
@@ -100,6 +100,14 @@
     lanes = CHANNEL_WIDTH
     blocks = channels // lanes
     row = lax.broadcasted_iota(jnp.int32, (lat, channels), 0)
+    sources = ret_ref.shape[0]
+    me = lim_ref[1]
+
+    sign = lim_ref[2]
+
+    def where(source):
+        return (me - sign * source + sources) % sources
+
     prior_one = []
     prior_two = []
     for t in range(STRIDE):
@@ -108,9 +116,9 @@
         for block in range(blocks):
             g = t * per_t + block // nq
             q = block % nq
-            pieces = [ret_ref[g * copies_n + s, pl.ds(q * qr, qr), :] for s in range(copies_n)]
+            pieces = [ret_ref[where(g * copies_n + s), pl.ds(q * qr, qr), :] for s in range(copies_n)]
             att_parts.append(pieces[0] if copies_n == 1 else jnp.concatenate(pieces, 0))
-            rim_parts.append(ret_ref[g * copies_n + copies_n - 1, pl.ds(nq * qr + 2 * q, 2), :])
+            rim_parts.append(ret_ref[where(g * copies_n + copies_n - 1), pl.ds(nq * qr + 2 * q, 2), :])
         att = jnp.concatenate(att_parts, 1).astype(jnp.float32)
         rim = jnp.concatenate(rim_parts, 1).astype(jnp.float32)
         one = jnp.where(row == 0, rim[1:2], pltpu.roll(att, 1, 0))
@@ -259,9 +267,18 @@
         ],
         1,
     )
-    returned = lax.all_to_all(outgoing, "ctx", split_axis=0, concat_axis=0, tiled=True)
-    limit = (doc_length[0] - device * rows_here).reshape(1).astype(jnp.int32)
-    return up_and_mix(limit, returned, byte_states, up_kernel, copies_n, per_t, nq, query_rows)
+    if n_ctx <= 8:
+        pieces = [lax.dynamic_index_in_dim(outgoing, device, 0, keepdims=False)]
+        for s in range(1, n_ctx):
+            send = lax.dynamic_index_in_dim(outgoing, (device + s) % n_ctx, 0, keepdims=False)
+            pieces.append(lax.ppermute(send, "ctx", [(i, (i + s) % n_ctx) for i in range(n_ctx)]))
+        returned = jnp.stack(pieces, 0)
+        shifted_by, sign = 1, 1
+    else:
+        returned = lax.all_to_all(outgoing, "ctx", split_axis=0, concat_axis=0, tiled=True)
+        shifted_by, sign = 0, -1
+    info = jnp.stack([doc_length[0] - device * rows_here, device * shifted_by, jnp.int32(sign)]).astype(jnp.int32)
+    return up_and_mix(info, returned, byte_states, up_kernel, copies_n, per_t, nq, query_rows)
 
 def solution(mesh):
     return jax.shard_map(

time: 46.1 us -> 45.8 us (level)
  waiting for transfers between devices: 23.6 us -> 17 us
  starting transfers between devices: 10.9 us -> 17.2 us
    ppermute x0 -> x7, starting transfers between devices: none -> 9.94 us  [body(): lax.ppermute(send, 'ctx', [(i, (i + s) % n_ctx) for i in range(n_ctx)])]
    all_to_all x1 -> x0, waiting for transfers between devices: 9.75 us -> none  [body(): lax.all_to_all(outgoing, 'ctx', split_axis=0, concat_axis=0, tiled=True)]
    all_to_all x1 -> x0, starting transfers between devices: 3.63 us -> none  [body(): lax.all_to_all(outgoing, 'ctx', split_axis=0, concat_axis=0, tiled=True)]
    ppermute x0 -> x7, waiting for transfers between devices: none -> 3.17 us  [body(): lax.ppermute(send, 'ctx', [(i, (i + s) % n_ctx) for i in range(n_ctx)])]
    concatenate x1, other arithmetic: 0.84 us -> 0.13 us  [body(): jnp.concatenate([attended.reshape(n_ctx, main_rows, CHANNEL_WIDTH), rim_o...]
    another operation x0 -> x1, other arithmetic: none -> 0.61 us  [body(): jnp.stack([doc_length[0] - device * rows_here, device * shifted_by, jnp.i...]
  transfers between devices with their start and end apart: 2 -> 8, of which waited for: 2 -> 4; matrix products, arithmetic and copies ran while one was open for 1% -> 3% of each run, Pallas kernels for 0% -> 0%
where the time goes in v6:
time: 45.8 us; the launch traced here: 45.5 us
  starting transfers between devices  17.2 us (38%)
  waiting for transfers between devices  17 us (37%)
  Pallas kernels  5.9 us (13%)
  other arithmetic  1.85 us (4%)
  matrix products  1.52 us (3%)
  local copies, waits for them, and re-layouts  1.14 us (2%)
  between operations  0.95 us (2%)
    all_to_all x1, waiting for transfers between devices, body(): lax.all_to_all(both_local, 'ctx', split_axis=0, concat_axis=0, tiled=True)  13.8 us
    ppermute x7, starting transfers between devices, body(): lax.ppermute(send, 'ctx', [(i, (i + s) % n_ctx) for i in range(n_ctx)])  9.94 us
    all_to_all x1, starting transfers between devices, body(): lax.all_to_all(both_local, 'ctx', split_axis=0, concat_axis=0, tiled=True)  7.25 us
    pallas_call x1, Pallas kernels, shorten_both(): pl.pallas_call(functools.partial(shorten_kernel, per_t, nq), out_shape=ja...  3.18 us
    ppermute x7, waiting for transfers between devices, body(): lax.ppermute(send, 'ctx', [(i, (i + s) % n_ctx) for i in range(n_ctx)])  3.17 us
    pallas_call x1, Pallas kernels, up_and_mix(): pl.pallas_call(functools.partial(up_kernel_fn, copies_n, per_t, nq, qr),...  2.72 us
    dot_general x1, matrix products, attend(): jnp.einsum('hqk,hkd->hqd', weights.astype(jnp.bfloat16), value_block, pre...  0.98 us
  transfers between devices with their start and end apart: 8, of which 4 were waited for; matrix products, arithmetic and copies ran while one was open for 3% of the time, Pallas kernels for 0%

profile of v6, /device:TPU:0, one launch (start us, length us, event | category | flops | bytes accessed | tf_op | source)
XLA Modules:
  0.0 45.5 jit_solution(14807718640147002504)
XLA Ops:
  0.0 0.0 copy-start.1
  0.0 3.2 %shard_map.64 = bf16[8,272,128]{2,1,0:T(8,128)(2,1)} custom-call(f32[256,512]{1,0:T(8,128)} %x_ref.3, f32[8,4,512]{2,1,0:T(4,128)} %qk_ref.1, f32[8,4,512]{2,1,0:T(4,128)} %vk_ref.1), custom_call_target="tpu_custom_call" | custom-call | flops 205520896 | bytes 1179648 | tf_op jit(solution)/shard_map/pallas_call | solution.py:84
  3.2 7.3 %all-to-all-start = ((bf16[8,272,128]{2,1,0:T(8,128)(2,1)}), bf16[8,272,128]{2,1,0:T(8,128)(2,1)S(1)}, u32[]{:S(2)}, u32[]{:S(2)}) async-start(bf16[8,272,128]{2,1,0:T(8,128)(2,1)} %shard_map.64), calls=%async_computation | async-start | bytes 1114112 | tf_op jit(solution)/shard_map/all_to_all | solution.py:182
  11.2 0.1 iota_add_fusion
  11.3 0.1 add.156
  11.4 0.1 pad.4.clone
  11.5 0.0 copy-done.1
  11.5 0.4 fusion.9
  11.8 13.8 %all-to-all-done = bf16[8,272,128]{2,1,0:T(8,128)(2,1)S(1)} async-done(((bf16[8,272,128]{2,1,0:T(8,128)(2,1)}), bf16[8,272,128]{2,1,0:T(8,128)(2,1)S(1)}, u32[]{:S(2)}, u32[]{:S(2)}) %all-to-all-start) | async-done | bytes 557088 | tf_op jit(solution)/shard_map/all_to_all | solution.py:182
  25.7 0.1 broadcast_select_fusion
  25.9 0.5 %select_reduce_fusion = (f32[2,512]{1,0:T(2,128)S(1)}, f32[2,512,512]{1,2,0:T(8,128)S(1)}) fusion(f32[512]{0:T(512)S(1)} %log_multiply_fusion, pred[512,512]{0,1:T(8,128)(4,1)S(1)} %fusion.9, bf16[2,512,128]{2,1,0:T(8,128)(2,1)S(1)} %bitcast.76), kind=kOutput, calls=%fused_computation.1 | convolution fusion | flops 135789568 | bytes 2627584 | tf_op jit(solution)/shard_map/while/body/eval_jaxpr/hqd,hkd->hqk/dot_general | solution.py:225
  26.5 0.5 %fusion = f32[2,512]{1,0:T(2,128)S(1)} fusion(f32[2,512,512]{1,2,0:T(8,128)S(1)} %get-tuple-element.83, f32[2,512]{1,0:T(2,128)S(1)} %broadcast_maximum_fusion, f32[512]{0:T(512)S(1)} %log_multiply_fusion, pred[512,512]{0,1:T(8,128)(4,1)S(1)} %fusion.9), kind=kLoop, calls=%fused_computation.2 | loop fusion | flops 2096128 | bytes 2369536 | tf_op jit(solution)/shard_map/while/body/eval_jaxpr/reduce_sum | solution.py:238
  27.0 1.0 %fusion.3 = bf16[2,512,128]{2,1,0:T(8,128)(2,1)S(1)} fusion(bf16[2,512,128]{2,1,0:T(8,128)(2,1)S(1)} %bitcast.82, f32[2,512,512]{1,2,0:T(8,128)S(1)} %get-tuple-element.83, f32[2,512]{1,0:T(2,128)S(1)} %broadcast_maximum_fusion, f32[512]{0:T(512)S(1)} %log_multiply_fusion, pred[512,512]{0,1:T(8,128)(4,1)S(1)} %fusion.9, f32[2,512]{1,0:T(2,128)S(1)} %get-tuple-element.81, ...), kind=kOutput, calls=%fused_computation.6 | convolution fusion | flops 136708096 | bytes 2897920 | tf_op jit(solution)/shard_map/while/body/eval_jaxpr/hqk,hkd->hqd/dot_general | solution.py:239
  28.1 0.1 maximum_maximum_fusion
  28.3 1.5 %collective-permute-start = (bf16[144,128]{1,0:T(8,128)(2,1)S(1)}, bf16[144,128]{1,0:T(8,128)(2,1)S(1)}, u32[]{:S(2)}, u32[]{:S(2)}) collective-permute-start(bf16[144,128]{1,0:T(8,128)(2,1)S(1)} %get-tuple-element.74), channel_id=1, source_target_pairs={{0,2},{2,4},{4,6},{6,8},{8,10},{10,12},{12,14},{14,0},{1,3},{3,5},... | collective-permute-start | bytes 110600 | tf_op jit(solution)/shard_map/ppermute | solution.py:274
  29.8 0.6 %pad_add_fusion.lim_ref = s32[3]{0:T(128)} fusion(s32[1]{0:T(128)} %constant.127.clone.1, s32[1]{0:T(128)} %bitcast.2, s32[1]{0:T(128)} %bitcast.1), kind=kLoop, calls=%fused_computation.47 | loop fusion | flops 6 | bytes 24 | tf_op jit(solution)/shard_map/stack | solution.py:280
  30.4 0.0 collective-permute-start.1
  30.4 1.7 %collective-permute-start.2 = (bf16[144,128]{1,0:T(8,128)(2,1)S(1)}, bf16[144,128]{1,0:T(8,128)(2,1)S(1)}, u32[]{:S(2)}, u32[]{:S(2)}) collective-permute-start(bf16[144,128]{1,0:T(8,128)(2,1)S(1)} %get-tuple-element.72), channel_id=1, source_target_pairs={{0,6},{2,8},{4,10},{6,12},{8,14},{10,0},{12,2},{14,4},{1,7},{3,9},... | collective-permute-start | bytes 110600 | tf_op jit(solution)/shard_map/ppermute | solution.py:274
  32.2 2.8 %collective-permute-start.3 = (bf16[144,128]{1,0:T(8,128)(2,1)S(1)}, bf16[144,128]{1,0:T(8,128)(2,1)S(1)}, u32[]{:S(2)}, u32[]{:S(2)}) collective-permute-start(bf16[144,128]{1,0:T(8,128)(2,1)S(1)} %get-tuple-element.71), channel_id=1, source_target_pairs={{0,8},{2,10},{4,12},{6,14},{8,0},{10,2},{12,4},{14,6},{1,9},{3,11}... | collective-permute-start | bytes 110600 | tf_op jit(solution)/shard_map/ppermute | solution.py:274
  34.9 1.3 %collective-permute-start.4 = (bf16[144,128]{1,0:T(8,128)(2,1)S(1)}, bf16[144,128]{1,0:T(8,128)(2,1)S(1)}, u32[]{:S(2)}, u32[]{:S(2)}) collective-permute-start(bf16[144,128]{1,0:T(8,128)(2,1)S(1)} %get-tuple-element.70), channel_id=1, source_target_pairs={{0,10},{2,12},{4,14},{6,0},{8,2},{10,4},{12,6},{14,8},{1,11},{3,13... | collective-permute-start | bytes 110600 | tf_op jit(solution)/shard_map/ppermute | solution.py:274
  36.3 0.0 collective-permute-done
  36.3 1.8 %collective-permute-start.5 = (bf16[144,128]{1,0:T(8,128)(2,1)S(1)}, bf16[144,128]{1,0:T(8,128)(2,1)S(1)}, u32[]{:S(2)}, u32[]{:S(2)}) collective-permute-start(bf16[144,128]{1,0:T(8,128)(2,1)S(1)} %get-tuple-element.69), channel_id=1, source_target_pairs={{0,12},{2,14},{4,0},{6,2},{8,4},{10,6},{12,8},{14,10},{1,13},{3,15... | collective-permute-start | bytes 110600 | tf_op jit(solution)/shard_map/ppermute | solution.py:274
  38.1 0.0 collective-permute-done.1
  38.1 0.8 %collective-permute-start.6 = (bf16[144,128]{1,0:T(8,128)(2,1)S(1)}, bf16[144,128]{1,0:T(8,128)(2,1)S(1)}, u32[]{:S(2)}, u32[]{:S(2)}) collective-permute-start(bf16[144,128]{1,0:T(8,128)(2,1)S(1)} %get-tuple-element.68), channel_id=1, source_target_pairs={{0,14},{2,0},{4,2},{6,4},{8,6},{10,8},{12,10},{14,12},{1,15},{3,1}... | collective-permute-start | bytes 110600 | tf_op jit(solution)/shard_map/ppermute | solution.py:274
  38.9 0.0 collective-permute-done.2
  38.9 0.0 collective-permute-done.3
  38.9 0.9 %collective-permute-done.4 = bf16[144,128]{1,0:T(8,128)(2,1)S(1)} collective-permute-done((bf16[144,128]{1,0:T(8,128)(2,1)S(1)}, bf16[144,128]{1,0:T(8,128)(2,1)S(1)}, u32[]{:S(2)}, u32[]{:S(2)}) %collective-permute-start.4) | collective-permute-done | bytes 36896 | tf_op jit(solution)/shard_map/ppermute | solution.py:274
  39.8 0.8 %collective-permute-done.5 = bf16[144,128]{1,0:T(8,128)(2,1)S(1)} collective-permute-done((bf16[144,128]{1,0:T(8,128)(2,1)S(1)}, bf16[144,128]{1,0:T(8,128)(2,1)S(1)}, u32[]{:S(2)}, u32[]{:S(2)}) %collective-permute-start.5) | collective-permute-done | bytes 36896 | tf_op jit(solution)/shard_map/ppermute | solution.py:274
  40.6 1.5 %collective-permute-done.6 = bf16[144,128]{1,0:T(8,128)(2,1)S(1)} collective-permute-done((bf16[144,128]{1,0:T(8,128)(2,1)S(1)}, bf16[144,128]{1,0:T(8,128)(2,1)S(1)}, u32[]{:S(2)}, u32[]{:S(2)}) %collective-permute-start.6) | collective-permute-done | bytes 36896 | tf_op jit(solution)/shard_map/ppermute | solution.py:274
  42.1 0.0 copy-start
  42.1 0.7 %copy-done = bf16[8,144,128]{2,1,0:T(8,128)(2,1)} copy-done((bf16[8,144,128]{2,1,0:T(8,128)(2,1)}, bf16[8,144,128]{2,1,0:T(8,128)(2,1)S(1)}, u32[]{:S(2)}) %copy-start) | copy-done | bytes 294936
  42.8 2.7 %shard_map.65 = f32[256,512]{1,0:T(8,128)} custom-call(s32[3]{0:T(128)} %pad_add_fusion.lim_ref, bf16[8,144,128]{2,1,0:T(8,128)(2,1)} %copy-done, f32[256,512]{1,0:T(8,128)} %x_ref.3, f32[8,4,512]{2,1,0:T(4,128)} %up_ref.1), custom_call_target="tpu_custom_call" | custom-call | flops 205520896 | bytes 1343488 | tf_op jit(solution)/shard_map/pallas_call | solution.py:147
  (27 shorter events, 0.3 us)
Async XLA Ops:
  0.0 11.5 %copy-start.1 = (s32[512]{0:T(512)S(1)}, s32[512]{0:T(512)}, u32[]{:S(2)}) copy-start(s32[512]{0:T(512)} %param.8) | copy-start | bytes 6148
  3.2 22.4 %all-to-all-start = ((bf16[8,272,128]{2,1,0:T(8,128)(2,1)}), bf16[8,272,128]{2,1,0:T(8,128)(2,1)S(1)}, u32[]{:S(2)}, u32[]{:S(2)}) async-start(bf16[8,272,128]{2,1,0:T(8,128)(2,1)} %shard_map.64), calls=%async_computation | async-start | bytes 1114112 | tf_op jit(solution)/shard_map/all_to_all | solution.py:182
  28.3 8.0 %collective-permute-start = (bf16[144,128]{1,0:T(8,128)(2,1)S(1)}, bf16[144,128]{1,0:T(8,128)(2,1)S(1)}, u32[]{:S(2)}, u32[]{:S(2)}) collective-permute-start(bf16[144,128]{1,0:T(8,128)(2,1)S(1)} %get-tuple-element.74), channel_id=1, source_target_pairs={{0,2},{2,4},{4,6},{6,8},{8,10},{10,12},{12,14},{14,0},{1,3},{3,5},... | collective-permute-start | bytes 110600 | tf_op jit(solution)/shard_map/ppermute | solution.py:274
  30.4 7.7 %collective-permute-start.1 = (bf16[144,128]{1,0:T(8,128)(2,1)S(1)}, bf16[144,128]{1,0:T(8,128)(2,1)S(1)}, u32[]{:S(2)}, u32[]{:S(2)}) collective-permute-start(bf16[144,128]{1,0:T(8,128)(2,1)S(1)} %get-tuple-element.73), channel_id=1, source_target_pairs={{0,4},{2,6},{4,8},{6,10},{8,12},{10,14},{12,0},{14,2},{1,5},{3,7},... | collective-permute-start | bytes 110600 | tf_op jit(solution)/shard_map/ppermute | solution.py:274
  30.4 8.4 %collective-permute-start.2 = (bf16[144,128]{1,0:T(8,128)(2,1)S(1)}, bf16[144,128]{1,0:T(8,128)(2,1)S(1)}, u32[]{:S(2)}, u32[]{:S(2)}) collective-permute-start(bf16[144,128]{1,0:T(8,128)(2,1)S(1)} %get-tuple-element.72), channel_id=1, source_target_pairs={{0,6},{2,8},{4,10},{6,12},{8,14},{10,0},{12,2},{14,4},{1,7},{3,9},... | collective-permute-start | bytes 110600 | tf_op jit(solution)/shard_map/ppermute | solution.py:274
  32.2 6.7 %collective-permute-start.3 = (bf16[144,128]{1,0:T(8,128)(2,1)S(1)}, bf16[144,128]{1,0:T(8,128)(2,1)S(1)}, u32[]{:S(2)}, u32[]{:S(2)}) collective-permute-start(bf16[144,128]{1,0:T(8,128)(2,1)S(1)} %get-tuple-element.71), channel_id=1, source_target_pairs={{0,8},{2,10},{4,12},{6,14},{8,0},{10,2},{12,4},{14,6},{1,9},{3,11}... | collective-permute-start | bytes 110600 | tf_op jit(solution)/shard_map/ppermute | solution.py:274
  34.9 4.9 %collective-permute-start.4 = (bf16[144,128]{1,0:T(8,128)(2,1)S(1)}, bf16[144,128]{1,0:T(8,128)(2,1)S(1)}, u32[]{:S(2)}, u32[]{:S(2)}) collective-permute-start(bf16[144,128]{1,0:T(8,128)(2,1)S(1)} %get-tuple-element.70), channel_id=1, source_target_pairs={{0,10},{2,12},{4,14},{6,0},{8,2},{10,4},{12,6},{14,8},{1,11},{3,13... | collective-permute-start | bytes 110600 | tf_op jit(solution)/shard_map/ppermute | solution.py:274
  36.3 4.3 %collective-permute-start.5 = (bf16[144,128]{1,0:T(8,128)(2,1)S(1)}, bf16[144,128]{1,0:T(8,128)(2,1)S(1)}, u32[]{:S(2)}, u32[]{:S(2)}) collective-permute-start(bf16[144,128]{1,0:T(8,128)(2,1)S(1)} %get-tuple-element.69), channel_id=1, source_target_pairs={{0,12},{2,14},{4,0},{6,2},{8,4},{10,6},{12,8},{14,10},{1,13},{3,15... | collective-permute-start | bytes 110600 | tf_op jit(solution)/shard_map/ppermute | solution.py:274
  38.1 4.0 %collective-permute-start.6 = (bf16[144,128]{1,0:T(8,128)(2,1)S(1)}, bf16[144,128]{1,0:T(8,128)(2,1)S(1)}, u32[]{:S(2)}, u32[]{:S(2)}) collective-permute-start(bf16[144,128]{1,0:T(8,128)(2,1)S(1)} %get-tuple-element.68), channel_id=1, source_target_pairs={{0,14},{2,0},{4,2},{6,4},{8,6},{10,8},{12,10},{14,12},{1,15},{3,1}... | collective-permute-start | bytes 110600 | tf_op jit(solution)/shard_map/ppermute | solution.py:274
  42.1 0.7 %copy-start = (bf16[8,144,128]{2,1,0:T(8,128)(2,1)}, bf16[8,144,128]{2,1,0:T(8,128)(2,1)S(1)}, u32[]{:S(2)}) copy-start(bf16[8,144,128]{2,1,0:T(8,128)(2,1)S(1)} %bitcast_dynamic-update-slice_fusion.ret_ref) | copy-start | bytes 884740

commit v7 on v4

--- a/solution.py
+++ b/solution.py
@@ -99,9 +99,16 @@
     lat = rows // STRIDE
     lanes = CHANNEL_WIDTH
     blocks = channels // lanes
-    row = lax.broadcasted_iota(jnp.int32, (lat, channels), 0)
-    prior_one = []
-    prior_two = []
+    wide = lat + 16
+    pick_row = lax.broadcasted_iota(jnp.int32, (rows, wide), 0)
+    pick_col = lax.broadcasted_iota(jnp.int32, (rows, wide), 1)
+    latent = pick_row // STRIDE
+    col_one = jnp.where(latent >= 1, latent - 1, lat + 1)
+    col_two = jnp.where(latent >= 2, latent - 2, lat + latent)
+    take_one = jnp.where(pick_col == col_one, 1.0, 0.0).astype(jnp.bfloat16)
+    take_two = jnp.where(pick_col == col_two, 1.0, 0.0).astype(jnp.bfloat16)
+    phase_row = lax.broadcasted_iota(jnp.int32, (8, channels), 0) % STRIDE
+    branch = None
     for t in range(STRIDE):
         att_parts = []
         rim_parts = []
@@ -113,22 +120,17 @@
             rim_parts.append(ret_ref[g * copies_n + copies_n - 1, pl.ds(nq * qr + 2 * q, 2), :])
         att = jnp.concatenate(att_parts, 1).astype(jnp.float32)
         rim = jnp.concatenate(rim_parts, 1).astype(jnp.float32)
-        one = jnp.where(row == 0, rim[1:2], pltpu.roll(att, 1, 0))
-        two = jnp.where(row == 0, rim[0:1], jnp.where(row == 1, rim[1:2], pltpu.roll(att, 2, 0)))
-        prior_one.append(one)
-        prior_two.append(two)
-    by_phase = []
-    for s in range(STRIDE):
-        total = prior_one[0] * up_ref[s, pl.ds(0, 1), :] + prior_two[0] * up_ref[s + STRIDE, pl.ds(0, 1), :]
-        for t in range(1, STRIDE):
-            total = total + prior_one[t] * up_ref[s, pl.ds(t, 1), :]
-            total = total + prior_two[t] * up_ref[s + STRIDE, pl.ds(t, 1), :]
-        by_phase.append(total)
-    by_phase = jnp.concatenate(by_phase, 0)
-    put_row = lax.broadcasted_iota(jnp.int32, (rows, rows), 0)
-    put_col = lax.broadcasted_iota(jnp.int32, (rows, rows), 1)
-    put = (put_col == (put_row % STRIDE) * lat + put_row // STRIDE).astype(jnp.bfloat16)
-    branch = exact_rows(put, by_phase)
+        extended = jnp.concatenate([att, rim, jnp.zeros((14, channels), jnp.float32)], 0).astype(jnp.bfloat16)
+        one = jnp.dot(take_one, extended, preferred_element_type=jnp.float32)
+        two = jnp.dot(take_two, extended, preferred_element_type=jnp.float32)
+        w_one = up_ref[0, pl.ds(t, 1), :]
+        w_two = up_ref[STRIDE, pl.ds(t, 1), :]
+        for s in range(1, STRIDE):
+            w_one = jnp.where(phase_row == s, up_ref[s, pl.ds(t, 1), :], w_one)
+            w_two = jnp.where(phase_row == s, up_ref[s + STRIDE, pl.ds(t, 1), :], w_two)
+        term = one.reshape(rows // 8, 8, channels) * w_one[None] + two.reshape(rows // 8, 8, channels) * w_two[None]
+        branch = term if branch is None else branch + term
+    branch = branch.reshape(rows, channels)
     byte_row = lax.broadcasted_iota(jnp.int32, (rows, channels), 0)
     out_ref[...] = x_ref[...] + jnp.where(byte_row < lim_ref[0], branch, 0.0)
 

time: 46.1 us -> 46 us (level)
  no operation moved by 1% of the time
where the time goes in v7:
time: 46 us; the launch traced here: 45.7 us
  waiting for transfers between devices  23.6 us (51%)
  starting transfers between devices  10.9 us (24%)
  Pallas kernels  5.83 us (13%)
  other arithmetic  1.96 us (4%)
  matrix products  1.53 us (3%)
  local copies, waits for them, and re-layouts  1.04 us (2%)
  between operations  0.81 us (2%)
    all_to_all x1, waiting for transfers between devices, body(): lax.all_to_all(both_local, 'ctx', split_axis=0, concat_axis=0, tiled=True)  13.9 us
    all_to_all x1, waiting for transfers between devices, body(): lax.all_to_all(outgoing, 'ctx', split_axis=0, concat_axis=0, tiled=True)  9.75 us
    all_to_all x1, starting transfers between devices, body(): lax.all_to_all(both_local, 'ctx', split_axis=0, concat_axis=0, tiled=True)  7.25 us
    all_to_all x1, starting transfers between devices, body(): lax.all_to_all(outgoing, 'ctx', split_axis=0, concat_axis=0, tiled=True)  3.63 us
    pallas_call x1, Pallas kernels, shorten_both(): pl.pallas_call(functools.partial(shorten_kernel, per_t, nq), out_shape=ja...  3.18 us
    pallas_call x1, Pallas kernels, up_and_mix(): pl.pallas_call(functools.partial(up_kernel_fn, copies_n, per_t, nq, qr),...  2.65 us
    dot_general x1, matrix products, attend(): jnp.einsum('hqk,hkd->hqd', weights.astype(jnp.bfloat16), value_block, pre...  0.98 us
  transfers between devices with their start and end apart: 2, of which 2 were waited for; matrix products, arithmetic and copies ran while one was open for 1% of the time, Pallas kernels for 0%

profile of v7, /device:TPU:0, one launch (start us, length us, event | category | flops | bytes accessed | tf_op | source)
XLA Modules:
  0.0 45.7 jit_solution(6068438673109082743)
XLA Ops:
  0.0 0.0 copy-start.1
  0.0 3.2 %shard_map.64 = bf16[8,272,128]{2,1,0:T(8,128)(2,1)} custom-call(f32[256,512]{1,0:T(8,128)} %x_ref.3, f32[8,4,512]{2,1,0:T(4,128)} %qk_ref.1, f32[8,4,512]{2,1,0:T(4,128)} %vk_ref.1), custom_call_target="tpu_custom_call" | custom-call | flops 205520896 | bytes 1179648 | tf_op jit(solution)/shard_map/pallas_call | solution.py:84
  3.2 7.3 %all-to-all-start = ((bf16[8,272,128]{2,1,0:T(8,128)(2,1)}), bf16[8,272,128]{2,1,0:T(8,128)(2,1)S(1)}, u32[]{:S(2)}, u32[]{:S(2)}) async-start(bf16[8,272,128]{2,1,0:T(8,128)(2,1)} %shard_map.64), calls=%async_computation | async-start | bytes 1114112 | tf_op jit(solution)/shard_map/all_to_all | solution.py:176
  11.1 0.1 iota_add_fusion
  11.2 0.1 add.89
  11.3 0.1 pad.4.clone
  11.4 0.0 copy-done.1
  11.4 0.4 fusion.9
  11.7 13.9 %all-to-all-done = bf16[8,272,128]{2,1,0:T(8,128)(2,1)S(1)} async-done(((bf16[8,272,128]{2,1,0:T(8,128)(2,1)}), bf16[8,272,128]{2,1,0:T(8,128)(2,1)S(1)}, u32[]{:S(2)}, u32[]{:S(2)}) %all-to-all-start) | async-done | bytes 557088 | tf_op jit(solution)/shard_map/all_to_all | solution.py:176
  25.7 0.1 broadcast_select_fusion
  25.9 0.5 %select_reduce_fusion = (f32[2,512]{1,0:T(2,128)S(1)}, f32[2,512,512]{1,2,0:T(8,128)S(1)}) fusion(f32[512]{0:T(512)S(1)} %log_multiply_fusion, pred[512,512]{0,1:T(8,128)(4,1)S(1)} %fusion.9, bf16[2,512,128]{2,1,0:T(8,128)(2,1)S(1)} %bitcast.47), kind=kOutput, calls=%fused_computation.1 | convolution fusion | flops 135789568 | bytes 2627584 | tf_op jit(solution)/shard_map/while/body/eval_jaxpr/hqd,hkd->hqk/dot_general | solution.py:219
  26.5 0.5 %fusion = f32[2,512]{1,0:T(2,128)S(1)} fusion(f32[2,512,512]{1,2,0:T(8,128)S(1)} %get-tuple-element.75, f32[2,512]{1,0:T(2,128)S(1)} %broadcast_maximum_fusion, f32[512]{0:T(512)S(1)} %log_multiply_fusion, pred[512,512]{0,1:T(8,128)(4,1)S(1)} %fusion.9), kind=kLoop, calls=%fused_computation.2 | loop fusion | flops 2096128 | bytes 2369536 | tf_op jit(solution)/shard_map/while/body/eval_jaxpr/reduce_sum | solution.py:232
  27.0 1.0 %fusion.3 = bf16[2,512,128]{2,1,0:T(8,128)(2,1)S(1)} fusion(bf16[2,512,128]{2,1,0:T(8,128)(2,1)S(1)} %bitcast.53, f32[2,512,512]{1,2,0:T(8,128)S(1)} %get-tuple-element.75, f32[2,512]{1,0:T(2,128)S(1)} %broadcast_maximum_fusion, f32[512]{0:T(512)S(1)} %log_multiply_fusion, pred[512,512]{0,1:T(8,128)(4,1)S(1)} %fusion.9, f32[2,512]{1,0:T(2,128)S(1)} %get-tuple-element.73, ...), kind=kOutput, calls=%fused_computation.6 | convolution fusion | flops 136708096 | bytes 2897920 | tf_op jit(solution)/shard_map/while/body/eval_jaxpr/hqk,hkd->hqd/dot_general | solution.py:233
  28.1 0.8 %maximum_maximum_fusion = bf16[8,144,128]{2,1,0:T(8,128)(2,1)} fusion(bf16[8,4,128]{2,1,0:T(4,128)(2,1)S(1)} %bitcast.55, bf16[8,128,128]{2,1,0:T(8,128)(2,1)S(1)} %bitcast.50, bf16[144]{0:T(256)(128)(2,1)S(1)} %pad.4.clone), kind=kLoop, calls=%fused_computation.15 | loop fusion | flops 884736 | bytes 565536 | tf_op jit(solution)/shard_map/concatenate | solution.py:256
  28.9 3.6 %all-to-all-start.1 = ((bf16[8,144,128]{2,1,0:T(8,128)(2,1)}), bf16[8,144,128]{2,1,0:T(8,128)(2,1)S(1)}, u32[]{:S(2)}, u32[]{:S(2)}) async-start(bf16[8,144,128]{2,1,0:T(8,128)(2,1)} %maximum_maximum_fusion), calls=%async_computation.1 | async-start | bytes 589824 | tf_op jit(solution)/shard_map/all_to_all | solution.py:264
  32.6 9.8 %all-to-all-done.1.ret_ref = bf16[8,144,128]{2,1,0:T(8,128)(2,1)S(1)} async-done(((bf16[8,144,128]{2,1,0:T(8,128)(2,1)}), bf16[8,144,128]{2,1,0:T(8,128)(2,1)S(1)}, u32[]{:S(2)}, u32[]{:S(2)}) %all-to-all-start.1) | async-done | bytes 294944 | tf_op jit(solution)/shard_map/all_to_all | solution.py:264
  42.3 0.0 copy-start
  42.3 0.7 %copy-done = bf16[8,144,128]{2,1,0:T(8,128)(2,1)} copy-done((bf16[8,144,128]{2,1,0:T(8,128)(2,1)}, bf16[8,144,128]{2,1,0:T(8,128)(2,1)S(1)}, u32[]{:S(2)}) %copy-start) | copy-done | bytes 294936
  43.0 2.6 %shard_map.65 = f32[256,512]{1,0:T(8,128)} custom-call(s32[1]{0:T(128)} %bitcast.1.lim_ref, bf16[8,144,128]{2,1,0:T(8,128)(2,1)} %copy-done, f32[256,512]{1,0:T(8,128)} %x_ref.3, f32[8,4,512]{2,1,0:T(4,128)} %up_ref.1), custom_call_target="tpu_custom_call" | custom-call | flops 205520896 | bytes 1343488 | tf_op jit(solution)/shard_map/pallas_call | solution.py:141
  (19 shorter events, 0.2 us)
Async XLA Ops:
  0.0 11.4 %copy-start.1 = (s32[512]{0:T(512)S(1)}, s32[512]{0:T(512)}, u32[]{:S(2)}) copy-start(s32[512]{0:T(512)} %param.8) | copy-start | bytes 6148
  3.2 22.4 %all-to-all-start = ((bf16[8,272,128]{2,1,0:T(8,128)(2,1)}), bf16[8,272,128]{2,1,0:T(8,128)(2,1)S(1)}, u32[]{:S(2)}, u32[]{:S(2)}) async-start(bf16[8,272,128]{2,1,0:T(8,128)(2,1)} %shard_map.64), calls=%async_computation | async-start | bytes 1114112 | tf_op jit(solution)/shard_map/all_to_all | solution.py:176
  28.9 13.4 %all-to-all-start.1 = ((bf16[8,144,128]{2,1,0:T(8,128)(2,1)}), bf16[8,144,128]{2,1,0:T(8,128)(2,1)S(1)}, u32[]{:S(2)}, u32[]{:S(2)}) async-start(bf16[8,144,128]{2,1,0:T(8,128)(2,1)} %maximum_maximum_fusion), calls=%async_computation.1 | async-start | bytes 589824 | tf_op jit(solution)/shard_map/all_to_all | solution.py:264
  42.3 0.7 %copy-start = (bf16[8,144,128]{2,1,0:T(8,128)(2,1)}, bf16[8,144,128]{2,1,0:T(8,128)(2,1)S(1)}, u32[]{:S(2)}) copy-start(bf16[8,144,128]{2,1,0:T(8,128)(2,1)S(1)} %all-to-all-done.1.ret_ref) | copy-start | bytes 884740

commit v8 on v7

--- a/solution.py
+++ b/solution.py
@@ -94,13 +94,13 @@
     )(byte_states, qk_kernel, value_kernel)
 
 
-def up_kernel_fn(copies_n, per_t, nq, qr, lim_ref, ret_ref, x_ref, up_ref, out_ref):
+def up_kernel_fn(copies_n, per_t, nq, qr, lat, lim_ref, ret_ref, x_ref, up_ref, out_ref):
     rows, channels = x_ref.shape
-    lat = rows // STRIDE
     lanes = CHANNEL_WIDTH
     blocks = channels // lanes
+    first = pl.program_id(0) * rows
     wide = lat + 16
-    pick_row = lax.broadcasted_iota(jnp.int32, (rows, wide), 0)
+    pick_row = lax.broadcasted_iota(jnp.int32, (rows, wide), 0) + first
     pick_col = lax.broadcasted_iota(jnp.int32, (rows, wide), 1)
     latent = pick_row // STRIDE
     col_one = jnp.where(latent >= 1, latent - 1, lat + 1)
@@ -131,20 +131,28 @@
         term = one.reshape(rows // 8, 8, channels) * w_one[None] + two.reshape(rows // 8, 8, channels) * w_two[None]
         branch = term if branch is None else branch + term
     branch = branch.reshape(rows, channels)
-    byte_row = lax.broadcasted_iota(jnp.int32, (rows, channels), 0)
+    byte_row = lax.broadcasted_iota(jnp.int32, (rows, channels), 0) + first
     out_ref[...] = x_ref[...] + jnp.where(byte_row < lim_ref[0], branch, 0.0)
 
 
 def up_and_mix(limit, returned, byte_states, up_kernel, copies_n, per_t, nq, qr):
     rows, channels = byte_states.shape
-    vmem = pl.BlockSpec(memory_space=pltpu.VMEM)
+    lat = rows // STRIDE
+    steps = 4 if rows % 32 == 0 else 1
+    part = rows // steps
     return pl.pallas_call(
-        functools.partial(up_kernel_fn, copies_n, per_t, nq, qr),
+        functools.partial(up_kernel_fn, copies_n, per_t, nq, qr, lat),
+        grid=(steps,),
         out_shape=jax.ShapeDtypeStruct((rows, channels), jnp.float32),
-        in_specs=[pl.BlockSpec(memory_space=pltpu.SMEM), vmem, vmem, vmem],
-        out_specs=vmem,
+        in_specs=[
+            pl.BlockSpec(memory_space=pltpu.SMEM),
+            pl.BlockSpec(returned.shape, lambda b: (0, 0, 0)),
+            pl.BlockSpec((part, channels), lambda b: (b, 0)),
+            pl.BlockSpec(up_kernel.shape, lambda b: (0, 0, 0)),
+        ],
+        out_specs=pl.BlockSpec((part, channels), lambda b: (b, 0)),
         cost_estimate=pl.CostEstimate(
-            flops=4 * KERNEL * rows * channels + 6 * rows * rows * channels,
+            flops=4 * KERNEL * rows * channels + 4 * STRIDE * rows * (lat + 16) * channels,
             bytes_accessed=8 * rows * channels + returned.size * 2,
             transcendentals=0,
         ),

time: 46 us -> 47.3 us (1.028)
  Pallas kernels: 5.83 us -> 7.05 us
    pallas_call x1, Pallas kernels: 2.65 us -> 3.87 us  [up_and_mix(): pl.pallas_call(functools.partial(up_kernel_fn, copies_n, per_t, nq, qr, l...]
where the time goes in v8:
time: 47.3 us; the launch traced here: 46.9 us
  waiting for transfers between devices  23.6 us (50%)
  starting transfers between devices  10.9 us (23%)
  Pallas kernels  7.05 us (15%)
  other arithmetic  1.96 us (4%)
  matrix products  1.53 us (3%)
  local copies, waits for them, and re-layouts  1.04 us (2%)
  between operations  0.81 us (2%)
    all_to_all x1, waiting for transfers between devices, body(): lax.all_to_all(both_local, 'ctx', split_axis=0, concat_axis=0, tiled=True)  13.9 us
    all_to_all x1, waiting for transfers between devices, body(): lax.all_to_all(outgoing, 'ctx', split_axis=0, concat_axis=0, tiled=True)  9.75 us
    all_to_all x1, starting transfers between devices, body(): lax.all_to_all(both_local, 'ctx', split_axis=0, concat_axis=0, tiled=True)  7.25 us
    pallas_call x1, Pallas kernels, up_and_mix(): pl.pallas_call(functools.partial(up_kernel_fn, copies_n, per_t, nq, qr, l...  3.87 us
    all_to_all x1, starting transfers between devices, body(): lax.all_to_all(outgoing, 'ctx', split_axis=0, concat_axis=0, tiled=True)  3.63 us
    pallas_call x1, Pallas kernels, shorten_both(): pl.pallas_call(functools.partial(shorten_kernel, per_t, nq), out_shape=ja...  3.18 us
    dot_general x1, matrix products, attend(): jnp.einsum('hqk,hkd->hqd', weights.astype(jnp.bfloat16), value_block, pre...  0.98 us
  transfers between devices with their start and end apart: 2, of which 2 were waited for; matrix products, arithmetic and copies ran while one was open for 1% of the time, Pallas kernels for 0%

profile of v8, /device:TPU:0, one launch (start us, length us, event | category | flops | bytes accessed | tf_op | source)
XLA Modules:
  0.0 46.9 jit_solution(16532589084739266225)
XLA Ops:
  0.0 0.0 copy-start.1
  0.0 3.2 %shard_map.64 = bf16[8,272,128]{2,1,0:T(8,128)(2,1)} custom-call(f32[256,512]{1,0:T(8,128)} %x_ref.3, f32[8,4,512]{2,1,0:T(4,128)} %qk_ref.1, f32[8,4,512]{2,1,0:T(4,128)} %vk_ref.1), custom_call_target="tpu_custom_call" | custom-call | flops 205520896 | bytes 1179648 | tf_op jit(solution)/shard_map/pallas_call | solution.py:84
  3.2 7.3 %all-to-all-start = ((bf16[8,272,128]{2,1,0:T(8,128)(2,1)}), bf16[8,272,128]{2,1,0:T(8,128)(2,1)S(1)}, u32[]{:S(2)}, u32[]{:S(2)}) async-start(bf16[8,272,128]{2,1,0:T(8,128)(2,1)} %shard_map.64), calls=%async_computation | async-start | bytes 1114112 | tf_op jit(solution)/shard_map/all_to_all | solution.py:184
  11.1 0.1 iota_add_fusion
  11.2 0.1 add.89
  11.3 0.1 pad.4.clone
  11.4 0.0 copy-done.1
  11.4 0.4 fusion.9
  11.7 13.9 %all-to-all-done = bf16[8,272,128]{2,1,0:T(8,128)(2,1)S(1)} async-done(((bf16[8,272,128]{2,1,0:T(8,128)(2,1)}), bf16[8,272,128]{2,1,0:T(8,128)(2,1)S(1)}, u32[]{:S(2)}, u32[]{:S(2)}) %all-to-all-start) | async-done | bytes 557088 | tf_op jit(solution)/shard_map/all_to_all | solution.py:184
  25.7 0.1 broadcast_select_fusion
  25.9 0.5 %select_reduce_fusion = (f32[2,512]{1,0:T(2,128)S(1)}, f32[2,512,512]{1,2,0:T(8,128)S(1)}) fusion(f32[512]{0:T(512)S(1)} %log_multiply_fusion, pred[512,512]{0,1:T(8,128)(4,1)S(1)} %fusion.9, bf16[2,512,128]{2,1,0:T(8,128)(2,1)S(1)} %bitcast.47), kind=kOutput, calls=%fused_computation.1 | convolution fusion | flops 135789568 | bytes 2627584 | tf_op jit(solution)/shard_map/while/body/eval_jaxpr/hqd,hkd->hqk/dot_general | solution.py:227
  26.5 0.5 %fusion = f32[2,512]{1,0:T(2,128)S(1)} fusion(f32[2,512,512]{1,2,0:T(8,128)S(1)} %get-tuple-element.75, f32[2,512]{1,0:T(2,128)S(1)} %broadcast_maximum_fusion, f32[512]{0:T(512)S(1)} %log_multiply_fusion, pred[512,512]{0,1:T(8,128)(4,1)S(1)} %fusion.9), kind=kLoop, calls=%fused_computation.2 | loop fusion | flops 2096128 | bytes 2369536 | tf_op jit(solution)/shard_map/while/body/eval_jaxpr/reduce_sum | solution.py:240
  27.0 1.0 %fusion.3 = bf16[2,512,128]{2,1,0:T(8,128)(2,1)S(1)} fusion(bf16[2,512,128]{2,1,0:T(8,128)(2,1)S(1)} %bitcast.53, f32[2,512,512]{1,2,0:T(8,128)S(1)} %get-tuple-element.75, f32[2,512]{1,0:T(2,128)S(1)} %broadcast_maximum_fusion, f32[512]{0:T(512)S(1)} %log_multiply_fusion, pred[512,512]{0,1:T(8,128)(4,1)S(1)} %fusion.9, f32[2,512]{1,0:T(2,128)S(1)} %get-tuple-element.73, ...), kind=kOutput, calls=%fused_computation.6 | convolution fusion | flops 136708096 | bytes 2897920 | tf_op jit(solution)/shard_map/while/body/eval_jaxpr/hqk,hkd->hqd/dot_general | solution.py:241
  28.1 0.8 %maximum_maximum_fusion = bf16[8,144,128]{2,1,0:T(8,128)(2,1)} fusion(bf16[8,4,128]{2,1,0:T(4,128)(2,1)S(1)} %bitcast.55, bf16[8,128,128]{2,1,0:T(8,128)(2,1)S(1)} %bitcast.50, bf16[144]{0:T(256)(128)(2,1)S(1)} %pad.4.clone), kind=kLoop, calls=%fused_computation.15 | loop fusion | flops 884736 | bytes 565536 | tf_op jit(solution)/shard_map/concatenate | solution.py:264
  28.9 3.6 %all-to-all-start.1 = ((bf16[8,144,128]{2,1,0:T(8,128)(2,1)}), bf16[8,144,128]{2,1,0:T(8,128)(2,1)S(1)}, u32[]{:S(2)}, u32[]{:S(2)}) async-start(bf16[8,144,128]{2,1,0:T(8,128)(2,1)} %maximum_maximum_fusion), calls=%async_computation.1 | async-start | bytes 589824 | tf_op jit(solution)/shard_map/all_to_all | solution.py:272
  32.6 9.8 %all-to-all-done.1.ret_ref = bf16[8,144,128]{2,1,0:T(8,128)(2,1)S(1)} async-done(((bf16[8,144,128]{2,1,0:T(8,128)(2,1)}), bf16[8,144,128]{2,1,0:T(8,128)(2,1)S(1)}, u32[]{:S(2)}, u32[]{:S(2)}) %all-to-all-start.1) | async-done | bytes 294944 | tf_op jit(solution)/shard_map/all_to_all | solution.py:272
  42.3 0.0 copy-start
  42.3 0.7 %copy-done = bf16[8,144,128]{2,1,0:T(8,128)(2,1)} copy-done((bf16[8,144,128]{2,1,0:T(8,128)(2,1)}, bf16[8,144,128]{2,1,0:T(8,128)(2,1)S(1)}, u32[]{:S(2)}) %copy-start) | copy-done | bytes 294936
  43.0 3.9 %shard_map.65 = f32[256,512]{1,0:T(8,128)} custom-call(s32[1]{0:T(128)} %bitcast.1.lim_ref, bf16[8,144,128]{2,1,0:T(8,128)(2,1)} %copy-done, f32[256,512]{1,0:T(8,128)} %x_ref.3, f32[8,4,512]{2,1,0:T(4,128)} %up_ref.1), custom_call_target="tpu_custom_call" | custom-call | flops 171966464 | bytes 1343488 | tf_op jit(solution)/shard_map/pallas_call | solution.py:143
  (19 shorter events, 0.2 us)
Async XLA Ops:
  0.0 11.4 %copy-start.1 = (s32[512]{0:T(512)S(1)}, s32[512]{0:T(512)}, u32[]{:S(2)}) copy-start(s32[512]{0:T(512)} %param.8) | copy-start | bytes 6148
  3.2 22.4 %all-to-all-start = ((bf16[8,272,128]{2,1,0:T(8,128)(2,1)}), bf16[8,272,128]{2,1,0:T(8,128)(2,1)S(1)}, u32[]{:S(2)}, u32[]{:S(2)}) async-start(bf16[8,272,128]{2,1,0:T(8,128)(2,1)} %shard_map.64), calls=%async_computation | async-start | bytes 1114112 | tf_op jit(solution)/shard_map/all_to_all | solution.py:184
  28.9 13.4 %all-to-all-start.1 = ((bf16[8,144,128]{2,1,0:T(8,128)(2,1)}), bf16[8,144,128]{2,1,0:T(8,128)(2,1)S(1)}, u32[]{:S(2)}, u32[]{:S(2)}) async-start(bf16[8,144,128]{2,1,0:T(8,128)(2,1)} %maximum_maximum_fusion), calls=%async_computation.1 | async-start | bytes 589824 | tf_op jit(solution)/shard_map/all_to_all | solution.py:272
  42.3 0.7 %copy-start = (bf16[8,144,128]{2,1,0:T(8,128)(2,1)}, bf16[8,144,128]{2,1,0:T(8,128)(2,1)S(1)}, u32[]{:S(2)}) copy-start(bf16[8,144,128]{2,1,0:T(8,128)(2,1)S(1)} %all-to-all-done.1.ret_ref) | copy-start | bytes 884740

commit v9 on v4

--- a/solution.py
+++ b/solution.py
@@ -149,6 +149,73 @@
     )(limit, returned, byte_states, up_kernel)
 
 
+def attend_kernel(lat, nq, denom, kv_ref, bias_ref, out_ref):
+    n_ctx = kv_ref.shape[0]
+    total = n_ctx * lat
+    lanes = CHANNEL_WIDTH
+    edge_at = 2 * nq * lat
+    edges = kv_ref[:, pl.ds(edge_at, 16), :].astype(jnp.float32)
+    first_row = lax.broadcasted_iota(jnp.int32, (lat, lanes), 0) == 0
+    sharp = jnp.log(lax.broadcasted_iota(jnp.int32, (total, 1), 0).astype(jnp.float32) + 2.0) / denom
+    tile_row = lax.broadcasted_iota(jnp.int32, (16, lanes), 0)
+    tiles = [jnp.zeros((16, lanes), jnp.float32) for _ in range(n_ctx)]
+
+    def gathered(slot):
+        pieces = []
+        for i in range(n_ctx):
+            own = edges[i, 0 * 2 * nq + slot : 0 * 2 * nq + slot + 1] + edges[i, 1 * 2 * nq + slot : 1 * 2 * nq + slot + 1]
+            if i > 0:
+                before = edges[i - 1, 2 * 2 * nq + slot : 2 * 2 * nq + slot + 1] + edges[
+                    i - 1, 3 * 2 * nq + slot : 3 * 2 * nq + slot + 1
+                ]
+            else:
+                before = jnp.zeros_like(own)
+            fixed = (own + before).astype(jnp.bfloat16).astype(jnp.float32)
+            piece = kv_ref[i, pl.ds(slot * lat, lat), :].astype(jnp.float32)
+            pieces.append(jnp.where(first_row, fixed, piece))
+        return jnp.concatenate(pieces, 0).astype(jnp.bfloat16)
+
+    for q in range(nq):
+        keys = gathered(q)
+        values = gathered(nq + q)
+        scores = lax.dot_general(
+            keys, keys, (((1,), (1,)), ((), ())), preferred_element_type=jnp.float32
+        ) * sharp
+        scores = scores + bias_ref[...]
+        top = jnp.max(scores, axis=1, keepdims=True)
+        weights = jnp.exp(scores - top)
+        sums = jnp.sum(weights, axis=1, keepdims=True)
+        rows = jnp.dot(weights.astype(jnp.bfloat16), values, preferred_element_type=jnp.float32)
+        rows = (rows / sums).astype(jnp.bfloat16)
+        for d in range(n_ctx):
+            out_ref[d, pl.ds(q * lat, lat), :] = rows[d * lat : (d + 1) * lat]
+        wide = rows.astype(jnp.float32)
+        for d in range(1, n_ctx):
+            for e in range(2):
+                at = d * lat - 2 + e
+                tiles[d] = jnp.where(tile_row == 2 * q + e, wide[at : at + 1], tiles[d])
+    for d in range(n_ctx):
+        out_ref[d, pl.ds(nq * lat, 16), :] = tiles[d].astype(jnp.bfloat16)
+
+
+def attend_whole(both_all, bias, nq, lat, denom):
+    n_ctx, _, lanes = both_all.shape
+    total = n_ctx * lat
+    vmem = pl.BlockSpec(memory_space=pltpu.VMEM)
+    ret_rows = nq * lat + 16
+    return pl.pallas_call(
+        functools.partial(attend_kernel, lat, nq, denom),
+        out_shape=jax.ShapeDtypeStruct((n_ctx, ret_rows, lanes), jnp.bfloat16),
+        in_specs=[vmem, vmem],
+        out_specs=vmem,
+        cost_estimate=pl.CostEstimate(
+            flops=4 * nq * total * total * lanes,
+            bytes_accessed=both_all.size * 2 + total * total * 4 + n_ctx * ret_rows * lanes * 2,
+            transcendentals=nq * total * total,
+        ),
+    )(both_all, bias)
+
+
 def body(byte_states, doc_length, block_ids, qk_kernel, value_kernel, up_kernel):
     rows_here, channels = byte_states.shape
     lat_dev = rows_here // STRIDE
@@ -172,6 +239,20 @@
             both_local[:, None], (groups_n, copies_n, kv_rows, CHANNEL_WIDTH)
         ).reshape(n_ctx, kv_rows, CHANNEL_WIDTH)
     both_all = lax.all_to_all(both_local, "ctx", split_axis=0, concat_axis=0, tiled=True)
+    if copies_n == 1 and lat_total <= 1024 and nq <= 8 and lat_dev % 16 == 0:
+        lat_len = doc_length[0] // STRIDE
+        places = jnp.arange(lat_total, dtype=jnp.int32)
+        visible = (
+            (block_ids[None, :] <= block_ids[:, None])
+            & (places[None, :] < lat_len)
+            & ((places[None, :] != places[:, None]) | (places[:, None] == 0))
+        )
+        bias = jnp.where(visible, 0.0, -1e30).astype(jnp.float32)
+        denom = math.sqrt(float(CHANNEL_WIDTH)) * math.sqrt(math.log(float(lat_total)))
+        outgoing = attend_whole(both_all, bias, nq, lat_dev, denom)
+        returned = lax.all_to_all(outgoing, "ctx", split_axis=0, concat_axis=0, tiled=True)
+        limit = (doc_length[0] - device * rows_here).reshape(1).astype(jnp.int32)
+        return up_and_mix(limit, returned, byte_states, up_kernel, copies_n, per_t, nq, query_rows)
     main_kv = both_all[:, : 2 * nq * lat_dev].reshape(n_ctx, 2 * nq, lat_dev, CHANNEL_WIDTH)
     edge = both_all[:, 2 * nq * lat_dev : 2 * nq * lat_dev + 8 * nq].astype(jnp.float32)
     edge = edge.reshape(n_ctx, 4, 2 * nq, CHANNEL_WIDTH)

time: 46.1 us -> 46.9 us (1.017)
  Pallas kernels: 5.88 us -> 9.11 us
  matrix products: 1.53 us -> 0 us
  waiting for transfers between devices: 23.6 us -> 22.3 us
  local copies, waits for them, and re-layouts: 1.04 us -> 2.22 us
  other arithmetic: 1.96 us -> 1.28 us
    pallas_call x0 -> x1, Pallas kernels: none -> 3.22 us  [attend_whole(): pl.pallas_call(functools.partial(attend_kernel, lat, nq, denom), out_shap...]
    dot_general x2 -> x0, matrix products: 1.53 us -> none  [the longest x1 0.98 us: attend(): jnp.einsum('hqk,hkd->hqd', weights.astype(jnp.bfloat16), value_block, pre...]
    unnamed x4 -> x6, local copies, waits for them, and re-layouts: 0.71 us -> 2.22 us
    all_to_all x1, waiting for transfers between devices: 13.9 us -> 12.5 us  [body(): lax.all_to_all(both_local, 'ctx', split_axis=0, concat_axis=0, tiled=True)]
    select_n x1, other arithmetic: 0.11 us -> 1.27 us  [body(): bias = jnp.where(visible, 0.0, -1e+30).astype(jnp.float32)]
    concatenate x1 -> x0, other arithmetic: 0.84 us -> none  [body(): jnp.concatenate([attended.reshape(n_ctx, main_rows, CHANNEL_WIDTH), rim_o...]
    reduce_sum x1 -> x0, other arithmetic: 0.52 us -> none  [attend(): new_sum = run_sum * factor + jnp.sum(weights, axis=2)]
  transfers between devices with their start and end apart: 2 -> 2, of which waited for: 2 -> 2; matrix products, arithmetic and copies ran while one was open for 1% -> 3% of each run, Pallas kernels for 0% -> 0%
where the time goes in v9:
time: 46.9 us; the launch traced here: 46.5 us
  waiting for transfers between devices  22.3 us (48%)
  starting transfers between devices  10.9 us (23%)
  Pallas kernels  9.11 us (19%)
  local copies, waits for them, and re-layouts  2.22 us (5%)
  other arithmetic  1.28 us (3%)
  between operations  0.69 us (1%)
    all_to_all x1, waiting for transfers between devices, body(): lax.all_to_all(both_local, 'ctx', split_axis=0, concat_axis=0, tiled=True)  12.5 us
    all_to_all x1, waiting for transfers between devices, body(): lax.all_to_all(outgoing, 'ctx', split_axis=0, concat_axis=0, tiled=True)  9.75 us
    all_to_all x1, starting transfers between devices, body(): lax.all_to_all(both_local, 'ctx', split_axis=0, concat_axis=0, tiled=True)  7.25 us
    all_to_all x1, starting transfers between devices, body(): lax.all_to_all(outgoing, 'ctx', split_axis=0, concat_axis=0, tiled=True)  3.64 us
    pallas_call x1, Pallas kernels, attend_whole(): pl.pallas_call(functools.partial(attend_kernel, lat, nq, denom), out_shap...  3.22 us
    pallas_call x1, Pallas kernels, shorten_both(): pl.pallas_call(functools.partial(shorten_kernel, per_t, nq), out_shape=ja...  3.19 us
    pallas_call x1, Pallas kernels, up_and_mix(): pl.pallas_call(functools.partial(up_kernel_fn, copies_n, per_t, nq, qr),...  2.7 us
    unnamed x6, local copies, waits for them, and re-layouts  2.22 us
  transfers between devices with their start and end apart: 2, of which 2 were waited for; matrix products, arithmetic and copies ran while one was open for 3% of the time, Pallas kernels for 0%

profile of v9, /device:TPU:0, one launch (start us, length us, event | category | flops | bytes accessed | tf_op | source)
XLA Modules:
  0.0 46.5 jit_solution(11822870475166374194)
XLA Ops:
  0.0 3.2 %shard_map.64 = bf16[8,272,128]{2,1,0:T(8,128)(2,1)} custom-call(f32[256,512]{1,0:T(8,128)} %x_ref.3, f32[8,4,512]{2,1,0:T(4,128)} %qk_ref.1, f32[8,4,512]{2,1,0:T(4,128)} %vk_ref.1), custom_call_target="tpu_custom_call" | custom-call | flops 205520896 | bytes 1179648 | tf_op jit(solution)/shard_map/pallas_call | solution.py:84
  3.2 7.3 %all-to-all-start = ((bf16[8,272,128]{2,1,0:T(8,128)(2,1)}), bf16[8,272,128]{2,1,0:T(8,128)(2,1)S(1)}, u32[]{:S(2)}, u32[]{:S(2)}) async-start(bf16[8,272,128]{2,1,0:T(8,128)(2,1)} %shard_map.64), calls=%async_computation | async-start | bytes 1114112 | tf_op jit(solution)/shard_map/all_to_all | solution.py:241
  11.1 0.0 copy-start.2
  11.1 0.7 %copy-done.2 = s32[512]{0:T(512)S(1)} copy-done((s32[512]{0:T(512)S(1)}, s32[512]{0:T(512)}, u32[]{:S(2)}) %copy-start.2) | copy-done | bytes 2072
  11.8 1.3 %fusion.2.bias_ref = f32[512,512]{1,0:T(8,128)} fusion(s32[512]{0:T(512)S(1)} %copy-done.2, pred[512]{0:T(512)(128)(4,1)S(1)} %get-tuple-element.5, pred[512]{0:T(512)(128)(4,1)S(1)} %get-tuple-element.6), kind=kLoop, calls=%fused_computation.3 | loop fusion | flops 1572864 | bytes 1051648 | tf_op jit(solution)/shard_map/jit(_where)/select_n | solution.py:250
  13.1 12.5 %all-to-all-done.kv_ref = bf16[8,272,128]{2,1,0:T(8,128)(2,1)S(1)} async-done(((bf16[8,272,128]{2,1,0:T(8,128)(2,1)}), bf16[8,272,128]{2,1,0:T(8,128)(2,1)S(1)}, u32[]{:S(2)}, u32[]{:S(2)}) %all-to-all-start) | async-done | bytes 557088 | tf_op jit(solution)/shard_map/all_to_all | solution.py:241
  25.6 0.0 copy-start
  25.6 0.8 %copy-done = bf16[8,272,128]{2,1,0:T(8,128)(2,1)} copy-done((bf16[8,272,128]{2,1,0:T(8,128)(2,1)}, bf16[8,272,128]{2,1,0:T(8,128)(2,1)S(1)}, u32[]{:S(2)}) %copy-start) | copy-done | bytes 557080
  26.5 3.2 %shard_map.65 = bf16[8,144,128]{2,1,0:T(8,128)(2,1)} custom-call(bf16[8,272,128]{2,1,0:T(8,128)(2,1)} %copy-done, f32[512,512]{1,0:T(8,128)} %fusion.2.bias_ref), custom_call_target="tpu_custom_call" | custom-call | flops 268435456 | bytes 1900544 | tf_op jit(solution)/shard_map/pallas_call | solution.py:206
  29.7 3.6 %all-to-all-start.1 = ((bf16[8,144,128]{2,1,0:T(8,128)(2,1)}), bf16[8,144,128]{2,1,0:T(8,128)(2,1)S(1)}, u32[]{:S(2)}, u32[]{:S(2)}) async-start(bf16[8,144,128]{2,1,0:T(8,128)(2,1)} %shard_map.65), calls=%async_computation.1 | async-start | bytes 589824 | tf_op jit(solution)/shard_map/all_to_all | solution.py:253
  33.3 9.8 %all-to-all-done.1.ret_ref = bf16[8,144,128]{2,1,0:T(8,128)(2,1)S(1)} async-done(((bf16[8,144,128]{2,1,0:T(8,128)(2,1)}), bf16[8,144,128]{2,1,0:T(8,128)(2,1)S(1)}, u32[]{:S(2)}, u32[]{:S(2)}) %all-to-all-start.1) | async-done | bytes 294944 | tf_op jit(solution)/shard_map/all_to_all | solution.py:253
  43.1 0.0 copy-start.1
  43.1 0.7 %copy-done.1 = bf16[8,144,128]{2,1,0:T(8,128)(2,1)} copy-done((bf16[8,144,128]{2,1,0:T(8,128)(2,1)}, bf16[8,144,128]{2,1,0:T(8,128)(2,1)S(1)}, u32[]{:S(2)}) %copy-start.1) | copy-done | bytes 294936
  43.8 2.7 %shard_map.66 = f32[256,512]{1,0:T(8,128)} custom-call(s32[1]{0:T(128)} %bitcast.1.lim_ref, bf16[8,144,128]{2,1,0:T(8,128)(2,1)} %copy-done.1, f32[256,512]{1,0:T(8,128)} %x_ref.3, f32[8,4,512]{2,1,0:T(4,128)} %up_ref.1), custom_call_target="tpu_custom_call" | custom-call | flops 205520896 | bytes 1343488 | tf_op jit(solution)/shard_map/pallas_call | solution.py:139
  (1 shorter events, 0.0 us)
Async XLA Ops:
  3.2 22.4 %all-to-all-start = ((bf16[8,272,128]{2,1,0:T(8,128)(2,1)}), bf16[8,272,128]{2,1,0:T(8,128)(2,1)S(1)}, u32[]{:S(2)}, u32[]{:S(2)}) async-start(bf16[8,272,128]{2,1,0:T(8,128)(2,1)} %shard_map.64), calls=%async_computation | async-start | bytes 1114112 | tf_op jit(solution)/shard_map/all_to_all | solution.py:241
  11.1 0.7 %copy-start.2 = (s32[512]{0:T(512)S(1)}, s32[512]{0:T(512)}, u32[]{:S(2)}) copy-start(s32[512]{0:T(512)} %param.8) | copy-start | bytes 6148
  25.6 0.8 %copy-start = (bf16[8,272,128]{2,1,0:T(8,128)(2,1)}, bf16[8,272,128]{2,1,0:T(8,128)(2,1)S(1)}, u32[]{:S(2)}) copy-start(bf16[8,272,128]{2,1,0:T(8,128)(2,1)S(1)} %all-to-all-done.kv_ref) | copy-start | bytes 1671172
  29.7 13.4 %all-to-all-start.1 = ((bf16[8,144,128]{2,1,0:T(8,128)(2,1)}), bf16[8,144,128]{2,1,0:T(8,128)(2,1)S(1)}, u32[]{:S(2)}, u32[]{:S(2)}) async-start(bf16[8,144,128]{2,1,0:T(8,128)(2,1)} %shard_map.65), calls=%async_computation.1 | async-start | bytes 589824 | tf_op jit(solution)/shard_map/all_to_all | solution.py:253
  43.1 0.7 %copy-start.1 = (bf16[8,144,128]{2,1,0:T(8,128)(2,1)}, bf16[8,144,128]{2,1,0:T(8,128)(2,1)S(1)}, u32[]{:S(2)}) copy-start(bf16[8,144,128]{2,1,0:T(8,128)(2,1)S(1)} %all-to-all-done.1.ret_ref) | copy-start | bytes 884740

commit v10 on v7

--- a/solution.py
+++ b/solution.py
@@ -94,12 +94,10 @@
     )(byte_states, qk_kernel, value_kernel)
 
 
-def up_kernel_fn(copies_n, per_t, nq, qr, lim_ref, ret_ref, x_ref, up_ref, out_ref):
+def up_kernel_fn(lim_ref, ext_ref, x_ref, up_ref, out_ref):
     rows, channels = x_ref.shape
     lat = rows // STRIDE
-    lanes = CHANNEL_WIDTH
-    blocks = channels // lanes
-    wide = lat + 16
+    wide = ext_ref.shape[1]
     pick_row = lax.broadcasted_iota(jnp.int32, (rows, wide), 0)
     pick_col = lax.broadcasted_iota(jnp.int32, (rows, wide), 1)
     latent = pick_row // STRIDE
@@ -110,17 +108,7 @@
     phase_row = lax.broadcasted_iota(jnp.int32, (8, channels), 0) % STRIDE
     branch = None
     for t in range(STRIDE):
-        att_parts = []
-        rim_parts = []
-        for block in range(blocks):
-            g = t * per_t + block // nq
-            q = block % nq
-            pieces = [ret_ref[g * copies_n + s, pl.ds(q * qr, qr), :] for s in range(copies_n)]
-            att_parts.append(pieces[0] if copies_n == 1 else jnp.concatenate(pieces, 0))
-            rim_parts.append(ret_ref[g * copies_n + copies_n - 1, pl.ds(nq * qr + 2 * q, 2), :])
-        att = jnp.concatenate(att_parts, 1).astype(jnp.float32)
-        rim = jnp.concatenate(rim_parts, 1).astype(jnp.float32)
-        extended = jnp.concatenate([att, rim, jnp.zeros((14, channels), jnp.float32)], 0).astype(jnp.bfloat16)
+        extended = ext_ref[t]
         one = jnp.dot(take_one, extended, preferred_element_type=jnp.float32)
         two = jnp.dot(take_two, extended, preferred_element_type=jnp.float32)
         w_one = up_ref[0, pl.ds(t, 1), :]
@@ -137,18 +125,27 @@
 
 def up_and_mix(limit, returned, byte_states, up_kernel, copies_n, per_t, nq, qr):
     rows, channels = byte_states.shape
+    lat = rows // STRIDE
+    lanes = CHANNEL_WIDTH
+    groups_n = returned.shape[0] // copies_n
+    by_source = returned.reshape(STRIDE, per_t, copies_n, returned.shape[1], lanes)
+    main = by_source[:, :, :, : nq * qr].reshape(STRIDE, per_t, copies_n, nq, qr, lanes)
+    main = main.transpose(0, 2, 4, 1, 3, 5).reshape(STRIDE, lat, channels)
+    rim = by_source[:, :, copies_n - 1, nq * qr : nq * qr + 2 * nq].reshape(STRIDE, per_t, nq, 2, lanes)
+    rim = rim.transpose(0, 3, 1, 2, 4).reshape(STRIDE, 2, channels)
+    extended = jnp.concatenate([main, rim, jnp.zeros((STRIDE, 14, channels), jnp.bfloat16)], 1)
     vmem = pl.BlockSpec(memory_space=pltpu.VMEM)
     return pl.pallas_call(
-        functools.partial(up_kernel_fn, copies_n, per_t, nq, qr),
+        up_kernel_fn,
         out_shape=jax.ShapeDtypeStruct((rows, channels), jnp.float32),
         in_specs=[pl.BlockSpec(memory_space=pltpu.SMEM), vmem, vmem, vmem],
         out_specs=vmem,
         cost_estimate=pl.CostEstimate(
-            flops=4 * KERNEL * rows * channels + 6 * rows * rows * channels,
-            bytes_accessed=8 * rows * channels + returned.size * 2,
+            flops=4 * KERNEL * rows * channels + 4 * STRIDE * rows * (lat + 16) * channels,
+            bytes_accessed=8 * rows * channels + extended.size * 2,
             transcendentals=0,
         ),
-    )(limit, returned, byte_states, up_kernel)
+    )(limit, extended, byte_states, up_kernel)
 
 
 def body(byte_states, doc_length, block_ids, qk_kernel, value_kernel, up_kernel):

time: 46 us -> 46.6 us (1.013)
  other arithmetic: 1.96 us -> 2.79 us
    concatenate x0 -> x1, other arithmetic: none -> 0.83 us  [up_and_mix(): jnp.concatenate([main, rim, jnp.zeros((STRIDE, 14, channels), jnp.bfloat1...]
    unnamed x4 -> x2, local copies, waits for them, and re-layouts: 0.71 us -> 0.01 us
where the time goes in v10:
time: 46.6 us; the launch traced here: 46.2 us
  waiting for transfers between devices  23.6 us (51%)
  starting transfers between devices  10.9 us (23%)
  Pallas kernels  5.83 us (13%)
  other arithmetic  2.79 us (6%)
  matrix products  1.52 us (3%)
  between operations  0.83 us (2%)
  local copies, waits for them, and re-layouts  0.81 us (2%)
    all_to_all x1, waiting for transfers between devices, body(): lax.all_to_all(both_local, 'ctx', split_axis=0, concat_axis=0, tiled=True)  13.9 us
    all_to_all x1, waiting for transfers between devices, body(): lax.all_to_all(outgoing, 'ctx', split_axis=0, concat_axis=0, tiled=True)  9.67 us
    all_to_all x1, starting transfers between devices, body(): lax.all_to_all(both_local, 'ctx', split_axis=0, concat_axis=0, tiled=True)  7.25 us
    all_to_all x1, starting transfers between devices, body(): lax.all_to_all(outgoing, 'ctx', split_axis=0, concat_axis=0, tiled=True)  3.64 us
    pallas_call x1, Pallas kernels, shorten_both(): pl.pallas_call(functools.partial(shorten_kernel, per_t, nq), out_shape=ja...  3.18 us
    pallas_call x1, Pallas kernels, up_and_mix(): pl.pallas_call(up_kernel_fn, out_shape=jax.ShapeDtypeStruct((rows, channe...  2.65 us
    dot_general x1, matrix products, attend(): jnp.einsum('hqk,hkd->hqd', weights.astype(jnp.bfloat16), value_block, pre...  0.98 us
  transfers between devices with their start and end apart: 2, of which 2 were waited for; matrix products, arithmetic and copies ran while one was open for 1% of the time, Pallas kernels for 0%

profile of v10, /device:TPU:0, one launch (start us, length us, event | category | flops | bytes accessed | tf_op | source)
XLA Modules:
  0.0 46.2 jit_solution(1986256866484763182)
XLA Ops:
  0.0 0.0 copy-start
  0.0 3.2 %shard_map.64 = bf16[8,272,128]{2,1,0:T(8,128)(2,1)} custom-call(f32[256,512]{1,0:T(8,128)} %x_ref.3, f32[8,4,512]{2,1,0:T(4,128)} %qk_ref.1, f32[8,4,512]{2,1,0:T(4,128)} %vk_ref.1), custom_call_target="tpu_custom_call" | custom-call | flops 205520896 | bytes 1179648 | tf_op jit(solution)/shard_map/pallas_call | solution.py:84
  3.2 7.3 %all-to-all-start = ((bf16[8,272,128]{2,1,0:T(8,128)(2,1)}), bf16[8,272,128]{2,1,0:T(8,128)(2,1)S(1)}, u32[]{:S(2)}, u32[]{:S(2)}) async-start(bf16[8,272,128]{2,1,0:T(8,128)(2,1)} %shard_map.64), calls=%async_computation | async-start | bytes 1114112 | tf_op jit(solution)/shard_map/all_to_all | solution.py:173
  11.1 0.1 iota_add_fusion
  11.2 0.1 add.89
  11.3 0.1 pad.7.clone
  11.4 0.0 copy-done
  11.4 0.4 fusion.9
  11.7 13.9 %all-to-all-done = bf16[8,272,128]{2,1,0:T(8,128)(2,1)S(1)} async-done(((bf16[8,272,128]{2,1,0:T(8,128)(2,1)}), bf16[8,272,128]{2,1,0:T(8,128)(2,1)S(1)}, u32[]{:S(2)}, u32[]{:S(2)}) %all-to-all-start) | async-done | bytes 557088 | tf_op jit(solution)/shard_map/all_to_all | solution.py:173
  25.7 0.1 broadcast_select_fusion
  25.9 0.5 %select_reduce_fusion = (f32[2,512]{1,0:T(2,128)S(1)}, f32[2,512,512]{1,2,0:T(8,128)S(1)}) fusion(f32[512]{0:T(512)S(1)} %log_multiply_fusion, pred[512,512]{0,1:T(8,128)(4,1)S(1)} %fusion.9, bf16[2,512,128]{2,1,0:T(8,128)(2,1)S(1)} %bitcast.58), kind=kOutput, calls=%fused_computation.1 | convolution fusion | flops 135789568 | bytes 2627584 | tf_op jit(solution)/shard_map/while/body/eval_jaxpr/hqd,hkd->hqk/dot_general | solution.py:216
  26.5 0.5 %fusion = f32[2,512]{1,0:T(2,128)S(1)} fusion(f32[2,512,512]{1,2,0:T(8,128)S(1)} %get-tuple-element.75, f32[2,512]{1,0:T(2,128)S(1)} %broadcast_maximum_fusion, f32[512]{0:T(512)S(1)} %log_multiply_fusion, pred[512,512]{0,1:T(8,128)(4,1)S(1)} %fusion.9), kind=kLoop, calls=%fused_computation.2 | loop fusion | flops 2096128 | bytes 2369536 | tf_op jit(solution)/shard_map/while/body/eval_jaxpr/reduce_sum | solution.py:229
  27.0 1.0 %fusion.3 = bf16[2,512,128]{2,1,0:T(8,128)(2,1)S(1)} fusion(bf16[2,512,128]{2,1,0:T(8,128)(2,1)S(1)} %bitcast.67, f32[2,512,512]{1,2,0:T(8,128)S(1)} %get-tuple-element.75, f32[2,512]{1,0:T(2,128)S(1)} %broadcast_maximum_fusion, f32[512]{0:T(512)S(1)} %log_multiply_fusion, pred[512,512]{0,1:T(8,128)(4,1)S(1)} %fusion.9, f32[2,512]{1,0:T(2,128)S(1)} %get-tuple-element.73, ...), kind=kOutput, calls=%fused_computation.6 | convolution fusion | flops 136708096 | bytes 2897920 | tf_op jit(solution)/shard_map/while/body/eval_jaxpr/hqk,hkd->hqd/dot_general | solution.py:230
  28.1 0.8 %maximum_maximum_fusion.1 = bf16[8,144,128]{2,1,0:T(8,128)(2,1)} fusion(bf16[8,4,128]{2,1,0:T(4,128)(2,1)S(1)} %bitcast.70, bf16[8,128,128]{2,1,0:T(8,128)(2,1)S(1)} %bitcast.63, bf16[144]{0:T(256)(128)(2,1)S(1)} %pad.7.clone), kind=kLoop, calls=%fused_computation.16 | loop fusion | flops 884736 | bytes 565536 | tf_op jit(solution)/shard_map/concatenate | solution.py:253
  28.9 3.6 %all-to-all-start.1 = ((bf16[8,144,128]{2,1,0:T(8,128)(2,1)}), bf16[8,144,128]{2,1,0:T(8,128)(2,1)S(1)}, u32[]{:S(2)}, u32[]{:S(2)}) async-start(bf16[8,144,128]{2,1,0:T(8,128)(2,1)} %maximum_maximum_fusion.1), calls=%async_computation.1 | async-start | bytes 589824 | tf_op jit(solution)/shard_map/all_to_all | solution.py:261
  32.6 0.1 pad.4.clone
  32.7 9.7 %all-to-all-done.1 = bf16[8,144,128]{2,1,0:T(8,128)(2,1)S(1)} async-done(((bf16[8,144,128]{2,1,0:T(8,128)(2,1)}), bf16[8,144,128]{2,1,0:T(8,128)(2,1)S(1)}, u32[]{:S(2)}, u32[]{:S(2)}) %all-to-all-start.1) | async-done | bytes 294944 | tf_op jit(solution)/shard_map/all_to_all | solution.py:261
  42.4 0.3 copy.20
  42.6 0.1 reshape.177
  42.8 0.8 %maximum_maximum_fusion.ext_ref = bf16[4,80,512]{2,1,0:T(8,128)(2,1)} fusion(bf16[4,2,512]{2,1,0:T(2,128)(2,1)S(1)} %bitcast.69, bf16[4,64,512]{2,1,0:T(8,128)(2,1)S(1)} %reshape.177, bf16[80]{0:T(256)(128)(2,1)S(1)} %pad.4.clone), kind=kLoop, calls=%fused_computation.15 | loop fusion | flops 983040 | bytes 598176 | tf_op jit(solution)/shard_map/concatenate | solution.py:136
  43.6 2.7 %shard_map.65 = f32[256,512]{1,0:T(8,128)} custom-call(s32[1]{0:T(128)} %bitcast.1.lim_ref, bf16[4,80,512]{2,1,0:T(8,128)(2,1)} %maximum_maximum_fusion.ext_ref, f32[256,512]{1,0:T(8,128)} %x_ref.3, f32[8,4,512]{2,1,0:T(4,128)} %up_ref.1), custom_call_target="tpu_custom_call" | custom-call | flops 171966464 | bytes 1376256 | tf_op jit(solution)/shard_map/pallas_call | solution.py:138
  (22 shorter events, 0.3 us)
Async XLA Ops:
  0.0 11.4 %copy-start = (s32[512]{0:T(512)S(1)}, s32[512]{0:T(512)}, u32[]{:S(2)}) copy-start(s32[512]{0:T(512)} %param.8) | copy-start | bytes 6148
  3.2 22.4 %all-to-all-start = ((bf16[8,272,128]{2,1,0:T(8,128)(2,1)}), bf16[8,272,128]{2,1,0:T(8,128)(2,1)S(1)}, u32[]{:S(2)}, u32[]{:S(2)}) async-start(bf16[8,272,128]{2,1,0:T(8,128)(2,1)} %shard_map.64), calls=%async_computation | async-start | bytes 1114112 | tf_op jit(solution)/shard_map/all_to_all | solution.py:173
  28.9 13.4 %all-to-all-start.1 = ((bf16[8,144,128]{2,1,0:T(8,128)(2,1)}), bf16[8,144,128]{2,1,0:T(8,128)(2,1)S(1)}, u32[]{:S(2)}, u32[]{:S(2)}) async-start(bf16[8,144,128]{2,1,0:T(8,128)(2,1)} %maximum_maximum_fusion.1), calls=%async_computation.1 | async-start | bytes 589824 | tf_op jit(solution)/shard_map/all_to_all | solution.py:261

commit v11 on v6

--- a/solution.py
+++ b/solution.py
@@ -250,8 +250,28 @@
         jnp.zeros((head_here, query_count), jnp.float32),
         jnp.zeros((head_here, query_count, CHANNEL_WIDTH), jnp.float32),
     )
-    finals, unused = lax.scan(attend, initial, jnp.arange(block_count, dtype=jnp.int32) * block_len)
-    attended = (finals[2] / finals[1][:, :, None]).astype(jnp.bfloat16)
+    if block_count == 1:
+        raw_affinity = (
+            jnp.einsum("hqd,hkd->hqk", query_heads, key_heads, preferred_element_type=jnp.float32)
+            * sharpness_divisor[None, :, None]
+        )
+        key_pos = jnp.arange(lat_total, dtype=jnp.int32)
+        visible = (
+            (block_ids[None, :] <= query_seg[:, None])
+            & (key_pos[None, :] < lat_len)
+            & ((key_pos[None, :] != asking_index[:, None]) | (asking_index[:, None] == 0))
+        )
+        raw_affinity = jnp.where(visible[None], raw_affinity, -1e30)
+        top = jnp.max(raw_affinity, axis=2, keepdims=True)
+        weights = jnp.where(visible[None], jnp.exp(raw_affinity - top), 0.0)
+        sums = jnp.sum(weights, axis=2, keepdims=True)
+        attended = jnp.einsum(
+            "hqk,hkd->hqd", weights.astype(jnp.bfloat16), value_heads, preferred_element_type=jnp.float32
+        )
+        attended = (attended / sums).astype(jnp.bfloat16)
+    else:
+        finals, unused = lax.scan(attend, initial, jnp.arange(block_count, dtype=jnp.int32) * block_len)
+        attended = (finals[2] / finals[1][:, :, None]).astype(jnp.bfloat16)
     attended = attended.reshape(nq, n_ctx, query_rows, CHANNEL_WIDTH).transpose(1, 0, 2, 3)
     rim_out = jnp.concatenate(
         [jnp.zeros((1, nq, 2, CHANNEL_WIDTH), jnp.bfloat16), attended[:-1, :, query_rows - 2 :]], 0

time: 45.8 us -> 46.4 us (1.013)
  matrix products: 1.52 us -> 2.75 us
  other arithmetic: 1.85 us -> 1.31 us
    sub x0 -> x1, matrix products: none -> 1.11 us  [body(): weights = jnp.where(visible[None], jnp.exp(raw_affinity - top), 0.0)]
    reduce_sum x1 -> x0, other arithmetic: 0.52 us -> none  [attend(): new_sum = run_sum * factor + jnp.sum(weights, axis=2)]
where the time goes in v11:
time: 46.4 us; the launch traced here: 46.2 us
  starting transfers between devices  17.2 us (37%)
  waiting for transfers between devices  17 us (37%)
  Pallas kernels  5.92 us (13%)
  matrix products  2.75 us (6%)
  other arithmetic  1.31 us (3%)
  local copies, waits for them, and re-layouts  1.14 us (2%)
  between operations  0.93 us (2%)
    all_to_all x1, waiting for transfers between devices, body(): lax.all_to_all(both_local, 'ctx', split_axis=0, concat_axis=0, tiled=True)  13.8 us
    ppermute x7, starting transfers between devices, body(): lax.ppermute(send, 'ctx', [(i, (i + s) % n_ctx) for i in range(n_ctx)])  9.94 us
    all_to_all x1, starting transfers between devices, body(): lax.all_to_all(both_local, 'ctx', split_axis=0, concat_axis=0, tiled=True)  7.25 us
    pallas_call x1, Pallas kernels, shorten_both(): pl.pallas_call(functools.partial(shorten_kernel, per_t, nq), out_shape=ja...  3.19 us
    ppermute x7, waiting for transfers between devices, body(): lax.ppermute(send, 'ctx', [(i, (i + s) % n_ctx) for i in range(n_ctx)])  3.17 us
    pallas_call x1, Pallas kernels, up_and_mix(): pl.pallas_call(functools.partial(up_kernel_fn, copies_n, per_t, nq, qr),...  2.72 us
    dot_general x1, matrix products, body(): jnp.einsum('hqk,hkd->hqd', weights.astype(jnp.bfloat16), value_heads, pre...  1.21 us
    sub x1, matrix products, body(): weights = jnp.where(visible[None], jnp.exp(raw_affinity - top), 0.0)  1.11 us
  transfers between devices with their start and end apart: 8, of which 4 were waited for; matrix products, arithmetic and copies ran while one was open for 3% of the time, Pallas kernels for 0%

profile of v11, /device:TPU:0, one launch (start us, length us, event | category | flops | bytes accessed | tf_op | source)
XLA Modules:
  0.0 46.2 jit_solution(17564263544289773996)
XLA Ops:
  0.0 0.0 copy-start.1
  0.0 3.2 %shard_map.64 = bf16[8,272,128]{2,1,0:T(8,128)(2,1)} custom-call(f32[256,512]{1,0:T(8,128)} %x_ref.3, f32[8,4,512]{2,1,0:T(4,128)} %qk_ref.1, f32[8,4,512]{2,1,0:T(4,128)} %vk_ref.1), custom_call_target="tpu_custom_call" | custom-call | flops 205520896 | bytes 1179648 | tf_op jit(solution)/shard_map/pallas_call | solution.py:84
  3.2 7.3 %all-to-all-start = ((bf16[8,272,128]{2,1,0:T(8,128)(2,1)}), bf16[8,272,128]{2,1,0:T(8,128)(2,1)S(1)}, u32[]{:S(2)}, u32[]{:S(2)}) async-start(bf16[8,272,128]{2,1,0:T(8,128)(2,1)} %shard_map.64), calls=%async_computation | async-start | bytes 1114112 | tf_op jit(solution)/shard_map/all_to_all | solution.py:182
  11.2 0.1 iota_add_fusion
  11.3 0.1 add.143
  11.4 0.1 pad.4.clone
  11.5 0.0 copy-done.1
  11.5 0.4 fusion.7
  11.9 13.8 %all-to-all-done = bf16[8,272,128]{2,1,0:T(8,128)(2,1)S(1)} async-done(((bf16[8,272,128]{2,1,0:T(8,128)(2,1)}), bf16[8,272,128]{2,1,0:T(8,128)(2,1)S(1)}, u32[]{:S(2)}, u32[]{:S(2)}) %all-to-all-start) | async-done | bytes 557088 | tf_op jit(solution)/shard_map/all_to_all | solution.py:182
  25.7 0.1 broadcast_select_fusion
  25.9 0.4 fusion.24
  26.4 1.1 %fusion.23 = f32[2,512]{1,0:T(2,128)S(1)} fusion(f32[512]{0:T(512)S(1)} %log_multiply_fusion, pred[512,512]{0,1:T(8,128)(4,1)S(1)} %fusion.7, bf16[2,512,128]{2,1,0:T(8,128)(2,1)S(1)} %bitcast.79), kind=kOutput, calls=%fused_computation.55 | convolution fusion | flops 136839680 | bytes 530432 | tf_op jit(solution)/shard_map/sub | solution.py:266
  27.5 1.2 %fusion.2 = bf16[2,512,128]{2,1,0:T(8,128)(2,1)S(1)} fusion(bf16[2,512,128]{2,1,0:T(8,128)(2,1)S(1)} %bitcast.85, f32[2,512]{1,0:T(2,128)S(1)} %fusion.23, f32[2,512,512]{1,2,0:T(8,128)S(1)} %fusion.24, f32[512]{0:T(512)S(1)} %log_multiply_fusion, pred[512,512]{0,1:T(8,128)(4,1)S(1)} %fusion.7), kind=kOutput, calls=%fused_computation.5 | convolution fusion | flops 137102848 | bytes 2889728 | tf_op jit(solution)/shard_map/hqk,hkd->hqd/dot_general | solution.py:268
  28.8 0.1 maximum_maximum_fusion
  29.0 1.5 %collective-permute-start = (bf16[144,128]{1,0:T(8,128)(2,1)S(1)}, bf16[144,128]{1,0:T(8,128)(2,1)S(1)}, u32[]{:S(2)}, u32[]{:S(2)}) collective-permute-start(bf16[144,128]{1,0:T(8,128)(2,1)S(1)} %get-tuple-element.13), channel_id=1, source_target_pairs={{0,2},{2,4},{4,6},{6,8},{8,10},{10,12},{12,14},{14,0},{1,3},{3,5},... | collective-permute-start | bytes 110600 | tf_op jit(solution)/shard_map/ppermute | solution.py:294
  30.5 0.6 %pad_add_fusion.lim_ref = s32[3]{0:T(128)} fusion(s32[1]{0:T(128)} %constant.103.clone.1, s32[1]{0:T(128)} %bitcast.2, s32[1]{0:T(128)} %bitcast.1), kind=kLoop, calls=%fused_computation.45 | loop fusion | flops 6 | bytes 24 | tf_op jit(solution)/shard_map/stack | solution.py:300
  31.1 0.0 collective-permute-start.1
  31.1 1.7 %collective-permute-start.2 = (bf16[144,128]{1,0:T(8,128)(2,1)S(1)}, bf16[144,128]{1,0:T(8,128)(2,1)S(1)}, u32[]{:S(2)}, u32[]{:S(2)}) collective-permute-start(bf16[144,128]{1,0:T(8,128)(2,1)S(1)} %get-tuple-element.11), channel_id=1, source_target_pairs={{0,6},{2,8},{4,10},{6,12},{8,14},{10,0},{12,2},{14,4},{1,7},{3,9},... | collective-permute-start | bytes 110600 | tf_op jit(solution)/shard_map/ppermute | solution.py:294
  32.8 2.8 %collective-permute-start.3 = (bf16[144,128]{1,0:T(8,128)(2,1)S(1)}, bf16[144,128]{1,0:T(8,128)(2,1)S(1)}, u32[]{:S(2)}, u32[]{:S(2)}) collective-permute-start(bf16[144,128]{1,0:T(8,128)(2,1)S(1)} %get-tuple-element.10), channel_id=1, source_target_pairs={{0,8},{2,10},{4,12},{6,14},{8,0},{10,2},{12,4},{14,6},{1,9},{3,11}... | collective-permute-start | bytes 110600 | tf_op jit(solution)/shard_map/ppermute | solution.py:294
  35.6 1.3 %collective-permute-start.4 = (bf16[144,128]{1,0:T(8,128)(2,1)S(1)}, bf16[144,128]{1,0:T(8,128)(2,1)S(1)}, u32[]{:S(2)}, u32[]{:S(2)}) collective-permute-start(bf16[144,128]{1,0:T(8,128)(2,1)S(1)} %get-tuple-element.9), channel_id=1, source_target_pairs={{0,10},{2,12},{4,14},{6,0},{8,2},{10,4},{12,6},{14,8},{1,11},{3,13... | collective-permute-start | bytes 110600 | tf_op jit(solution)/shard_map/ppermute | solution.py:294
  36.9 0.0 collective-permute-done
  36.9 1.8 %collective-permute-start.5 = (bf16[144,128]{1,0:T(8,128)(2,1)S(1)}, bf16[144,128]{1,0:T(8,128)(2,1)S(1)}, u32[]{:S(2)}, u32[]{:S(2)}) collective-permute-start(bf16[144,128]{1,0:T(8,128)(2,1)S(1)} %get-tuple-element.8), channel_id=1, source_target_pairs={{0,12},{2,14},{4,0},{6,2},{8,4},{10,6},{12,8},{14,10},{1,13},{3,15... | collective-permute-start | bytes 110600 | tf_op jit(solution)/shard_map/ppermute | solution.py:294
  38.8 0.0 collective-permute-done.1
  38.8 0.8 %collective-permute-start.6 = (bf16[144,128]{1,0:T(8,128)(2,1)S(1)}, bf16[144,128]{1,0:T(8,128)(2,1)S(1)}, u32[]{:S(2)}, u32[]{:S(2)}) collective-permute-start(bf16[144,128]{1,0:T(8,128)(2,1)S(1)} %get-tuple-element.7), channel_id=1, source_target_pairs={{0,14},{2,0},{4,2},{6,4},{8,6},{10,8},{12,10},{14,12},{1,15},{3,1}... | collective-permute-start | bytes 110600 | tf_op jit(solution)/shard_map/ppermute | solution.py:294
  39.5 0.0 collective-permute-done.2
  39.6 0.0 collective-permute-done.3
  39.6 0.9 %collective-permute-done.4 = bf16[144,128]{1,0:T(8,128)(2,1)S(1)} collective-permute-done((bf16[144,128]{1,0:T(8,128)(2,1)S(1)}, bf16[144,128]{1,0:T(8,128)(2,1)S(1)}, u32[]{:S(2)}, u32[]{:S(2)}) %collective-permute-start.4) | collective-permute-done | bytes 36896 | tf_op jit(solution)/shard_map/ppermute | solution.py:294
  40.5 0.8 %collective-permute-done.5 = bf16[144,128]{1,0:T(8,128)(2,1)S(1)} collective-permute-done((bf16[144,128]{1,0:T(8,128)(2,1)S(1)}, bf16[144,128]{1,0:T(8,128)(2,1)S(1)}, u32[]{:S(2)}, u32[]{:S(2)}) %collective-permute-start.5) | collective-permute-done | bytes 36896 | tf_op jit(solution)/shard_map/ppermute | solution.py:294
  41.3 1.5 %collective-permute-done.6 = bf16[144,128]{1,0:T(8,128)(2,1)S(1)} collective-permute-done((bf16[144,128]{1,0:T(8,128)(2,1)S(1)}, bf16[144,128]{1,0:T(8,128)(2,1)S(1)}, u32[]{:S(2)}, u32[]{:S(2)}) %collective-permute-start.6) | collective-permute-done | bytes 36896 | tf_op jit(solution)/shard_map/ppermute | solution.py:294
  42.8 0.0 copy-start
  42.8 0.7 %copy-done = bf16[8,144,128]{2,1,0:T(8,128)(2,1)} copy-done((bf16[8,144,128]{2,1,0:T(8,128)(2,1)}, bf16[8,144,128]{2,1,0:T(8,128)(2,1)S(1)}, u32[]{:S(2)}) %copy-start) | copy-done | bytes 294936
  43.5 2.7 %shard_map.65 = f32[256,512]{1,0:T(8,128)} custom-call(s32[3]{0:T(128)} %pad_add_fusion.lim_ref, bf16[8,144,128]{2,1,0:T(8,128)(2,1)} %copy-done, f32[256,512]{1,0:T(8,128)} %x_ref.3, f32[8,4,512]{2,1,0:T(4,128)} %up_ref.1), custom_call_target="tpu_custom_call" | custom-call | flops 205520896 | bytes 1343488 | tf_op jit(solution)/shard_map/pallas_call | solution.py:147
  (25 shorter events, 0.3 us)
Async XLA Ops:
  0.0 11.5 %copy-start.1 = (s32[512]{0:T(512)S(1)}, s32[512]{0:T(512)}, u32[]{:S(2)}) copy-start(s32[512]{0:T(512)} %param.8) | copy-start | bytes 6148
  3.2 22.4 %all-to-all-start = ((bf16[8,272,128]{2,1,0:T(8,128)(2,1)}), bf16[8,272,128]{2,1,0:T(8,128)(2,1)S(1)}, u32[]{:S(2)}, u32[]{:S(2)}) async-start(bf16[8,272,128]{2,1,0:T(8,128)(2,1)} %shard_map.64), calls=%async_computation | async-start | bytes 1114112 | tf_op jit(solution)/shard_map/all_to_all | solution.py:182
  29.0 8.0 %collective-permute-start = (bf16[144,128]{1,0:T(8,128)(2,1)S(1)}, bf16[144,128]{1,0:T(8,128)(2,1)S(1)}, u32[]{:S(2)}, u32[]{:S(2)}) collective-permute-start(bf16[144,128]{1,0:T(8,128)(2,1)S(1)} %get-tuple-element.13), channel_id=1, source_target_pairs={{0,2},{2,4},{4,6},{6,8},{8,10},{10,12},{12,14},{14,0},{1,3},{3,5},... | collective-permute-start | bytes 110600 | tf_op jit(solution)/shard_map/ppermute | solution.py:294
  31.1 7.7 %collective-permute-start.1 = (bf16[144,128]{1,0:T(8,128)(2,1)S(1)}, bf16[144,128]{1,0:T(8,128)(2,1)S(1)}, u32[]{:S(2)}, u32[]{:S(2)}) collective-permute-start(bf16[144,128]{1,0:T(8,128)(2,1)S(1)} %get-tuple-element.12), channel_id=1, source_target_pairs={{0,4},{2,6},{4,8},{6,10},{8,12},{10,14},{12,0},{14,2},{1,5},{3,7},... | collective-permute-start | bytes 110600 | tf_op jit(solution)/shard_map/ppermute | solution.py:294
  31.1 8.4 %collective-permute-start.2 = (bf16[144,128]{1,0:T(8,128)(2,1)S(1)}, bf16[144,128]{1,0:T(8,128)(2,1)S(1)}, u32[]{:S(2)}, u32[]{:S(2)}) collective-permute-start(bf16[144,128]{1,0:T(8,128)(2,1)S(1)} %get-tuple-element.11), channel_id=1, source_target_pairs={{0,6},{2,8},{4,10},{6,12},{8,14},{10,0},{12,2},{14,4},{1,7},{3,9},... | collective-permute-start | bytes 110600 | tf_op jit(solution)/shard_map/ppermute | solution.py:294
  32.8 6.7 %collective-permute-start.3 = (bf16[144,128]{1,0:T(8,128)(2,1)S(1)}, bf16[144,128]{1,0:T(8,128)(2,1)S(1)}, u32[]{:S(2)}, u32[]{:S(2)}) collective-permute-start(bf16[144,128]{1,0:T(8,128)(2,1)S(1)} %get-tuple-element.10), channel_id=1, source_target_pairs={{0,8},{2,10},{4,12},{6,14},{8,0},{10,2},{12,4},{14,6},{1,9},{3,11}... | collective-permute-start | bytes 110600 | tf_op jit(solution)/shard_map/ppermute | solution.py:294
  35.6 4.9 %collective-permute-start.4 = (bf16[144,128]{1,0:T(8,128)(2,1)S(1)}, bf16[144,128]{1,0:T(8,128)(2,1)S(1)}, u32[]{:S(2)}, u32[]{:S(2)}) collective-permute-start(bf16[144,128]{1,0:T(8,128)(2,1)S(1)} %get-tuple-element.9), channel_id=1, source_target_pairs={{0,10},{2,12},{4,14},{6,0},{8,2},{10,4},{12,6},{14,8},{1,11},{3,13... | collective-permute-start | bytes 110600 | tf_op jit(solution)/shard_map/ppermute | solution.py:294
  36.9 4.3 %collective-permute-start.5 = (bf16[144,128]{1,0:T(8,128)(2,1)S(1)}, bf16[144,128]{1,0:T(8,128)(2,1)S(1)}, u32[]{:S(2)}, u32[]{:S(2)}) collective-permute-start(bf16[144,128]{1,0:T(8,128)(2,1)S(1)} %get-tuple-element.8), channel_id=1, source_target_pairs={{0,12},{2,14},{4,0},{6,2},{8,4},{10,6},{12,8},{14,10},{1,13},{3,15... | collective-permute-start | bytes 110600 | tf_op jit(solution)/shard_map/ppermute | solution.py:294
  38.8 4.0 %collective-permute-start.6 = (bf16[144,128]{1,0:T(8,128)(2,1)S(1)}, bf16[144,128]{1,0:T(8,128)(2,1)S(1)}, u32[]{:S(2)}, u32[]{:S(2)}) collective-permute-start(bf16[144,128]{1,0:T(8,128)(2,1)S(1)} %get-tuple-element.7), channel_id=1, source_target_pairs={{0,14},{2,0},{4,2},{6,4},{8,6},{10,8},{12,10},{14,12},{1,15},{3,1}... | collective-permute-start | bytes 110600 | tf_op jit(solution)/shard_map/ppermute | solution.py:294
  42.8 0.7 %copy-start = (bf16[8,144,128]{2,1,0:T(8,128)(2,1)}, bf16[8,144,128]{2,1,0:T(8,128)(2,1)S(1)}, u32[]{:S(2)}) copy-start(bf16[8,144,128]{2,1,0:T(8,128)(2,1)S(1)} %bitcast_dynamic-update-slice_fusion.ret_ref) | copy-start | bytes 884740

commit v12 on v4

--- a/solution.py
+++ b/solution.py
@@ -41,7 +41,7 @@
     return hi, lo
 
 
-def shorten_kernel(per_t, nq, x_ref, qk_ref, vk_ref, out_ref):
+def shorten_kernel(per_t, nq, x_ref, qk_ref, vk_ref, out_hbm, out_ref, sems):
     rows, channels = x_ref.shape
     lat = rows // STRIDE
     lanes = CHANNEL_WIDTH
@@ -53,9 +53,10 @@
     phase = [by_phase[s * lat : (s + 1) * lat] for s in range(STRIDE)]
     first_row = lax.broadcasted_iota(jnp.int32, (lat, channels), 0) == 0
     edge_row = lax.broadcasted_iota(jnp.int32, (16, lanes), 0)
-    edge = [jnp.zeros((16, lanes), jnp.float32) for _ in range(STRIDE * per_t)]
-    for which, kern_ref in enumerate((qk_ref, vk_ref)):
-        for t in range(STRIDE):
+    copies = []
+    for t in range(STRIDE):
+        edge = [jnp.zeros((16, lanes), jnp.float32) for _ in range(per_t)]
+        for which, kern_ref in enumerate((qk_ref, vk_ref)):
             own = phase[0] * kern_ref[STRIDE, pl.ds(t, 1), :]
             before = phase[0] * kern_ref[0, pl.ds(t, 1), :]
             for s in range(1, STRIDE):
@@ -67,13 +68,20 @@
             next_hi, next_lo = split_pair(before[lat - 1 : lat])
             for block in range(blocks):
                 lane = slice(block * lanes, (block + 1) * lanes)
-                g = t * per_t + block // nq
+                sub = block // nq
                 slot = which * nq + block % nq
-                out_ref[g, pl.ds(slot * lat, lat), :] = total[:, lane]
+                out_ref[t * per_t + sub, pl.ds(slot * lat, lat), :] = total[:, lane]
                 for e, piece in enumerate((own_hi, own_lo, next_hi, next_lo)):
-                    edge[g] = jnp.where(edge_row == e * 2 * nq + slot, piece[:, lane].astype(jnp.float32), edge[g])
-    for g in range(STRIDE * per_t):
-        out_ref[g, pl.ds(2 * nq * lat, 16), :] = edge[g].astype(jnp.bfloat16)
+                    edge[sub] = jnp.where(edge_row == e * 2 * nq + slot, piece[:, lane].astype(jnp.float32), edge[sub])
+        for sub in range(per_t):
+            g = t * per_t + sub
+            out_ref[g, pl.ds(2 * nq * lat, 16), :] = edge[sub].astype(jnp.bfloat16)
+        group = pl.ds(t * per_t, per_t)
+        copy = pltpu.make_async_copy(out_ref.at[group], out_hbm.at[group], sems.at[t])
+        copy.start()
+        copies.append(copy)
+    for copy in copies:
+        copy.wait()
 
 
 def shorten_both(byte_states, qk_kernel, value_kernel, groups_n, per_t, nq):
@@ -85,7 +93,11 @@
         functools.partial(shorten_kernel, per_t, nq),
         out_shape=jax.ShapeDtypeStruct((groups_n, kv_rows, CHANNEL_WIDTH), jnp.bfloat16),
         in_specs=[vmem] * 3,
-        out_specs=vmem,
+        out_specs=pl.BlockSpec(memory_space=pl.ANY),
+        scratch_shapes=[
+            pltpu.VMEM((groups_n, kv_rows, CHANNEL_WIDTH), jnp.bfloat16),
+            pltpu.SemaphoreType.DMA((STRIDE,)),
+        ],
         cost_estimate=pl.CostEstimate(
             flops=4 * KERNEL * rows * channels + 6 * rows * rows * channels,
             bytes_accessed=4 * rows * channels + 2 * KERNEL * STRIDE * channels * 4 + 2 * rows * channels * 2,
@@ -94,7 +106,9 @@
     )(byte_states, qk_kernel, value_kernel)
 
 
-def up_kernel_fn(copies_n, per_t, nq, qr, lim_ref, ret_ref, x_ref, up_ref, out_ref):
+def up_kernel_fn(copies_n, per_t, nq, qr, lim_ref, ret_ref, x_hbm, up_ref, out_ref, x_ref, sems):
+    x_copy = pltpu.make_async_copy(x_hbm, x_ref, sems.at[0])
+    x_copy.start()
     rows, channels = x_ref.shape
     lat = rows // STRIDE
     lanes = CHANNEL_WIDTH
@@ -130,6 +144,7 @@
     put = (put_col == (put_row % STRIDE) * lat + put_row // STRIDE).astype(jnp.bfloat16)
     branch = exact_rows(put, by_phase)
     byte_row = lax.broadcasted_iota(jnp.int32, (rows, channels), 0)
+    x_copy.wait()
     out_ref[...] = x_ref[...] + jnp.where(byte_row < lim_ref[0], branch, 0.0)
 
 
@@ -139,8 +154,9 @@
     return pl.pallas_call(
         functools.partial(up_kernel_fn, copies_n, per_t, nq, qr),
         out_shape=jax.ShapeDtypeStruct((rows, channels), jnp.float32),
-        in_specs=[pl.BlockSpec(memory_space=pltpu.SMEM), vmem, vmem, vmem],
+        in_specs=[pl.BlockSpec(memory_space=pltpu.SMEM), vmem, pl.BlockSpec(memory_space=pl.ANY), vmem],
         out_specs=vmem,
+        scratch_shapes=[pltpu.VMEM((rows, channels), jnp.float32), pltpu.SemaphoreType.DMA((1,))],
         cost_estimate=pl.CostEstimate(
             flops=4 * KERNEL * rows * channels + 6 * rows * rows * channels,
             bytes_accessed=8 * rows * channels + returned.size * 2,

time: 46.1 us -> 46.3 us (level)
  no operation moved by 1% of the time
where the time goes in v12:
time: 46.3 us; the launch traced here: 45.9 us
  waiting for transfers between devices  23.6 us (51%)
  starting transfers between devices  10.9 us (24%)
  Pallas kernels  6.04 us (13%)
  other arithmetic  1.96 us (4%)
  matrix products  1.52 us (3%)
  local copies, waits for them, and re-layouts  1.04 us (2%)
  between operations  0.82 us (2%)
    all_to_all x1, waiting for transfers between devices, body(): lax.all_to_all(both_local, 'ctx', split_axis=0, concat_axis=0, tiled=True)  13.9 us
    all_to_all x1, waiting for transfers between devices, body(): lax.all_to_all(outgoing, 'ctx', split_axis=0, concat_axis=0, tiled=True)  9.75 us
    all_to_all x1, starting transfers between devices, body(): lax.all_to_all(both_local, 'ctx', split_axis=0, concat_axis=0, tiled=True)  7.27 us
    all_to_all x1, starting transfers between devices, body(): lax.all_to_all(outgoing, 'ctx', split_axis=0, concat_axis=0, tiled=True)  3.64 us
    pallas_call x1, Pallas kernels, shorten_both(): pl.pallas_call(functools.partial(shorten_kernel, per_t, nq), out_shape=ja...  3.17 us
    pallas_call x1, Pallas kernels, up_and_mix(): pl.pallas_call(functools.partial(up_kernel_fn, copies_n, per_t, nq, qr),...  2.86 us
    dot_general x1, matrix products, attend(): jnp.einsum('hqk,hkd->hqd', weights.astype(jnp.bfloat16), value_block, pre...  0.98 us
  transfers between devices with their start and end apart: 2, of which 2 were waited for; matrix products, arithmetic and copies ran while one was open for 1% of the time, Pallas kernels for 0%

profile of v12, /device:TPU:0, one launch (start us, length us, event | category | flops | bytes accessed | tf_op | source)
XLA Modules:
  0.0 45.9 jit_solution(13552079417215440478)
XLA Ops:
  0.0 0.0 copy-start.1
  0.0 3.2 %shard_map.64 = bf16[8,272,128]{2,1,0:T(8,128)(2,1)} custom-call(f32[256,512]{1,0:T(8,128)} %x_hbm.1, f32[8,4,512]{2,1,0:T(4,128)} %qk_ref.1, f32[8,4,512]{2,1,0:T(4,128)} %vk_ref.1), custom_call_target="tpu_custom_call" | custom-call | flops 205520896 | bytes 1179648 | tf_op jit(solution)/shard_map/pallas_call | solution.py:92
  3.2 7.3 %all-to-all-start = ((bf16[8,272,128]{2,1,0:T(8,128)(2,1)}), bf16[8,272,128]{2,1,0:T(8,128)(2,1)S(1)}, u32[]{:S(2)}, u32[]{:S(2)}) async-start(bf16[8,272,128]{2,1,0:T(8,128)(2,1)} %shard_map.64), calls=%async_computation | async-start | bytes 1114112 | tf_op jit(solution)/shard_map/all_to_all | solution.py:190
  11.1 0.1 iota_add_fusion
  11.2 0.1 add.89
  11.3 0.1 pad.4.clone
  11.4 0.0 copy-done.1
  11.4 0.4 fusion.9
  11.8 13.9 %all-to-all-done = bf16[8,272,128]{2,1,0:T(8,128)(2,1)S(1)} async-done(((bf16[8,272,128]{2,1,0:T(8,128)(2,1)}), bf16[8,272,128]{2,1,0:T(8,128)(2,1)S(1)}, u32[]{:S(2)}, u32[]{:S(2)}) %all-to-all-start) | async-done | bytes 557088 | tf_op jit(solution)/shard_map/all_to_all | solution.py:190
  25.7 0.1 broadcast_select_fusion
  25.9 0.5 %select_reduce_fusion = (f32[2,512]{1,0:T(2,128)S(1)}, f32[2,512,512]{1,2,0:T(8,128)S(1)}) fusion(f32[512]{0:T(512)S(1)} %log_multiply_fusion, pred[512,512]{0,1:T(8,128)(4,1)S(1)} %fusion.9, bf16[2,512,128]{2,1,0:T(8,128)(2,1)S(1)} %bitcast.47), kind=kOutput, calls=%fused_computation.1 | convolution fusion | flops 135789568 | bytes 2627584 | tf_op jit(solution)/shard_map/while/body/eval_jaxpr/hqd,hkd->hqk/dot_general | solution.py:233
  26.5 0.5 %fusion = f32[2,512]{1,0:T(2,128)S(1)} fusion(f32[2,512,512]{1,2,0:T(8,128)S(1)} %get-tuple-element.75, f32[2,512]{1,0:T(2,128)S(1)} %broadcast_maximum_fusion, f32[512]{0:T(512)S(1)} %log_multiply_fusion, pred[512,512]{0,1:T(8,128)(4,1)S(1)} %fusion.9), kind=kLoop, calls=%fused_computation.2 | loop fusion | flops 2096128 | bytes 2369536 | tf_op jit(solution)/shard_map/while/body/eval_jaxpr/reduce_sum | solution.py:246
  27.1 1.0 %fusion.3 = bf16[2,512,128]{2,1,0:T(8,128)(2,1)S(1)} fusion(bf16[2,512,128]{2,1,0:T(8,128)(2,1)S(1)} %bitcast.53, f32[2,512,512]{1,2,0:T(8,128)S(1)} %get-tuple-element.75, f32[2,512]{1,0:T(2,128)S(1)} %broadcast_maximum_fusion, f32[512]{0:T(512)S(1)} %log_multiply_fusion, pred[512,512]{0,1:T(8,128)(4,1)S(1)} %fusion.9, f32[2,512]{1,0:T(2,128)S(1)} %get-tuple-element.73, ...), kind=kOutput, calls=%fused_computation.6 | convolution fusion | flops 136708096 | bytes 2897920 | tf_op jit(solution)/shard_map/while/body/eval_jaxpr/hqk,hkd->hqd/dot_general | solution.py:247
  28.1 0.8 %maximum_maximum_fusion = bf16[8,144,128]{2,1,0:T(8,128)(2,1)} fusion(bf16[8,4,128]{2,1,0:T(4,128)(2,1)S(1)} %bitcast.55, bf16[8,128,128]{2,1,0:T(8,128)(2,1)S(1)} %bitcast.50, bf16[144]{0:T(256)(128)(2,1)S(1)} %pad.4.clone), kind=kLoop, calls=%fused_computation.15 | loop fusion | flops 884736 | bytes 565536 | tf_op jit(solution)/shard_map/concatenate | solution.py:270
  29.0 3.6 %all-to-all-start.1 = ((bf16[8,144,128]{2,1,0:T(8,128)(2,1)}), bf16[8,144,128]{2,1,0:T(8,128)(2,1)S(1)}, u32[]{:S(2)}, u32[]{:S(2)}) async-start(bf16[8,144,128]{2,1,0:T(8,128)(2,1)} %maximum_maximum_fusion), calls=%async_computation.1 | async-start | bytes 589824 | tf_op jit(solution)/shard_map/all_to_all | solution.py:278
  32.6 9.8 %all-to-all-done.1.ret_ref = bf16[8,144,128]{2,1,0:T(8,128)(2,1)S(1)} async-done(((bf16[8,144,128]{2,1,0:T(8,128)(2,1)}), bf16[8,144,128]{2,1,0:T(8,128)(2,1)S(1)}, u32[]{:S(2)}, u32[]{:S(2)}) %all-to-all-start.1) | async-done | bytes 294944 | tf_op jit(solution)/shard_map/all_to_all | solution.py:278
  42.3 0.0 copy-start
  42.3 0.7 %copy-done = bf16[8,144,128]{2,1,0:T(8,128)(2,1)} copy-done((bf16[8,144,128]{2,1,0:T(8,128)(2,1)}, bf16[8,144,128]{2,1,0:T(8,128)(2,1)S(1)}, u32[]{:S(2)}) %copy-start) | copy-done | bytes 294936
  43.1 2.9 %shard_map.65 = f32[256,512]{1,0:T(8,128)} custom-call(s32[1]{0:T(128)} %bitcast.1.lim_ref, bf16[8,144,128]{2,1,0:T(8,128)(2,1)} %copy-done, f32[256,512]{1,0:T(8,128)} %x_hbm.1, f32[8,4,512]{2,1,0:T(4,128)} %up_ref.1), custom_call_target="tpu_custom_call" | custom-call | flops 205520896 | bytes 1343488 | tf_op jit(solution)/shard_map/pallas_call | solution.py:154
  (19 shorter events, 0.2 us)
Async XLA Ops:
  0.0 11.4 %copy-start.1 = (s32[512]{0:T(512)S(1)}, s32[512]{0:T(512)}, u32[]{:S(2)}) copy-start(s32[512]{0:T(512)} %param.8) | copy-start | bytes 6148
  3.2 22.5 %all-to-all-start = ((bf16[8,272,128]{2,1,0:T(8,128)(2,1)}), bf16[8,272,128]{2,1,0:T(8,128)(2,1)S(1)}, u32[]{:S(2)}, u32[]{:S(2)}) async-start(bf16[8,272,128]{2,1,0:T(8,128)(2,1)} %shard_map.64), calls=%async_computation | async-start | bytes 1114112 | tf_op jit(solution)/shard_map/all_to_all | solution.py:190
  29.0 13.4 %all-to-all-start.1 = ((bf16[8,144,128]{2,1,0:T(8,128)(2,1)}), bf16[8,144,128]{2,1,0:T(8,128)(2,1)S(1)}, u32[]{:S(2)}, u32[]{:S(2)}) async-start(bf16[8,144,128]{2,1,0:T(8,128)(2,1)} %maximum_maximum_fusion), calls=%async_computation.1 | async-start | bytes 589824 | tf_op jit(solution)/shard_map/all_to_all | solution.py:278
  42.3 0.7 %copy-start = (bf16[8,144,128]{2,1,0:T(8,128)(2,1)}, bf16[8,144,128]{2,1,0:T(8,128)(2,1)S(1)}, u32[]{:S(2)}) copy-start(bf16[8,144,128]{2,1,0:T(8,128)(2,1)S(1)} %all-to-all-done.1.ret_ref) | copy-start | bytes 884740

commit v13 on v4

--- a/solution.py
+++ b/solution.py
@@ -52,8 +52,9 @@
     by_phase = exact_rows(pick, x_ref[...])
     phase = [by_phase[s * lat : (s + 1) * lat] for s in range(STRIDE)]
     first_row = lax.broadcasted_iota(jnp.int32, (lat, channels), 0) == 0
-    edge_row = lax.broadcasted_iota(jnp.int32, (16, lanes), 0)
-    edge = [jnp.zeros((16, lanes), jnp.float32) for _ in range(STRIDE * per_t)]
+    edge_rows = -(-6 * nq // 8) * 8
+    edge_row = lax.broadcasted_iota(jnp.int32, (edge_rows, lanes), 0)
+    edge = [jnp.zeros((edge_rows, lanes), jnp.float32) for _ in range(STRIDE * per_t)]
     for which, kern_ref in enumerate((qk_ref, vk_ref)):
         for t in range(STRIDE):
             own = phase[0] * kern_ref[STRIDE, pl.ds(t, 1), :]
@@ -70,16 +71,16 @@
                 g = t * per_t + block // nq
                 slot = which * nq + block % nq
                 out_ref[g, pl.ds(slot * lat, lat), :] = total[:, lane]
-                for e, piece in enumerate((own_hi, own_lo, next_hi, next_lo)):
+                for e, piece in enumerate((own_lo, next_hi, next_lo)):
                     edge[g] = jnp.where(edge_row == e * 2 * nq + slot, piece[:, lane].astype(jnp.float32), edge[g])
     for g in range(STRIDE * per_t):
-        out_ref[g, pl.ds(2 * nq * lat, 16), :] = edge[g].astype(jnp.bfloat16)
+        out_ref[g, pl.ds(2 * nq * lat, 6 * nq), :] = edge[g][: 6 * nq].astype(jnp.bfloat16)
 
 
 def shorten_both(byte_states, qk_kernel, value_kernel, groups_n, per_t, nq):
     rows, channels = byte_states.shape
     lat = rows // STRIDE
-    kv_rows = 2 * nq * lat + 16
+    kv_rows = 2 * nq * lat + 6 * nq
     vmem = pl.BlockSpec(memory_space=pltpu.VMEM)
     return pl.pallas_call(
         functools.partial(shorten_kernel, per_t, nq),
@@ -173,10 +174,10 @@
         ).reshape(n_ctx, kv_rows, CHANNEL_WIDTH)
     both_all = lax.all_to_all(both_local, "ctx", split_axis=0, concat_axis=0, tiled=True)
     main_kv = both_all[:, : 2 * nq * lat_dev].reshape(n_ctx, 2 * nq, lat_dev, CHANNEL_WIDTH)
-    edge = both_all[:, 2 * nq * lat_dev : 2 * nq * lat_dev + 8 * nq].astype(jnp.float32)
-    edge = edge.reshape(n_ctx, 4, 2 * nq, CHANNEL_WIDTH)
-    own_first = edge[:, 0] + edge[:, 1]
-    from_before = edge[:, 2] + edge[:, 3]
+    edge = both_all[:, 2 * nq * lat_dev : 2 * nq * lat_dev + 6 * nq].astype(jnp.float32)
+    edge = edge.reshape(n_ctx, 3, 2 * nq, CHANNEL_WIDTH)
+    own_first = main_kv[:, :, 0].astype(jnp.float32) + edge[:, 0]
+    from_before = edge[:, 1] + edge[:, 2]
     from_before = jnp.concatenate([jnp.zeros_like(from_before[:1]), from_before[:-1]], 0)
     first_rows = (own_first + from_before).astype(jnp.bfloat16)
     at_first = lax.broadcasted_iota(jnp.int32, main_kv.shape, 2) == 0
@@ -250,7 +251,7 @@
     )
     main_rows = nq * query_rows
     used_rows = main_rows + 2 * nq
-    ret_rows = -(-used_rows // 16) * 16
+    ret_rows = used_rows
     outgoing = jnp.concatenate(
         [
             attended.reshape(n_ctx, main_rows, CHANNEL_WIDTH),

time: 46.1 us -> 45.7 us (level)
  no operation moved by 1% of the time
where the time goes in v13:
time: 45.7 us; the launch traced here: 45.3 us
  waiting for transfers between devices  23.4 us (51%)
  starting transfers between devices  10.9 us (24%)
  Pallas kernels  5.87 us (13%)
  other arithmetic  1.84 us (4%)
  matrix products  1.53 us (3%)
  local copies, waits for them, and re-layouts  0.99 us (2%)
  between operations  0.83 us (2%)
    all_to_all x1, waiting for transfers between devices, body(): lax.all_to_all(both_local, 'ctx', split_axis=0, concat_axis=0, tiled=True)  14 us
    all_to_all x1, waiting for transfers between devices, body(): lax.all_to_all(outgoing, 'ctx', split_axis=0, concat_axis=0, tiled=True)  9.4 us
    all_to_all x1, starting transfers between devices, body(): lax.all_to_all(both_local, 'ctx', split_axis=0, concat_axis=0, tiled=True)  7.26 us
    all_to_all x1, starting transfers between devices, body(): lax.all_to_all(outgoing, 'ctx', split_axis=0, concat_axis=0, tiled=True)  3.64 us
    pallas_call x1, Pallas kernels, shorten_both(): pl.pallas_call(functools.partial(shorten_kernel, per_t, nq), out_shape=ja...  3.17 us
    pallas_call x1, Pallas kernels, up_and_mix(): pl.pallas_call(functools.partial(up_kernel_fn, copies_n, per_t, nq, qr),...  2.69 us
    dot_general x1, matrix products, attend(): jnp.einsum('hqk,hkd->hqd', weights.astype(jnp.bfloat16), value_block, pre...  0.98 us
  transfers between devices with their start and end apart: 2, of which 2 were waited for; matrix products, arithmetic and copies ran while one was open for 1% of the time, Pallas kernels for 0%

profile of v13, /device:TPU:0, one launch (start us, length us, event | category | flops | bytes accessed | tf_op | source)
XLA Modules:
  0.0 45.3 jit_solution(1523973430283542385)
XLA Ops:
  0.0 0.0 copy-start.1
  0.0 3.2 %shard_map.64 = bf16[8,268,128]{2,1,0:T(8,128)(2,1)} custom-call(f32[256,512]{1,0:T(8,128)} %x_ref.3, f32[8,4,512]{2,1,0:T(4,128)} %qk_ref.1, f32[8,4,512]{2,1,0:T(4,128)} %vk_ref.1), custom_call_target="tpu_custom_call" | custom-call | flops 205520896 | bytes 1179648 | tf_op jit(solution)/shard_map/pallas_call | solution.py:85
  3.2 7.3 %all-to-all-start = ((bf16[8,268,128]{2,1,0:T(8,128)(2,1)}), bf16[8,268,128]{2,1,0:T(8,128)(2,1)S(1)}, u32[]{:S(2)}, u32[]{:S(2)}) async-start(bf16[8,268,128]{2,1,0:T(8,128)(2,1)} %shard_map.64), calls=%async_computation | async-start | bytes 1114112 | tf_op jit(solution)/shard_map/all_to_all | solution.py:175
  11.1 0.1 iota_add_fusion
  11.2 0.1 add.86
  11.3 0.0 copy-done.1
  11.3 0.4 fusion.9
  11.7 14.0 %all-to-all-done = bf16[8,268,128]{2,1,0:T(8,128)(2,1)S(1)} async-done(((bf16[8,268,128]{2,1,0:T(8,128)(2,1)}), bf16[8,268,128]{2,1,0:T(8,128)(2,1)S(1)}, u32[]{:S(2)}, u32[]{:S(2)}) %all-to-all-start) | async-done | bytes 548896 | tf_op jit(solution)/shard_map/all_to_all | solution.py:175
  25.8 0.1 broadcast_select_fusion
  26.0 0.5 %select_reduce_fusion = (f32[2,512]{1,0:T(2,128)S(1)}, f32[2,512,512]{1,2,0:T(8,128)S(1)}) fusion(f32[512]{0:T(512)S(1)} %log_multiply_fusion, pred[512,512]{0,1:T(8,128)(4,1)S(1)} %fusion.9, bf16[2,512,128]{2,1,0:T(8,128)(2,1)S(1)} %bitcast.39), kind=kOutput, calls=%fused_computation.1 | convolution fusion | flops 135789568 | bytes 2627584 | tf_op jit(solution)/shard_map/while/body/eval_jaxpr/hqd,hkd->hqk/dot_general | solution.py:218
  26.6 0.5 %fusion = f32[2,512]{1,0:T(2,128)S(1)} fusion(f32[2,512,512]{1,2,0:T(8,128)S(1)} %get-tuple-element.75, f32[2,512]{1,0:T(2,128)S(1)} %broadcast_maximum_fusion, f32[512]{0:T(512)S(1)} %log_multiply_fusion, pred[512,512]{0,1:T(8,128)(4,1)S(1)} %fusion.9), kind=kLoop, calls=%fused_computation.2 | loop fusion | flops 2096128 | bytes 2369536 | tf_op jit(solution)/shard_map/while/body/eval_jaxpr/reduce_sum | solution.py:231
  27.1 1.0 %fusion.3 = bf16[2,512,128]{2,1,0:T(8,128)(2,1)S(1)} fusion(bf16[2,512,128]{2,1,0:T(8,128)(2,1)S(1)} %bitcast.44, f32[2,512,512]{1,2,0:T(8,128)S(1)} %get-tuple-element.75, f32[2,512]{1,0:T(2,128)S(1)} %broadcast_maximum_fusion, f32[512]{0:T(512)S(1)} %log_multiply_fusion, pred[512,512]{0,1:T(8,128)(4,1)S(1)} %fusion.9, f32[2,512]{1,0:T(2,128)S(1)} %get-tuple-element.73, ...), kind=kOutput, calls=%fused_computation.6 | convolution fusion | flops 136708096 | bytes 2897920 | tf_op jit(solution)/shard_map/while/body/eval_jaxpr/hqk,hkd->hqd/dot_general | solution.py:232
  28.2 0.7 %pad_maximum_fusion = bf16[8,132,128]{2,1,0:T(8,128)(2,1)} fusion(bf16[8,4,128]{2,1,0:T(4,128)(2,1)S(1)} %bitcast.48, bf16[8,128,128]{2,1,0:T(8,128)(2,1)S(1)} %bitcast.43), kind=kLoop, calls=%fused_computation.15 | loop fusion | flops 540672 | bytes 540672 | tf_op jit(solution)/shard_map/concatenate | solution.py:255
  28.9 3.6 %all-to-all-start.1 = ((bf16[8,132,128]{2,1,0:T(8,128)(2,1)}), bf16[8,132,128]{2,1,0:T(8,128)(2,1)S(1)}, u32[]{:S(2)}, u32[]{:S(2)}) async-start(bf16[8,132,128]{2,1,0:T(8,128)(2,1)} %pad_maximum_fusion), calls=%async_computation.1 | async-start | bytes 557056 | tf_op jit(solution)/shard_map/all_to_all | solution.py:263
  32.5 9.4 %all-to-all-done.1.ret_ref = bf16[8,132,128]{2,1,0:T(8,128)(2,1)S(1)} async-done(((bf16[8,132,128]{2,1,0:T(8,128)(2,1)}), bf16[8,132,128]{2,1,0:T(8,128)(2,1)S(1)}, u32[]{:S(2)}, u32[]{:S(2)}) %all-to-all-start.1) | async-done | bytes 270368 | tf_op jit(solution)/shard_map/all_to_all | solution.py:263
  41.9 0.0 copy-start
  41.9 0.7 %copy-done = bf16[8,132,128]{2,1,0:T(8,128)(2,1)} copy-done((bf16[8,132,128]{2,1,0:T(8,128)(2,1)}, bf16[8,132,128]{2,1,0:T(8,128)(2,1)S(1)}, u32[]{:S(2)}) %copy-start) | copy-done | bytes 270360
  42.6 2.7 %shard_map.65 = f32[256,512]{1,0:T(8,128)} custom-call(s32[1]{0:T(128)} %bitcast.1.lim_ref, bf16[8,132,128]{2,1,0:T(8,128)(2,1)} %copy-done, f32[256,512]{1,0:T(8,128)} %x_ref.3, f32[8,4,512]{2,1,0:T(4,128)} %up_ref.1), custom_call_target="tpu_custom_call" | custom-call | flops 205520896 | bytes 1318912 | tf_op jit(solution)/shard_map/pallas_call | solution.py:140
  (20 shorter events, 0.3 us)
Async XLA Ops:
  0.0 11.3 %copy-start.1 = (s32[512]{0:T(512)S(1)}, s32[512]{0:T(512)}, u32[]{:S(2)}) copy-start(s32[512]{0:T(512)} %param.8) | copy-start | bytes 6148
  3.2 22.4 %all-to-all-start = ((bf16[8,268,128]{2,1,0:T(8,128)(2,1)}), bf16[8,268,128]{2,1,0:T(8,128)(2,1)S(1)}, u32[]{:S(2)}, u32[]{:S(2)}) async-start(bf16[8,268,128]{2,1,0:T(8,128)(2,1)} %shard_map.64), calls=%async_computation | async-start | bytes 1114112 | tf_op jit(solution)/shard_map/all_to_all | solution.py:175
  28.9 13.0 %all-to-all-start.1 = ((bf16[8,132,128]{2,1,0:T(8,128)(2,1)}), bf16[8,132,128]{2,1,0:T(8,128)(2,1)S(1)}, u32[]{:S(2)}, u32[]{:S(2)}) async-start(bf16[8,132,128]{2,1,0:T(8,128)(2,1)} %pad_maximum_fusion), calls=%async_computation.1 | async-start | bytes 557056 | tf_op jit(solution)/shard_map/all_to_all | solution.py:263
  41.9 0.7 %copy-start = (bf16[8,132,128]{2,1,0:T(8,128)(2,1)}, bf16[8,132,128]{2,1,0:T(8,128)(2,1)S(1)}, u32[]{:S(2)}) copy-start(bf16[8,132,128]{2,1,0:T(8,128)(2,1)S(1)} %all-to-all-done.1.ret_ref) | copy-start | bytes 811012

commit v14 on v13

--- a/solution.py
+++ b/solution.py
@@ -144,7 +144,7 @@
         out_specs=vmem,
         cost_estimate=pl.CostEstimate(
             flops=4 * KERNEL * rows * channels + 6 * rows * rows * channels,
-            bytes_accessed=8 * rows * channels + returned.size * 2,
+            bytes_accessed=8 * rows * channels + returned.size * 4,
             transcendentals=0,
         ),
     )(limit, returned, byte_states, up_kernel)
@@ -262,7 +262,9 @@
     )
     returned = lax.all_to_all(outgoing, "ctx", split_axis=0, concat_axis=0, tiled=True)
     limit = (doc_length[0] - device * rows_here).reshape(1).astype(jnp.int32)
-    return up_and_mix(limit, returned, byte_states, up_kernel, copies_n, per_t, nq, query_rows)
+    return up_and_mix(
+        limit, returned.astype(jnp.float32), byte_states, up_kernel, copies_n, per_t, nq, query_rows
+    )
 
 def solution(mesh):
     return jax.shard_map(

time: 45.7 us -> 45.9 us (level)
  other arithmetic: 1.84 us -> 2.68 us
  local copies, waits for them, and re-layouts: 0.99 us -> 0.29 us
    convert_element_type x0 -> x1, other arithmetic: none -> 0.84 us  [body(): returned.astype(jnp.float32)]
    unnamed x4 -> x2, local copies, waits for them, and re-layouts: 0.71 us -> 0.01 us
where the time goes in v14:
time: 45.9 us; the launch traced here: 45.5 us
  waiting for transfers between devices  23.4 us (51%)
  starting transfers between devices  10.9 us (24%)
  Pallas kernels  5.95 us (13%)
  other arithmetic  2.68 us (6%)
  matrix products  1.52 us (3%)
  between operations  0.83 us (2%)
    all_to_all x1, waiting for transfers between devices, body(): lax.all_to_all(both_local, 'ctx', split_axis=0, concat_axis=0, tiled=True)  14 us
    all_to_all x1, waiting for transfers between devices, body(): lax.all_to_all(outgoing, 'ctx', split_axis=0, concat_axis=0, tiled=True)  9.4 us
    all_to_all x1, starting transfers between devices, body(): lax.all_to_all(both_local, 'ctx', split_axis=0, concat_axis=0, tiled=True)  7.26 us
    all_to_all x1, starting transfers between devices, body(): lax.all_to_all(outgoing, 'ctx', split_axis=0, concat_axis=0, tiled=True)  3.64 us
    pallas_call x1, Pallas kernels, shorten_both(): pl.pallas_call(functools.partial(shorten_kernel, per_t, nq), out_shape=ja...  3.17 us
    pallas_call x1, Pallas kernels, up_and_mix(): pl.pallas_call(functools.partial(up_kernel_fn, copies_n, per_t, nq, qr),...  2.78 us
    dot_general x1, matrix products, attend(): jnp.einsum('hqk,hkd->hqd', weights.astype(jnp.bfloat16), value_block, pre...  0.98 us
  transfers between devices with their start and end apart: 2, of which 2 were waited for; matrix products, arithmetic and copies ran while one was open for 1% of the time, Pallas kernels for 0%

profile of v14, /device:TPU:0, one launch (start us, length us, event | category | flops | bytes accessed | tf_op | source)
XLA Modules:
  0.0 45.5 jit_solution(4066725487916081849)
XLA Ops:
  0.0 0.0 copy-start
  0.0 3.2 %shard_map.64 = bf16[8,268,128]{2,1,0:T(8,128)(2,1)} custom-call(f32[256,512]{1,0:T(8,128)} %x_ref.3, f32[8,4,512]{2,1,0:T(4,128)} %qk_ref.1, f32[8,4,512]{2,1,0:T(4,128)} %vk_ref.1), custom_call_target="tpu_custom_call" | custom-call | flops 205520896 | bytes 1179648 | tf_op jit(solution)/shard_map/pallas_call | solution.py:85
  3.2 7.3 %all-to-all-start = ((bf16[8,268,128]{2,1,0:T(8,128)(2,1)}), bf16[8,268,128]{2,1,0:T(8,128)(2,1)S(1)}, u32[]{:S(2)}, u32[]{:S(2)}) async-start(bf16[8,268,128]{2,1,0:T(8,128)(2,1)} %shard_map.64), calls=%async_computation | async-start | bytes 1114112 | tf_op jit(solution)/shard_map/all_to_all | solution.py:175
  11.1 0.1 iota_add_fusion
  11.2 0.1 add.86
  11.3 0.0 copy-done
  11.3 0.4 fusion.9
  11.6 14.0 %all-to-all-done = bf16[8,268,128]{2,1,0:T(8,128)(2,1)S(1)} async-done(((bf16[8,268,128]{2,1,0:T(8,128)(2,1)}), bf16[8,268,128]{2,1,0:T(8,128)(2,1)S(1)}, u32[]{:S(2)}, u32[]{:S(2)}) %all-to-all-start) | async-done | bytes 548896 | tf_op jit(solution)/shard_map/all_to_all | solution.py:175
  25.8 0.1 broadcast_select_fusion
  26.0 0.5 %select_reduce_fusion = (f32[2,512]{1,0:T(2,128)S(1)}, f32[2,512,512]{1,2,0:T(8,128)S(1)}) fusion(f32[512]{0:T(512)S(1)} %log_multiply_fusion, pred[512,512]{0,1:T(8,128)(4,1)S(1)} %fusion.9, bf16[2,512,128]{2,1,0:T(8,128)(2,1)S(1)} %bitcast.39), kind=kOutput, calls=%fused_computation.1 | convolution fusion | flops 135789568 | bytes 2627584 | tf_op jit(solution)/shard_map/while/body/eval_jaxpr/hqd,hkd->hqk/dot_general | solution.py:218
  26.6 0.5 %fusion = f32[2,512]{1,0:T(2,128)S(1)} fusion(f32[2,512,512]{1,2,0:T(8,128)S(1)} %get-tuple-element.75, f32[2,512]{1,0:T(2,128)S(1)} %broadcast_maximum_fusion, f32[512]{0:T(512)S(1)} %log_multiply_fusion, pred[512,512]{0,1:T(8,128)(4,1)S(1)} %fusion.9), kind=kLoop, calls=%fused_computation.2 | loop fusion | flops 2096128 | bytes 2369536 | tf_op jit(solution)/shard_map/while/body/eval_jaxpr/reduce_sum | solution.py:231
  27.1 1.0 %fusion.3 = bf16[2,512,128]{2,1,0:T(8,128)(2,1)S(1)} fusion(bf16[2,512,128]{2,1,0:T(8,128)(2,1)S(1)} %bitcast.44, f32[2,512,512]{1,2,0:T(8,128)S(1)} %get-tuple-element.75, f32[2,512]{1,0:T(2,128)S(1)} %broadcast_maximum_fusion, f32[512]{0:T(512)S(1)} %log_multiply_fusion, pred[512,512]{0,1:T(8,128)(4,1)S(1)} %fusion.9, f32[2,512]{1,0:T(2,128)S(1)} %get-tuple-element.73, ...), kind=kOutput, calls=%fused_computation.6 | convolution fusion | flops 136708096 | bytes 2897920 | tf_op jit(solution)/shard_map/while/body/eval_jaxpr/hqk,hkd->hqd/dot_general | solution.py:232
  28.1 0.7 %pad_maximum_fusion = bf16[8,132,128]{2,1,0:T(8,128)(2,1)} fusion(bf16[8,4,128]{2,1,0:T(4,128)(2,1)S(1)} %bitcast.48, bf16[8,128,128]{2,1,0:T(8,128)(2,1)S(1)} %bitcast.43), kind=kLoop, calls=%fused_computation.15 | loop fusion | flops 540672 | bytes 540672 | tf_op jit(solution)/shard_map/concatenate | solution.py:255
  28.9 3.6 %all-to-all-start.1 = ((bf16[8,132,128]{2,1,0:T(8,128)(2,1)}), bf16[8,132,128]{2,1,0:T(8,128)(2,1)S(1)}, u32[]{:S(2)}, u32[]{:S(2)}) async-start(bf16[8,132,128]{2,1,0:T(8,128)(2,1)} %pad_maximum_fusion), calls=%async_computation.1 | async-start | bytes 557056 | tf_op jit(solution)/shard_map/all_to_all | solution.py:263
  32.5 9.4 %all-to-all-done.1 = bf16[8,132,128]{2,1,0:T(8,128)(2,1)S(1)} async-done(((bf16[8,132,128]{2,1,0:T(8,128)(2,1)}), bf16[8,132,128]{2,1,0:T(8,128)(2,1)S(1)}, u32[]{:S(2)}, u32[]{:S(2)}) %all-to-all-start.1) | async-done | bytes 270368 | tf_op jit(solution)/shard_map/all_to_all | solution.py:263
  41.9 0.8 %convert_element_type.30.ret_ref = f32[8,132,128]{2,1,0:T(8,128)} convert(bf16[8,132,128]{2,1,0:T(8,128)(2,1)S(1)} %all-to-all-done.1) | non-fusion elementwise | flops 135168 | bytes 811008 | tf_op jit(solution)/shard_map/convert_element_type | solution.py:266
  42.8 2.8 %shard_map.65 = f32[256,512]{1,0:T(8,128)} custom-call(s32[1]{0:T(128)} %bitcast.1.lim_ref, f32[8,132,128]{2,1,0:T(8,128)} %convert_element_type.30.ret_ref, f32[256,512]{1,0:T(8,128)} %x_ref.3, f32[8,4,512]{2,1,0:T(4,128)} %up_ref.1), custom_call_target="tpu_custom_call" | custom-call | flops 205520896 | bytes 1589248 | tf_op jit(solution)/shard_map/pallas_call | solution.py:140
  (20 shorter events, 0.3 us)
Async XLA Ops:
  0.0 11.3 %copy-start = (s32[512]{0:T(512)S(1)}, s32[512]{0:T(512)}, u32[]{:S(2)}) copy-start(s32[512]{0:T(512)} %param.8) | copy-start | bytes 6148
  3.2 22.4 %all-to-all-start = ((bf16[8,268,128]{2,1,0:T(8,128)(2,1)}), bf16[8,268,128]{2,1,0:T(8,128)(2,1)S(1)}, u32[]{:S(2)}, u32[]{:S(2)}) async-start(bf16[8,268,128]{2,1,0:T(8,128)(2,1)} %shard_map.64), calls=%async_computation | async-start | bytes 1114112 | tf_op jit(solution)/shard_map/all_to_all | solution.py:175
  28.9 13.0 %all-to-all-start.1 = ((bf16[8,132,128]{2,1,0:T(8,128)(2,1)}), bf16[8,132,128]{2,1,0:T(8,128)(2,1)S(1)}, u32[]{:S(2)}, u32[]{:S(2)}) async-start(bf16[8,132,128]{2,1,0:T(8,128)(2,1)} %pad_maximum_fusion), calls=%async_computation.1 | async-start | bytes 557056 | tf_op jit(solution)/shard_map/all_to_all | solution.py:263

commit v15 on v13

--- a/solution.py
+++ b/solution.py
@@ -41,7 +41,7 @@
     return hi, lo
 
 
-def shorten_kernel(per_t, nq, x_ref, qk_ref, vk_ref, out_ref):
+def shorten_kernel(per_t, nq, x_ref, qk_ref, vk_ref, out_ref, taps_ref):
     rows, channels = x_ref.shape
     lat = rows // STRIDE
     lanes = CHANNEL_WIDTH
@@ -50,27 +50,50 @@
     pick_col = lax.broadcasted_iota(jnp.int32, (rows, rows), 1)
     pick = (pick_col == (pick_row % lat) * STRIDE + pick_row // lat).astype(jnp.bfloat16)
     by_phase = exact_rows(pick, x_ref[...])
-    phase = [by_phase[s * lat : (s + 1) * lat] for s in range(STRIDE)]
     first_row = lax.broadcasted_iota(jnp.int32, (lat, channels), 0) == 0
+    phase = []
+    for s in range(STRIDE):
+        current = by_phase[s * lat : (s + 1) * lat]
+        phase.append(current)
+        taps_ref[STRIDE + s] = current
+        taps_ref[s] = jnp.where(first_row, 0.0, pltpu.roll(current, 1, 0))
+    kerns = (qk_ref, vk_ref)
+    chunk = 16
+
+    def rows_of(r, carry):
+        start = pl.multiple_of(r * chunk, chunk)
+        for block in range(blocks):
+            lane = pl.ds(block * lanes, lanes)
+            taps = [taps_ref[k, pl.ds(start, chunk), lane] for k in range(KERNEL)]
+            for which, kern_ref in enumerate(kerns):
+                slot = which * nq + block % nq
+                for t in range(STRIDE):
+                    total = taps[0] * kern_ref[0, pl.ds(t, 1), lane]
+                    for k in range(1, KERNEL):
+                        total = total + taps[k] * kern_ref[k, pl.ds(t, 1), lane]
+                    g = t * per_t + block // nq
+                    out_ref[g, pl.ds(pl.multiple_of(slot * lat + start, chunk), chunk), :] = total.astype(
+                        jnp.bfloat16
+                    )
+        return carry
+
+    lax.fori_loop(0, lat // chunk, rows_of, 0)
     edge_rows = -(-6 * nq // 8) * 8
     edge_row = lax.broadcasted_iota(jnp.int32, (edge_rows, lanes), 0)
     edge = [jnp.zeros((edge_rows, lanes), jnp.float32) for _ in range(STRIDE * per_t)]
-    for which, kern_ref in enumerate((qk_ref, vk_ref)):
+    for which, kern_ref in enumerate(kerns):
         for t in range(STRIDE):
-            own = phase[0] * kern_ref[STRIDE, pl.ds(t, 1), :]
-            before = phase[0] * kern_ref[0, pl.ds(t, 1), :]
+            own = phase[0][0:1] * kern_ref[STRIDE, pl.ds(t, 1), :]
+            before = phase[0][lat - 1 : lat] * kern_ref[0, pl.ds(t, 1), :]
             for s in range(1, STRIDE):
-                own = own + phase[s] * kern_ref[STRIDE + s, pl.ds(t, 1), :]
-                before = before + phase[s] * kern_ref[s, pl.ds(t, 1), :]
-            total = own + jnp.where(first_row, 0.0, pltpu.roll(before, 1, 0))
-            total = total.astype(jnp.bfloat16)
-            own_hi, own_lo = split_pair(own[0:1])
-            next_hi, next_lo = split_pair(before[lat - 1 : lat])
+                own = own + phase[s][0:1] * kern_ref[STRIDE + s, pl.ds(t, 1), :]
+                before = before + phase[s][lat - 1 : lat] * kern_ref[s, pl.ds(t, 1), :]
+            own_hi, own_lo = split_pair(own)
+            next_hi, next_lo = split_pair(before)
             for block in range(blocks):
                 lane = slice(block * lanes, (block + 1) * lanes)
                 g = t * per_t + block // nq
                 slot = which * nq + block % nq
-                out_ref[g, pl.ds(slot * lat, lat), :] = total[:, lane]
                 for e, piece in enumerate((own_lo, next_hi, next_lo)):
                     edge[g] = jnp.where(edge_row == e * 2 * nq + slot, piece[:, lane].astype(jnp.float32), edge[g])
     for g in range(STRIDE * per_t):
@@ -87,6 +110,7 @@
         out_shape=jax.ShapeDtypeStruct((groups_n, kv_rows, CHANNEL_WIDTH), jnp.bfloat16),
         in_specs=[vmem] * 3,
         out_specs=vmem,
+        scratch_shapes=[pltpu.VMEM((KERNEL, lat, channels), jnp.float32)],
         cost_estimate=pl.CostEstimate(
             flops=4 * KERNEL * rows * channels + 6 * rows * rows * channels,
             bytes_accessed=4 * rows * channels + 2 * KERNEL * STRIDE * channels * 4 + 2 * rows * channels * 2,

time: 45.7 us -> 45.5 us (level)
  no operation moved by 1% of the time
where the time goes in v15:
time: 45.5 us; the launch traced here: 45.2 us
  waiting for transfers between devices  23.4 us (51%)
  starting transfers between devices  10.9 us (24%)
  Pallas kernels  5.74 us (13%)
  other arithmetic  1.84 us (4%)
  matrix products  1.52 us (3%)
  local copies, waits for them, and re-layouts  0.99 us (2%)
  between operations  0.83 us (2%)
    all_to_all x1, waiting for transfers between devices, body(): lax.all_to_all(both_local, 'ctx', split_axis=0, concat_axis=0, tiled=True)  14 us
    all_to_all x1, waiting for transfers between devices, body(): lax.all_to_all(outgoing, 'ctx', split_axis=0, concat_axis=0, tiled=True)  9.4 us
    all_to_all x1, starting transfers between devices, body(): lax.all_to_all(both_local, 'ctx', split_axis=0, concat_axis=0, tiled=True)  7.25 us
    all_to_all x1, starting transfers between devices, body(): lax.all_to_all(outgoing, 'ctx', split_axis=0, concat_axis=0, tiled=True)  3.64 us
    pallas_call x1, Pallas kernels, shorten_both(): pl.pallas_call(functools.partial(shorten_kernel, per_t, nq), out_shape=ja...  3.04 us
    pallas_call x1, Pallas kernels, up_and_mix(): pl.pallas_call(functools.partial(up_kernel_fn, copies_n, per_t, nq, qr),...  2.7 us
    dot_general x1, matrix products, attend(): jnp.einsum('hqk,hkd->hqd', weights.astype(jnp.bfloat16), value_block, pre...  0.98 us
  transfers between devices with their start and end apart: 2, of which 2 were waited for; matrix products, arithmetic and copies ran while one was open for 1% of the time, Pallas kernels for 0%

profile of v15, /device:TPU:0, one launch (start us, length us, event | category | flops | bytes accessed | tf_op | source)
XLA Modules:
  0.0 45.2 jit_solution(8342979514481647217)
XLA Ops:
  0.0 0.0 copy-start.1
  0.0 3.0 %shard_map.64 = bf16[8,268,128]{2,1,0:T(8,128)(2,1)} custom-call(f32[256,512]{1,0:T(8,128)} %x_ref.3, f32[8,4,512]{2,1,0:T(4,128)} %qk_ref.1, f32[8,4,512]{2,1,0:T(4,128)} %vk_ref.1), custom_call_target="tpu_custom_call" | custom-call | flops 205520896 | bytes 1179648 | tf_op jit(solution)/shard_map/pallas_call | solution.py:108
  3.0 7.3 %all-to-all-start = ((bf16[8,268,128]{2,1,0:T(8,128)(2,1)}), bf16[8,268,128]{2,1,0:T(8,128)(2,1)S(1)}, u32[]{:S(2)}, u32[]{:S(2)}) async-start(bf16[8,268,128]{2,1,0:T(8,128)(2,1)} %shard_map.64), calls=%async_computation | async-start | bytes 1114112 | tf_op jit(solution)/shard_map/all_to_all | solution.py:199
  11.0 0.1 iota_add_fusion
  11.0 0.1 add.86
  11.1 0.0 copy-done.1
  11.2 0.4 fusion.9
  11.5 14.0 %all-to-all-done = bf16[8,268,128]{2,1,0:T(8,128)(2,1)S(1)} async-done(((bf16[8,268,128]{2,1,0:T(8,128)(2,1)}), bf16[8,268,128]{2,1,0:T(8,128)(2,1)S(1)}, u32[]{:S(2)}, u32[]{:S(2)}) %all-to-all-start) | async-done | bytes 548896 | tf_op jit(solution)/shard_map/all_to_all | solution.py:199
  25.7 0.1 broadcast_select_fusion
  25.9 0.5 %select_reduce_fusion = (f32[2,512]{1,0:T(2,128)S(1)}, f32[2,512,512]{1,2,0:T(8,128)S(1)}) fusion(f32[512]{0:T(512)S(1)} %log_multiply_fusion, pred[512,512]{0,1:T(8,128)(4,1)S(1)} %fusion.9, bf16[2,512,128]{2,1,0:T(8,128)(2,1)S(1)} %bitcast.39), kind=kOutput, calls=%fused_computation.1 | convolution fusion | flops 135789568 | bytes 2627584 | tf_op jit(solution)/shard_map/while/body/eval_jaxpr/hqd,hkd->hqk/dot_general | solution.py:242
  26.4 0.5 %fusion = f32[2,512]{1,0:T(2,128)S(1)} fusion(f32[2,512,512]{1,2,0:T(8,128)S(1)} %get-tuple-element.75, f32[2,512]{1,0:T(2,128)S(1)} %broadcast_maximum_fusion, f32[512]{0:T(512)S(1)} %log_multiply_fusion, pred[512,512]{0,1:T(8,128)(4,1)S(1)} %fusion.9), kind=kLoop, calls=%fused_computation.2 | loop fusion | flops 2096128 | bytes 2369536 | tf_op jit(solution)/shard_map/while/body/eval_jaxpr/reduce_sum | solution.py:255
  27.0 1.0 %fusion.3 = bf16[2,512,128]{2,1,0:T(8,128)(2,1)S(1)} fusion(bf16[2,512,128]{2,1,0:T(8,128)(2,1)S(1)} %bitcast.44, f32[2,512,512]{1,2,0:T(8,128)S(1)} %get-tuple-element.75, f32[2,512]{1,0:T(2,128)S(1)} %broadcast_maximum_fusion, f32[512]{0:T(512)S(1)} %log_multiply_fusion, pred[512,512]{0,1:T(8,128)(4,1)S(1)} %fusion.9, f32[2,512]{1,0:T(2,128)S(1)} %get-tuple-element.73, ...), kind=kOutput, calls=%fused_computation.6 | convolution fusion | flops 136708096 | bytes 2897920 | tf_op jit(solution)/shard_map/while/body/eval_jaxpr/hqk,hkd->hqd/dot_general | solution.py:256
  28.0 0.7 %pad_maximum_fusion = bf16[8,132,128]{2,1,0:T(8,128)(2,1)} fusion(bf16[8,4,128]{2,1,0:T(4,128)(2,1)S(1)} %bitcast.48, bf16[8,128,128]{2,1,0:T(8,128)(2,1)S(1)} %bitcast.43), kind=kLoop, calls=%fused_computation.15 | loop fusion | flops 540672 | bytes 540672 | tf_op jit(solution)/shard_map/concatenate | solution.py:279
  28.8 3.6 %all-to-all-start.1 = ((bf16[8,132,128]{2,1,0:T(8,128)(2,1)}), bf16[8,132,128]{2,1,0:T(8,128)(2,1)S(1)}, u32[]{:S(2)}, u32[]{:S(2)}) async-start(bf16[8,132,128]{2,1,0:T(8,128)(2,1)} %pad_maximum_fusion), calls=%async_computation.1 | async-start | bytes 557056 | tf_op jit(solution)/shard_map/all_to_all | solution.py:287
  32.4 9.4 %all-to-all-done.1.ret_ref = bf16[8,132,128]{2,1,0:T(8,128)(2,1)S(1)} async-done(((bf16[8,132,128]{2,1,0:T(8,128)(2,1)}), bf16[8,132,128]{2,1,0:T(8,128)(2,1)S(1)}, u32[]{:S(2)}, u32[]{:S(2)}) %all-to-all-start.1) | async-done | bytes 270368 | tf_op jit(solution)/shard_map/all_to_all | solution.py:287
  41.8 0.0 copy-start
  41.8 0.7 %copy-done = bf16[8,132,128]{2,1,0:T(8,128)(2,1)} copy-done((bf16[8,132,128]{2,1,0:T(8,128)(2,1)}, bf16[8,132,128]{2,1,0:T(8,128)(2,1)S(1)}, u32[]{:S(2)}) %copy-start) | copy-done | bytes 270360
  42.5 2.7 %shard_map.65 = f32[256,512]{1,0:T(8,128)} custom-call(s32[1]{0:T(128)} %bitcast.1.lim_ref, bf16[8,132,128]{2,1,0:T(8,128)(2,1)} %copy-done, f32[256,512]{1,0:T(8,128)} %x_ref.3, f32[8,4,512]{2,1,0:T(4,128)} %up_ref.1), custom_call_target="tpu_custom_call" | custom-call | flops 205520896 | bytes 1318912 | tf_op jit(solution)/shard_map/pallas_call | solution.py:164
  (20 shorter events, 0.3 us)
Async XLA Ops:
  0.0 11.2 %copy-start.1 = (s32[512]{0:T(512)S(1)}, s32[512]{0:T(512)}, u32[]{:S(2)}) copy-start(s32[512]{0:T(512)} %param.8) | copy-start | bytes 6148
  3.0 22.4 %all-to-all-start = ((bf16[8,268,128]{2,1,0:T(8,128)(2,1)}), bf16[8,268,128]{2,1,0:T(8,128)(2,1)S(1)}, u32[]{:S(2)}, u32[]{:S(2)}) async-start(bf16[8,268,128]{2,1,0:T(8,128)(2,1)} %shard_map.64), calls=%async_computation | async-start | bytes 1114112 | tf_op jit(solution)/shard_map/all_to_all | solution.py:199
  28.8 13.0 %all-to-all-start.1 = ((bf16[8,132,128]{2,1,0:T(8,128)(2,1)}), bf16[8,132,128]{2,1,0:T(8,128)(2,1)S(1)}, u32[]{:S(2)}, u32[]{:S(2)}) async-start(bf16[8,132,128]{2,1,0:T(8,128)(2,1)} %pad_maximum_fusion), calls=%async_computation.1 | async-start | bytes 557056 | tf_op jit(solution)/shard_map/all_to_all | solution.py:287
  41.8 0.7 %copy-start = (bf16[8,132,128]{2,1,0:T(8,128)(2,1)}, bf16[8,132,128]{2,1,0:T(8,128)(2,1)S(1)}, u32[]{:S(2)}) copy-start(bf16[8,132,128]{2,1,0:T(8,128)(2,1)S(1)} %all-to-all-done.1.ret_ref) | copy-start | bytes 811012

commit v16 on v15

--- a/solution.py
+++ b/solution.py
@@ -119,14 +119,12 @@
     )(byte_states, qk_kernel, value_kernel)
 
 
-def up_kernel_fn(copies_n, per_t, nq, qr, lim_ref, ret_ref, x_ref, up_ref, out_ref):
+def up_kernel_fn(copies_n, per_t, nq, qr, lim_ref, ret_ref, x_ref, up_ref, out_ref, prior_ref, phase_ref):
     rows, channels = x_ref.shape
     lat = rows // STRIDE
     lanes = CHANNEL_WIDTH
     blocks = channels // lanes
     row = lax.broadcasted_iota(jnp.int32, (lat, channels), 0)
-    prior_one = []
-    prior_two = []
     for t in range(STRIDE):
         att_parts = []
         rim_parts = []
@@ -138,18 +136,26 @@
             rim_parts.append(ret_ref[g * copies_n + copies_n - 1, pl.ds(nq * qr + 2 * q, 2), :])
         att = jnp.concatenate(att_parts, 1).astype(jnp.float32)
         rim = jnp.concatenate(rim_parts, 1).astype(jnp.float32)
-        one = jnp.where(row == 0, rim[1:2], pltpu.roll(att, 1, 0))
-        two = jnp.where(row == 0, rim[0:1], jnp.where(row == 1, rim[1:2], pltpu.roll(att, 2, 0)))
-        prior_one.append(one)
-        prior_two.append(two)
-    by_phase = []
-    for s in range(STRIDE):
-        total = prior_one[0] * up_ref[s, pl.ds(0, 1), :] + prior_two[0] * up_ref[s + STRIDE, pl.ds(0, 1), :]
-        for t in range(1, STRIDE):
-            total = total + prior_one[t] * up_ref[s, pl.ds(t, 1), :]
-            total = total + prior_two[t] * up_ref[s + STRIDE, pl.ds(t, 1), :]
-        by_phase.append(total)
-    by_phase = jnp.concatenate(by_phase, 0)
+        prior_ref[t] = jnp.where(row == 0, rim[1:2], pltpu.roll(att, 1, 0))
+        prior_ref[STRIDE + t] = jnp.where(row == 0, rim[0:1], jnp.where(row == 1, rim[1:2], pltpu.roll(att, 2, 0)))
+    chunk = 16
+
+    def rows_of(r, carry):
+        start = pl.multiple_of(r * chunk, chunk)
+        for block in range(blocks):
+            lane = pl.ds(block * lanes, lanes)
+            one = [prior_ref[t, pl.ds(start, chunk), lane] for t in range(STRIDE)]
+            two = [prior_ref[STRIDE + t, pl.ds(start, chunk), lane] for t in range(STRIDE)]
+            for s in range(STRIDE):
+                total = one[0] * up_ref[s, pl.ds(0, 1), lane] + two[0] * up_ref[s + STRIDE, pl.ds(0, 1), lane]
+                for t in range(1, STRIDE):
+                    total = total + one[t] * up_ref[s, pl.ds(t, 1), lane]
+                    total = total + two[t] * up_ref[s + STRIDE, pl.ds(t, 1), lane]
+                phase_ref[pl.ds(pl.multiple_of(s * lat + start, chunk), chunk), lane] = total
+        return carry
+
+    lax.fori_loop(0, lat // chunk, rows_of, 0)
+    by_phase = phase_ref[...]
     put_row = lax.broadcasted_iota(jnp.int32, (rows, rows), 0)
     put_col = lax.broadcasted_iota(jnp.int32, (rows, rows), 1)
     put = (put_col == (put_row % STRIDE) * lat + put_row // STRIDE).astype(jnp.bfloat16)
@@ -166,6 +172,10 @@
         out_shape=jax.ShapeDtypeStruct((rows, channels), jnp.float32),
         in_specs=[pl.BlockSpec(memory_space=pltpu.SMEM), vmem, vmem, vmem],
         out_specs=vmem,
+        scratch_shapes=[
+            pltpu.VMEM((2 * STRIDE, rows // STRIDE, channels), jnp.float32),
+            pltpu.VMEM((rows, channels), jnp.float32),
+        ],
         cost_estimate=pl.CostEstimate(
             flops=4 * KERNEL * rows * channels + 6 * rows * rows * channels,
             bytes_accessed=8 * rows * channels + returned.size * 2,

time: 45.5 us -> 45.6 us (level)
  no operation moved by 1% of the time
where the time goes in v16:
time: 45.6 us; the launch traced here: 45.2 us
  waiting for transfers between devices  23.4 us (51%)
  starting transfers between devices  10.9 us (24%)
  Pallas kernels  5.78 us (13%)
  other arithmetic  1.84 us (4%)
  matrix products  1.52 us (3%)
  local copies, waits for them, and re-layouts  0.99 us (2%)
  between operations  0.83 us (2%)
    all_to_all x1, waiting for transfers between devices, body(): lax.all_to_all(both_local, 'ctx', split_axis=0, concat_axis=0, tiled=True)  14 us
    all_to_all x1, waiting for transfers between devices, body(): lax.all_to_all(outgoing, 'ctx', split_axis=0, concat_axis=0, tiled=True)  9.4 us
    all_to_all x1, starting transfers between devices, body(): lax.all_to_all(both_local, 'ctx', split_axis=0, concat_axis=0, tiled=True)  7.25 us
    all_to_all x1, starting transfers between devices, body(): lax.all_to_all(outgoing, 'ctx', split_axis=0, concat_axis=0, tiled=True)  3.64 us
    pallas_call x1, Pallas kernels, shorten_both(): pl.pallas_call(functools.partial(shorten_kernel, per_t, nq), out_shape=ja...  3.04 us
    pallas_call x1, Pallas kernels, up_and_mix(): pl.pallas_call(functools.partial(up_kernel_fn, copies_n, per_t, nq, qr),...  2.73 us
    dot_general x1, matrix products, attend(): jnp.einsum('hqk,hkd->hqd', weights.astype(jnp.bfloat16), value_block, pre...  0.98 us
  transfers between devices with their start and end apart: 2, of which 2 were waited for; matrix products, arithmetic and copies ran while one was open for 1% of the time, Pallas kernels for 0%

profile of v16, /device:TPU:0, one launch (start us, length us, event | category | flops | bytes accessed | tf_op | source)
XLA Modules:
  0.0 45.2 jit_solution(6205104558116600212)
XLA Ops:
  0.0 0.0 copy-start.1
  0.0 3.0 %shard_map.64 = bf16[8,268,128]{2,1,0:T(8,128)(2,1)} custom-call(f32[256,512]{1,0:T(8,128)} %x_ref.3, f32[8,4,512]{2,1,0:T(4,128)} %qk_ref.1, f32[8,4,512]{2,1,0:T(4,128)} %vk_ref.1), custom_call_target="tpu_custom_call" | custom-call | flops 205520896 | bytes 1179648 | tf_op jit(solution)/shard_map/pallas_call | solution.py:108
  3.0 7.3 %all-to-all-start = ((bf16[8,268,128]{2,1,0:T(8,128)(2,1)}), bf16[8,268,128]{2,1,0:T(8,128)(2,1)S(1)}, u32[]{:S(2)}, u32[]{:S(2)}) async-start(bf16[8,268,128]{2,1,0:T(8,128)(2,1)} %shard_map.64), calls=%async_computation | async-start | bytes 1114112 | tf_op jit(solution)/shard_map/all_to_all | solution.py:209
  11.0 0.1 iota_add_fusion
  11.0 0.1 add.86
  11.1 0.0 copy-done.1
  11.2 0.4 fusion.9
  11.5 14.0 %all-to-all-done = bf16[8,268,128]{2,1,0:T(8,128)(2,1)S(1)} async-done(((bf16[8,268,128]{2,1,0:T(8,128)(2,1)}), bf16[8,268,128]{2,1,0:T(8,128)(2,1)S(1)}, u32[]{:S(2)}, u32[]{:S(2)}) %all-to-all-start) | async-done | bytes 548896 | tf_op jit(solution)/shard_map/all_to_all | solution.py:209
  25.7 0.1 broadcast_select_fusion
  25.9 0.5 %select_reduce_fusion = (f32[2,512]{1,0:T(2,128)S(1)}, f32[2,512,512]{1,2,0:T(8,128)S(1)}) fusion(f32[512]{0:T(512)S(1)} %log_multiply_fusion, pred[512,512]{0,1:T(8,128)(4,1)S(1)} %fusion.9, bf16[2,512,128]{2,1,0:T(8,128)(2,1)S(1)} %bitcast.39), kind=kOutput, calls=%fused_computation.1 | convolution fusion | flops 135789568 | bytes 2627584 | tf_op jit(solution)/shard_map/while/body/eval_jaxpr/hqd,hkd->hqk/dot_general | solution.py:252
  26.4 0.5 %fusion = f32[2,512]{1,0:T(2,128)S(1)} fusion(f32[2,512,512]{1,2,0:T(8,128)S(1)} %get-tuple-element.75, f32[2,512]{1,0:T(2,128)S(1)} %broadcast_maximum_fusion, f32[512]{0:T(512)S(1)} %log_multiply_fusion, pred[512,512]{0,1:T(8,128)(4,1)S(1)} %fusion.9), kind=kLoop, calls=%fused_computation.2 | loop fusion | flops 2096128 | bytes 2369536 | tf_op jit(solution)/shard_map/while/body/eval_jaxpr/reduce_sum | solution.py:265
  27.0 1.0 %fusion.3 = bf16[2,512,128]{2,1,0:T(8,128)(2,1)S(1)} fusion(bf16[2,512,128]{2,1,0:T(8,128)(2,1)S(1)} %bitcast.44, f32[2,512,512]{1,2,0:T(8,128)S(1)} %get-tuple-element.75, f32[2,512]{1,0:T(2,128)S(1)} %broadcast_maximum_fusion, f32[512]{0:T(512)S(1)} %log_multiply_fusion, pred[512,512]{0,1:T(8,128)(4,1)S(1)} %fusion.9, f32[2,512]{1,0:T(2,128)S(1)} %get-tuple-element.73, ...), kind=kOutput, calls=%fused_computation.6 | convolution fusion | flops 136708096 | bytes 2897920 | tf_op jit(solution)/shard_map/while/body/eval_jaxpr/hqk,hkd->hqd/dot_general | solution.py:266
  28.0 0.7 %pad_maximum_fusion = bf16[8,132,128]{2,1,0:T(8,128)(2,1)} fusion(bf16[8,4,128]{2,1,0:T(4,128)(2,1)S(1)} %bitcast.48, bf16[8,128,128]{2,1,0:T(8,128)(2,1)S(1)} %bitcast.43), kind=kLoop, calls=%fused_computation.15 | loop fusion | flops 540672 | bytes 540672 | tf_op jit(solution)/shard_map/concatenate | solution.py:289
  28.8 3.6 %all-to-all-start.1 = ((bf16[8,132,128]{2,1,0:T(8,128)(2,1)}), bf16[8,132,128]{2,1,0:T(8,128)(2,1)S(1)}, u32[]{:S(2)}, u32[]{:S(2)}) async-start(bf16[8,132,128]{2,1,0:T(8,128)(2,1)} %pad_maximum_fusion), calls=%async_computation.1 | async-start | bytes 557056 | tf_op jit(solution)/shard_map/all_to_all | solution.py:297
  32.4 9.4 %all-to-all-done.1.ret_ref = bf16[8,132,128]{2,1,0:T(8,128)(2,1)S(1)} async-done(((bf16[8,132,128]{2,1,0:T(8,128)(2,1)}), bf16[8,132,128]{2,1,0:T(8,128)(2,1)S(1)}, u32[]{:S(2)}, u32[]{:S(2)}) %all-to-all-start.1) | async-done | bytes 270368 | tf_op jit(solution)/shard_map/all_to_all | solution.py:297
  41.8 0.0 copy-start
  41.8 0.7 %copy-done = bf16[8,132,128]{2,1,0:T(8,128)(2,1)} copy-done((bf16[8,132,128]{2,1,0:T(8,128)(2,1)}, bf16[8,132,128]{2,1,0:T(8,128)(2,1)S(1)}, u32[]{:S(2)}) %copy-start) | copy-done | bytes 270360
  42.5 2.7 %shard_map.65 = f32[256,512]{1,0:T(8,128)} custom-call(s32[1]{0:T(128)} %bitcast.1.lim_ref, bf16[8,132,128]{2,1,0:T(8,128)(2,1)} %copy-done, f32[256,512]{1,0:T(8,128)} %x_ref.3, f32[8,4,512]{2,1,0:T(4,128)} %up_ref.1), custom_call_target="tpu_custom_call" | custom-call | flops 205520896 | bytes 1318912 | tf_op jit(solution)/shard_map/pallas_call | solution.py:170
  (20 shorter events, 0.3 us)
Async XLA Ops:
  0.0 11.2 %copy-start.1 = (s32[512]{0:T(512)S(1)}, s32[512]{0:T(512)}, u32[]{:S(2)}) copy-start(s32[512]{0:T(512)} %param.8) | copy-start | bytes 6148
  3.0 22.4 %all-to-all-start = ((bf16[8,268,128]{2,1,0:T(8,128)(2,1)}), bf16[8,268,128]{2,1,0:T(8,128)(2,1)S(1)}, u32[]{:S(2)}, u32[]{:S(2)}) async-start(bf16[8,268,128]{2,1,0:T(8,128)(2,1)} %shard_map.64), calls=%async_computation | async-start | bytes 1114112 | tf_op jit(solution)/shard_map/all_to_all | solution.py:209
  28.8 13.0 %all-to-all-start.1 = ((bf16[8,132,128]{2,1,0:T(8,128)(2,1)}), bf16[8,132,128]{2,1,0:T(8,128)(2,1)S(1)}, u32[]{:S(2)}, u32[]{:S(2)}) async-start(bf16[8,132,128]{2,1,0:T(8,128)(2,1)} %pad_maximum_fusion), calls=%async_computation.1 | async-start | bytes 557056 | tf_op jit(solution)/shard_map/all_to_all | solution.py:297
  41.8 0.7 %copy-start = (bf16[8,132,128]{2,1,0:T(8,128)(2,1)}, bf16[8,132,128]{2,1,0:T(8,128)(2,1)S(1)}, u32[]{:S(2)}) copy-start(bf16[8,132,128]{2,1,0:T(8,128)(2,1)S(1)} %all-to-all-done.1.ret_ref) | copy-start | bytes 811012

commit v17 on v13

--- a/solution.py
+++ b/solution.py
@@ -52,7 +52,7 @@
     by_phase = exact_rows(pick, x_ref[...])
     phase = [by_phase[s * lat : (s + 1) * lat] for s in range(STRIDE)]
     first_row = lax.broadcasted_iota(jnp.int32, (lat, channels), 0) == 0
-    edge_rows = -(-6 * nq // 8) * 8
+    edge_rows = -(-2 * nq // 8) * 8
     edge_row = lax.broadcasted_iota(jnp.int32, (edge_rows, lanes), 0)
     edge = [jnp.zeros((edge_rows, lanes), jnp.float32) for _ in range(STRIDE * per_t)]
     for which, kern_ref in enumerate((qk_ref, vk_ref)):
@@ -71,16 +71,16 @@
                 g = t * per_t + block // nq
                 slot = which * nq + block % nq
                 out_ref[g, pl.ds(slot * lat, lat), :] = total[:, lane]
-                for e, piece in enumerate((own_lo, next_hi, next_lo)):
+                for e, piece in enumerate((next_hi,)):
                     edge[g] = jnp.where(edge_row == e * 2 * nq + slot, piece[:, lane].astype(jnp.float32), edge[g])
     for g in range(STRIDE * per_t):
-        out_ref[g, pl.ds(2 * nq * lat, 6 * nq), :] = edge[g][: 6 * nq].astype(jnp.bfloat16)
+        out_ref[g, pl.ds(2 * nq * lat, 2 * nq), :] = edge[g][: 2 * nq].astype(jnp.bfloat16)
 
 
 def shorten_both(byte_states, qk_kernel, value_kernel, groups_n, per_t, nq):
     rows, channels = byte_states.shape
     lat = rows // STRIDE
-    kv_rows = 2 * nq * lat + 6 * nq
+    kv_rows = 2 * nq * lat + 2 * nq
     vmem = pl.BlockSpec(memory_space=pltpu.VMEM)
     return pl.pallas_call(
         functools.partial(shorten_kernel, per_t, nq),
@@ -174,10 +174,9 @@
         ).reshape(n_ctx, kv_rows, CHANNEL_WIDTH)
     both_all = lax.all_to_all(both_local, "ctx", split_axis=0, concat_axis=0, tiled=True)
     main_kv = both_all[:, : 2 * nq * lat_dev].reshape(n_ctx, 2 * nq, lat_dev, CHANNEL_WIDTH)
-    edge = both_all[:, 2 * nq * lat_dev : 2 * nq * lat_dev + 6 * nq].astype(jnp.float32)
-    edge = edge.reshape(n_ctx, 3, 2 * nq, CHANNEL_WIDTH)
-    own_first = main_kv[:, :, 0].astype(jnp.float32) + edge[:, 0]
-    from_before = edge[:, 1] + edge[:, 2]
+    edge = both_all[:, 2 * nq * lat_dev : 2 * nq * lat_dev + 2 * nq].astype(jnp.float32)
+    own_first = main_kv[:, :, 0].astype(jnp.float32)
+    from_before = edge
     from_before = jnp.concatenate([jnp.zeros_like(from_before[:1]), from_before[:-1]], 0)
     first_rows = (own_first + from_before).astype(jnp.bfloat16)
     at_first = lax.broadcasted_iota(jnp.int32, main_kv.shape, 2) == 0

time: 45.7 us -> 45.2 us (0.989)
  no operation moved by 1% of the time
where the time goes in v17:
time: 45.2 us; the launch traced here: 44.9 us
  waiting for transfers between devices  23 us (51%)
  starting transfers between devices  10.9 us (24%)
  Pallas kernels  5.82 us (13%)
  other arithmetic  1.83 us (4%)
  matrix products  1.52 us (3%)
  local copies, waits for them, and re-layouts  0.97 us (2%)
  between operations  0.8 us (2%)
    all_to_all x1, waiting for transfers between devices, body(): lax.all_to_all(both_local, 'ctx', split_axis=0, concat_axis=0, tiled=True)  13.6 us
    all_to_all x1, waiting for transfers between devices, body(): lax.all_to_all(outgoing, 'ctx', split_axis=0, concat_axis=0, tiled=True)  9.4 us
    all_to_all x1, starting transfers between devices, body(): lax.all_to_all(both_local, 'ctx', split_axis=0, concat_axis=0, tiled=True)  7.25 us
    all_to_all x1, starting transfers between devices, body(): lax.all_to_all(outgoing, 'ctx', split_axis=0, concat_axis=0, tiled=True)  3.64 us
    pallas_call x1, Pallas kernels, shorten_both(): pl.pallas_call(functools.partial(shorten_kernel, per_t, nq), out_shape=ja...  3.12 us
    pallas_call x1, Pallas kernels, up_and_mix(): pl.pallas_call(functools.partial(up_kernel_fn, copies_n, per_t, nq, qr),...  2.69 us
    dot_general x1, matrix products, attend(): jnp.einsum('hqk,hkd->hqd', weights.astype(jnp.bfloat16), value_block, pre...  0.98 us
  transfers between devices with their start and end apart: 2, of which 2 were waited for; matrix products, arithmetic and copies ran while one was open for 1% of the time, Pallas kernels for 0%

profile of v17, /device:TPU:0, one launch (start us, length us, event | category | flops | bytes accessed | tf_op | source)
XLA Modules:
  0.0 44.9 jit_solution(11695719453385062416)
XLA Ops:
  0.0 0.0 copy-start.1
  0.0 3.1 %shard_map.64 = bf16[8,260,128]{2,1,0:T(8,128)(2,1)} custom-call(f32[256,512]{1,0:T(8,128)} %x_ref.3, f32[8,4,512]{2,1,0:T(4,128)} %qk_ref.1, f32[8,4,512]{2,1,0:T(4,128)} %vk_ref.1), custom_call_target="tpu_custom_call" | custom-call | flops 205520896 | bytes 1179648 | tf_op jit(solution)/shard_map/pallas_call | solution.py:85
  3.1 7.3 %all-to-all-start = ((bf16[8,260,128]{2,1,0:T(8,128)(2,1)}), bf16[8,260,128]{2,1,0:T(8,128)(2,1)S(1)}, u32[]{:S(2)}, u32[]{:S(2)}) async-start(bf16[8,260,128]{2,1,0:T(8,128)(2,1)} %shard_map.64), calls=%async_computation | async-start | bytes 1081344 | tf_op jit(solution)/shard_map/all_to_all | solution.py:175
  11.1 0.1 iota_add_fusion
  11.1 0.1 add.79
  11.2 0.0 copy-done.1
  11.2 0.4 fusion.9
  11.6 13.6 %all-to-all-done = bf16[8,260,128]{2,1,0:T(8,128)(2,1)S(1)} async-done(((bf16[8,260,128]{2,1,0:T(8,128)(2,1)}), bf16[8,260,128]{2,1,0:T(8,128)(2,1)S(1)}, u32[]{:S(2)}, u32[]{:S(2)}) %all-to-all-start) | async-done | bytes 532512 | tf_op jit(solution)/shard_map/all_to_all | solution.py:175
  25.3 0.1 broadcast_select_fusion
  25.5 0.5 %select_reduce_fusion = (f32[2,512]{1,0:T(2,128)S(1)}, f32[2,512,512]{1,2,0:T(8,128)S(1)}) fusion(f32[512]{0:T(512)S(1)} %log_multiply_fusion, pred[512,512]{0,1:T(8,128)(4,1)S(1)} %fusion.9, bf16[2,512,128]{2,1,0:T(8,128)(2,1)S(1)} %bitcast.28), kind=kOutput, calls=%fused_computation.1 | convolution fusion | flops 135789568 | bytes 2627584 | tf_op jit(solution)/shard_map/while/body/eval_jaxpr/hqd,hkd->hqk/dot_general | solution.py:217
  26.1 0.5 %fusion = f32[2,512]{1,0:T(2,128)S(1)} fusion(f32[2,512,512]{1,2,0:T(8,128)S(1)} %get-tuple-element.73, f32[2,512]{1,0:T(2,128)S(1)} %broadcast_maximum_fusion, f32[512]{0:T(512)S(1)} %log_multiply_fusion, pred[512,512]{0,1:T(8,128)(4,1)S(1)} %fusion.9), kind=kLoop, calls=%fused_computation.2 | loop fusion | flops 2096128 | bytes 2369536 | tf_op jit(solution)/shard_map/while/body/eval_jaxpr/reduce_sum | solution.py:230
  26.6 1.0 %fusion.3 = bf16[2,512,128]{2,1,0:T(8,128)(2,1)S(1)} fusion(bf16[2,512,128]{2,1,0:T(8,128)(2,1)S(1)} %bitcast.33, f32[2,512,512]{1,2,0:T(8,128)S(1)} %get-tuple-element.73, f32[2,512]{1,0:T(2,128)S(1)} %broadcast_maximum_fusion, f32[512]{0:T(512)S(1)} %log_multiply_fusion, pred[512,512]{0,1:T(8,128)(4,1)S(1)} %fusion.9, f32[2,512]{1,0:T(2,128)S(1)} %get-tuple-element.71, ...), kind=kOutput, calls=%fused_computation.6 | convolution fusion | flops 136708096 | bytes 2897920 | tf_op jit(solution)/shard_map/while/body/eval_jaxpr/hqk,hkd->hqd/dot_general | solution.py:231
  27.7 0.7 %pad_maximum_fusion = bf16[8,132,128]{2,1,0:T(8,128)(2,1)} fusion(bf16[8,4,128]{2,1,0:T(4,128)(2,1)S(1)} %bitcast.35, bf16[8,128,128]{2,1,0:T(8,128)(2,1)S(1)} %bitcast.32), kind=kLoop, calls=%fused_computation.15 | loop fusion | flops 540672 | bytes 540672 | tf_op jit(solution)/shard_map/concatenate | solution.py:254
  28.4 3.6 %all-to-all-start.1 = ((bf16[8,132,128]{2,1,0:T(8,128)(2,1)}), bf16[8,132,128]{2,1,0:T(8,128)(2,1)S(1)}, u32[]{:S(2)}, u32[]{:S(2)}) async-start(bf16[8,132,128]{2,1,0:T(8,128)(2,1)} %pad_maximum_fusion), calls=%async_computation.1 | async-start | bytes 557056 | tf_op jit(solution)/shard_map/all_to_all | solution.py:262
  32.1 9.4 %all-to-all-done.1.ret_ref = bf16[8,132,128]{2,1,0:T(8,128)(2,1)S(1)} async-done(((bf16[8,132,128]{2,1,0:T(8,128)(2,1)}), bf16[8,132,128]{2,1,0:T(8,128)(2,1)S(1)}, u32[]{:S(2)}, u32[]{:S(2)}) %all-to-all-start.1) | async-done | bytes 270368 | tf_op jit(solution)/shard_map/all_to_all | solution.py:262
  41.5 0.0 copy-start
  41.5 0.7 %copy-done = bf16[8,132,128]{2,1,0:T(8,128)(2,1)} copy-done((bf16[8,132,128]{2,1,0:T(8,128)(2,1)}, bf16[8,132,128]{2,1,0:T(8,128)(2,1)S(1)}, u32[]{:S(2)}) %copy-start) | copy-done | bytes 270360
  42.2 2.7 %shard_map.65 = f32[256,512]{1,0:T(8,128)} custom-call(s32[1]{0:T(128)} %bitcast.1.lim_ref, bf16[8,132,128]{2,1,0:T(8,128)(2,1)} %copy-done, f32[256,512]{1,0:T(8,128)} %x_ref.3, f32[8,4,512]{2,1,0:T(4,128)} %up_ref.1), custom_call_target="tpu_custom_call" | custom-call | flops 205520896 | bytes 1318912 | tf_op jit(solution)/shard_map/pallas_call | solution.py:140
  (16 shorter events, 0.2 us)
Async XLA Ops:
  0.0 11.2 %copy-start.1 = (s32[512]{0:T(512)S(1)}, s32[512]{0:T(512)}, u32[]{:S(2)}) copy-start(s32[512]{0:T(512)} %param.8) | copy-start | bytes 6148
  3.1 22.1 %all-to-all-start = ((bf16[8,260,128]{2,1,0:T(8,128)(2,1)}), bf16[8,260,128]{2,1,0:T(8,128)(2,1)S(1)}, u32[]{:S(2)}, u32[]{:S(2)}) async-start(bf16[8,260,128]{2,1,0:T(8,128)(2,1)} %shard_map.64), calls=%async_computation | async-start | bytes 1081344 | tf_op jit(solution)/shard_map/all_to_all | solution.py:175
  28.4 13.0 %all-to-all-start.1 = ((bf16[8,132,128]{2,1,0:T(8,128)(2,1)}), bf16[8,132,128]{2,1,0:T(8,128)(2,1)S(1)}, u32[]{:S(2)}, u32[]{:S(2)}) async-start(bf16[8,132,128]{2,1,0:T(8,128)(2,1)} %pad_maximum_fusion), calls=%async_computation.1 | async-start | bytes 557056 | tf_op jit(solution)/shard_map/all_to_all | solution.py:262
  41.5 0.7 %copy-start = (bf16[8,132,128]{2,1,0:T(8,128)(2,1)}, bf16[8,132,128]{2,1,0:T(8,128)(2,1)S(1)}, u32[]{:S(2)}) copy-start(bf16[8,132,128]{2,1,0:T(8,128)(2,1)S(1)} %all-to-all-done.1.ret_ref) | copy-start | bytes 811012
